TPU v7x, 512 devices: a whole 4x8x8 slice. The times are simulated.
512 devices in a mesh: grp: 16 (over z, core), dev: 32 (over y, x).
Axes of the slice: x: 4, y: 8, z: 8, core: 2. Of those that a mesh axis runs over, the one named last changes fastest.
Arguments:
- desc: bfloat16 [2097152, 128], P(('grp', 'dev')), may hold values from -6 to 6
- positions: float32 [3, 2097152], P(None, ('grp', 'dev')), may hold values from -1 to 1
- species: int32 [2097152], P(('grp', 'dev')), may hold values from 0 to 5
- w_in: bfloat16 [128, 128], replicated, may hold values from -0.5 to 0.5
- w_mid: bfloat16 [128, 128], replicated, may hold values from -0.5 to 0.5
- w_head: float32 [128], replicated, may hold values from -0.5 to 0.5
- species_charge: float32 [6], replicated, may hold values from -1 to 1
- m2l_kernels: float32 [98, 16, 16], replicated, may hold values from -0.5 to 0.5
- expand_u: float32 [64, 16], replicated, may hold values from -1.5 to 1.5
- compress_v: float32 [64, 16], replicated, may hold values from -0.75 to 0.75
- send_list: int32 [16384, 256], P(('grp', 'dev')), may hold values from -1 to 4095, as said below
- slot_box: int32 [16384, 256], P(('grp', 'dev')), may hold values from 0 to 1023
Outputs:
- potential: float32 [2097152], P(('grp', 'dev'))
- grad_in: float32 [128, 128], replicated
- grad_mid: float32 [128, 128], replicated
- grad_head: float32 [128], replicated
- grad_species: float32 [6], replicated
Inputs may be any that keep to these rules, and one draw needn't show every extreme that they name: `send_list`: each of a device's 4096 atoms stands in exactly one slot of the device's 32 rows; used slots come first in a row; in every device exactly one row has all 256 slots used and one row none.
All inputs are finite; a program needn't handle non-finite values.
Results may differ from a plain program's by a relative error of at most 0.002.
Values sent between devices are 32-bit elements; how exact they have to be, the bound alone decides.
No kernel may reach another device: no remote copies, remote signals or barrier semaphores. Data moves between devices by JAX's collectives and lax.ppermute only.
A program may use at most 64 MiB of HBM per device.

v0:
```python
import math

import jax
import jax.numpy as jnp
import numpy as np
from jax import lax
from jax.sharding import Mesh
from jax.sharding import PartitionSpec as P

NODES = 64
RANK = 16
BZ = 4
BX = 4
BY = 64
BOXES = 1024
GRP = ("grp_0", "grp_1")
DEV = ("dev_0", "dev_1")
GRP_DEV = ("grp_0", "grp_1", "dev_0", "dev_1")


NODE_POINTS = [math.cos((2 * node_number + 1) * math.pi / 8) for node_number in range(4)]


def extended_2(cells, sides, width):
    for axis, dim in sides:
        count = lax.axis_size(axis)
        ends = count - 1
        head = lax.slice_in_dim(cells, 0, width, axis=dim)
        tail = lax.slice_in_dim(cells, cells.shape[dim] - width, cells.shape[dim], axis=dim)
        cells = jnp.concatenate(
            [
                lax.ppermute(tail, axis, [(i, (i + 1) % count) for i in range(ends)]),
                cells,
                lax.ppermute(head, axis, [((i + 1) % count, i) for i in range(ends)]),
            ],
            axis=dim,
        )
    return cells


def in_blocks(x, dim, peers):
    before, after = (x.shape[:dim], x.shape[dim + 1 :])
    return jnp.moveaxis(x.reshape(*before, peers, -1, *after), dim, 0)


def sent_and_summed(x, axis, dim):
    blocks = in_blocks(x, dim, lax.axis_size(axis))
    arrived = lax.all_to_all(blocks, axis, split_axis=0, concat_axis=0, tiled=True)
    return arrived.sum(axis=0)


def sum_in_two_steps(x, axes, dim):
    far, near = axes
    blocks = in_blocks(x, dim, lax.axis_size(far))
    nearer = sent_and_summed(blocks, near, dim + 1)
    arrived = lax.all_to_all(nearer, far, split_axis=0, concat_axis=0, tiled=True)
    return arrived.sum(axis=0)


def padded_to(lines, peers):
    spare = -lines.shape[0] % peers
    if not spare:
        return lines
    return jnp.concatenate([lines, jnp.zeros((spare, *lines.shape[1:]), lines.dtype)])


def sent_to_all(x, axis):
    copies = jnp.broadcast_to(x, (lax.axis_size(axis), *x.shape))
    return lax.all_to_all(copies, axis, split_axis=0, concat_axis=0, tiled=True)


def laid_out(blocks, dim):
    dims = list(blocks.shape[1:])
    dims[dim] *= blocks.shape[0]
    return jnp.moveaxis(blocks, 0, dim).reshape(dims)


def whole_of(x, axes, dim):
    far, near = axes
    blocks = sent_to_all(sent_to_all(x, far), near)
    return laid_out(blocks.swapaxes(0, 1).reshape(-1, *x.shape), dim)


def nested_sum(x, axes):
    own = sum_in_two_steps(padded_to(x, lax.axis_size(axes[0]) * lax.axis_size(axes[1])), axes, 0)
    whole = whole_of(own, axes, 0)
    return whole[: len(x)].reshape(x.shape)


def together(arrays, axis):
    ends = [0]
    for a in arrays:
        ends.append(ends[-1] + a.size)
    total = nested_sum(jnp.concatenate([a.ravel() for a in arrays]), axis)
    return tuple((total[b:e].reshape(a.shape) for a, b, e in zip(arrays, ends, ends[1:])))


def shell_table():
    table = np.full((5, 5, 5), 98, dtype=np.int32)
    counter = 0
    for shift_z in range(-2, 3):
        for shift_x in range(-2, 3):
            for shift_y in range(-2, 3):
                if max(abs(shift_z), abs(shift_x), abs(shift_y)) == 2:
                    table[shift_z + 2, shift_x + 2, shift_y + 2] = counter
                    counter += 1
    return table


def chebyshev_rows(coordinate):
    order_two = 2.0 * coordinate * coordinate - 1.0
    order_three = 4.0 * coordinate * coordinate * coordinate - 3.0 * coordinate
    stacked = []
    for node_point in NODE_POINTS:
        cheb_two = 2.0 * node_point * node_point - 1.0
        cheb_three = 4.0 * node_point * node_point * node_point - 3.0 * node_point
        stacked.append(
            0.25 + 0.5 * (node_point * coordinate + cheb_two * order_two + cheb_three * order_three)
        )
    return jnp.stack(stacked, 0)


def node_weights(coords):
    along_z = chebyshev_rows(coords[0])
    along_x = chebyshev_rows(coords[1])
    along_y = chebyshev_rows(coords[2])
    product = along_z[:, None, None, :] * along_x[None, :, None, :] * along_y[None, None, :, :]
    return product.reshape(64, coords.shape[1])


def silu_slope(value):
    sigma = jax.nn.sigmoid(value)
    return sigma * (1.0 + value * (1.0 - sigma))


def translate(padded, m2l_kernels):
    rank_count = padded.shape[0]
    depth_z = padded.shape[1] - 4
    wide_x = padded.shape[2]
    depth_x = wide_x - 4
    length_y = padded.shape[3]
    y_source = jnp.arange(length_y, dtype=jnp.int32)[:, None]
    y_target = jnp.arange(length_y, dtype=jnp.int32)[None, :]
    shift_y = jnp.stack(
        [(y_source == y_target + step).astype(jnp.float32) for step in range(-2, 3)], 0
    )
    x_source = jnp.arange(wide_x, dtype=jnp.int32)[:, None]
    x_target = jnp.arange(depth_x, dtype=jnp.int32)[None, :]
    shift_x = jnp.stack(
        [(x_source == x_target + 2 + step).astype(jnp.float32) for step in range(-2, 3)], 0
    )
    shifted = jnp.einsum("gvy,bzxv->gbzxy", shift_y, padded, precision=lax.Precision.HIGHEST)
    extended = jnp.concatenate(
        [m2l_kernels, jnp.zeros((1, rank_count, rank_count), jnp.float32)], axis=0
    )
    stencil = extended[jnp.asarray(shell_table())]
    summed = jnp.zeros((rank_count, depth_z, depth_x, length_y), jnp.float32)
    for plane in range(5):
        slab = shifted[:, :, plane : plane + depth_z]
        partial_value = jnp.einsum(
            "fgab,gbzpy->afzpy", stencil[plane], slab, precision=lax.Precision.HIGHEST
        )
        summed = summed + jnp.einsum(
            "afzpy,fpq->azqy", partial_value, shift_x, precision=lax.Precision.HIGHEST
        )
    return summed


def shards(
    desc,
    positions,
    species,
    w_in,
    w_mid,
    w_head,
    species_charge,
    m2l_kernels,
    expand_u,
    compress_v,
    send_list,
    slot_box,
):
    atom_count = desc.shape[0]
    total_atoms = atom_count * lax.axis_size(GRP) * lax.axis_size(DEV)
    grad_scale = 1.0 / math.sqrt(total_atoms)
    pre_one = jnp.dot(desc, w_in, preferred_element_type=jnp.float32)
    hidden_one = jax.nn.silu(pre_one).astype(jnp.bfloat16)
    pre_two = jnp.dot(hidden_one, w_mid, preferred_element_type=jnp.float32)
    hidden_two = jax.nn.silu(pre_two)
    species_hot = (
        species[None, :] == jnp.arange(species_charge.shape[0], dtype=jnp.int32)[:, None]
    ).astype(jnp.float32)
    charge = jnp.sum(hidden_two * w_head[None, :], axis=1) + jnp.dot(
        species_charge, species_hot, precision=lax.Precision.HIGHEST
    )
    is_used = send_list >= 0
    safe_index = jnp.where(is_used, send_list, 0)
    packed = jnp.concatenate([charge[None, :], positions], axis=0)
    picked = jnp.where(is_used[None], packed[:, safe_index], 0.0)
    arrived, box_ids = (
        lax.all_to_all(picked, DEV, split_axis=1, concat_axis=1, tiled=True),
        lax.all_to_all(slot_box[None], DEV, split_axis=1, concat_axis=1, tiled=True),
    )
    arrived_charge = arrived[0].reshape(-1)
    arrived_coords = arrived[1:].reshape(3, -1)
    slot_boxes = box_ids.reshape(-1)
    weight_table = node_weights(arrived_coords)
    moments = (
        jnp.zeros((NODES, BOXES), jnp.float32)
        .at[:, slot_boxes]
        .add(weight_table * arrived_charge[None, :])
    )
    node_grid = moments.reshape(NODES, BZ, BX, BY)
    reduced = jnp.einsum("nr,nzxy->rzxy", compress_v, node_grid, precision=lax.Precision.HIGHEST)
    padded = extended_2(reduced, ((GRP, 1), (DEV, 2)), 2)
    local_terms = translate(padded, m2l_kernels)
    expansion = jnp.dot(expand_u, local_terms.reshape(RANK, BOXES), precision=lax.Precision.HIGHEST)
    slot_potential = jnp.sum(weight_table * expansion[:, slot_boxes], axis=0).reshape(
        send_list.shape
    )
    returned = lax.all_to_all(slot_potential, DEV, split_axis=0, concat_axis=0, tiled=True)
    target_rows = jnp.where(is_used, send_list, atom_count).reshape(-1)
    potential = (
        jnp.zeros((atom_count,), jnp.float32).at[target_rows].set(returned.reshape(-1), mode="drop")
    )
    head_part = jnp.sum(potential[:, None] * hidden_two, axis=0) * grad_scale
    species_part = jnp.dot(species_hot, potential, precision=lax.Precision.HIGHEST) * grad_scale
    delta_two = (potential[:, None] * w_head[None, :] * silu_slope(pre_two)).astype(jnp.bfloat16)
    mid_part = (
        lax.dot_general(
            hidden_one, delta_two, (((0,), (0,)), ((), ())), preferred_element_type=jnp.float32
        )
        * grad_scale
    )
    back_one = lax.dot_general(
        delta_two, w_mid, (((1,), (1,)), ((), ())), preferred_element_type=jnp.float32
    )
    delta_one = (back_one * silu_slope(pre_one)).astype(jnp.bfloat16)
    in_part = (
        lax.dot_general(
            desc, delta_one, (((0,), (0,)), ((), ())), preferred_element_type=jnp.float32
        )
        * grad_scale
    )
    grad_in, grad_mid, grad_head, grad_species = together(
        (in_part, mid_part, head_part, species_part), ("grp_0", ("grp_1", "dev_0", "dev_1"))
    )
    return (potential, grad_in, grad_mid, grad_head, grad_species)


def solution(mesh):
    torus = Mesh(mesh.devices.reshape(8, 2, 8, 4), ("grp_0", "grp_1", "dev_0", "dev_1"))
    placed = (
        P(GRP_DEV, None),
        P(None, GRP_DEV),
        P(GRP_DEV),
        P(),
        P(),
        P(),
        P(),
        P(),
        P(),
        P(),
        P(GRP_DEV, None),
        P(GRP_DEV, None),
    )
    return jax.shard_map(
        shards,
        mesh=torus,
        in_specs=placed,
        out_specs=(P(GRP_DEV), P(), P(), P(), P()),
        check_vma=False,
    )
```

profile of v0, /device:TPU:8, one launch (start us, length us, event | category | flops | bytes accessed | tf_op | source)
XLA Modules:
  0.0 323.9 jit_solution(12040090106949201596)
XLA Ops:
  0.6 1.5 broadcast_in_dim.69
  2.1 10.2 %all-to-all-start.1 = ((s32[1,32,256]{2,0,1:T(1,128)}), s32[1,32,256]{2,0,1:T(1,128)S(1)}, u32[]{:S(2)}, u32[]{:S(2)}) async-start(s32[1,32,256]{2,0,1:T(1,128)} %broadcast_in_dim.69), calls=%async_computation.1 | async-start | bytes 65536 | tf_op jit(solution)/shard_map/all_to_all | solution.py:202
  12.3 1.4 fusion.69
  13.7 0.8 broadcast_compare_fusion
  14.6 2.8 multiply_convert_fusion.1
  17.6 2.0 multiply_reduce_fusion.1
  19.7 0.6 copy.46
  20.5 1.3 copy.50
  21.8 2.1 concatenate.18
  24.2 2.8 gather_fusion.1
  27.0 0.6 broadcast_clamp_fusion
  27.6 27.7 %gather_fusion = f32[8192,4]{1,0:T(8,128)} fusion(f32[4,4096]{0,1:T(8,128)S(1)} %copy.46, s32[8192]{0:T(1024)S(1)} %get-tuple-element.41), kind=kCustom, calls=%fused_computation | custom fusion | bytes 294912 | tf_op jit(solution)/shard_map/gather | solution.py:199
  55.4 2.9 copy.47
  58.3 0.7 select_bitcast_fusion
  59.0 9.8 %all-to-all-start = ((f32[4,32,256]{2,0,1:T(4,128)}), f32[4,32,256]{2,0,1:T(4,128)S(1)}, u32[]{:S(2)}, u32[]{:S(2)}) async-start(f32[4,32,256]{2,0,1:T(4,128)} %select_bitcast_fusion), calls=%async_computation | async-start | bytes 262144 | tf_op jit(solution)/shard_map/all_to_all | solution.py:201
  68.8 0.9 fusion.86
  69.8 8.6 %all-to-all-done = f32[4,32,256]{2,0,1:T(4,128)S(1)} async-done(((f32[4,32,256]{2,0,1:T(4,128)}), f32[4,32,256]{2,0,1:T(4,128)S(1)}, u32[]{:S(2)}, u32[]{:S(2)}) %all-to-all-start) | async-done | bytes 131104 | tf_op jit(solution)/shard_map/all_to_all | solution.py:201
  78.5 0.3 multiply_add_fusion.11
  78.8 0.3 multiply_add_fusion.7
  79.1 0.3 multiply_add_fusion.3
  79.9 1.9 broadcast_multiply_fusion
  81.8 2.0 mul.1040
  83.8 1.5 multiply_bitcast_fusion
  85.3 3.8 %copy.48 = f32[8192,64]{1,0:T(8,128)} copy(f32[8192,64]{0,1:T(8,128)} %multiply_bitcast_fusion) | data formatting | bytes 4194304 | tf_op jit(solution)/shard_map/mul | solution.py:211
  89.1 45.1 %scatter_custom_fusion = f32[64,1024]{0,1:T(8,128)} fusion(s32[8192]{0:T(1024)S(1)} %bitcast.214, f32[8192,64]{1,0:T(8,128)} %copy.48, f32[]{:T(128)} %constant.26.clone.1), kind=kCustom, calls=%fused_computation.69 | custom fusion | flops 524288 | bytes 262656 | tf_op jit(solution)/shard_map/scatter-add | solution.py:211
  134.2 2.4 convolution_bitcast_fusion.7
  136.6 1.3 collective-permute-start
  137.9 1.3 collective-permute-start.1
  139.2 4.4 %collective-permute-done.1 = f32[16,2,4,64]{3,0,2,1:T(8,128)S(1)} collective-permute-done((f32[16,2,4,64]{3,0,2,1:T(8,128)S(1)}, f32[16,2,4,64]{3,0,2,1:T(8,128)S(1)}, u32[]{:S(2)}, u32[]{:S(2)}) %collective-permute-start.1) | collective-permute-done | bytes 32800 | tf_op jit(solution)/shard_map/ppermute | solution.py:34
  143.6 0.7 fusion.87
  144.3 2.6 collective-permute-start.2
  146.9 5.4 %collective-permute-start.3 = (f32[16,8,2,64]{3,0,2,1:T(8,128)}, f32[16,8,2,64]{3,0,2,1:T(8,128)}, u32[]{:S(2)}, u32[]{:S(2)}) collective-permute-start(f32[16,8,2,64]{3,0,2,1:T(8,128)} %get-tuple-element.13), channel_id=1, source_target_pairs={{1,0},{2,1},{3,2},{4,3},{5,4},{6,5},{7,6},{8,7},{9,8},{10,9},{11,1... | collective-permute-start | bytes 196616 | tf_op jit(solution)/shard_map/ppermute | solution.py:34
  152.4 1.4 copy.87
  153.8 2.7 copy.57
  156.5 2.2 convolution_bitcast_fusion
  158.7 1.3 convolution_bitcast_fusion.2
  160.1 1.3 convolution_bitcast_fusion.3
  161.4 1.3 convolution_bitcast_fusion.4
  162.7 1.3 convolution_bitcast_fusion.5
  164.0 1.3 convolution_bitcast_fusion.1
  165.3 1.0 fusion.14
  166.4 1.0 fusion.41
  167.4 1.0 fusion.38
  168.4 1.0 fusion.35
  169.5 1.2 fusion.32
  170.9 0.4 convolution_bitcast_fusion.6
  171.5 27.7 %gather_fusion.2 = f32[8192,64]{1,0:T(8,128)} fusion(f32[64,1024]{0,1:T(8,128)S(1)} %copy.56, s32[8192]{0:T(1024)S(1)} %copy-done.9), kind=kCustom, calls=%fused_computation.2 | custom fusion | bytes 4227072 | tf_op jit(solution)/shard_map/gather | solution.py:218
  199.2 5.2 %fusion.1 = f32[8192]{0:T(1024)} fusion(f32[64,8192]{0,1:T(8,128)} %copy.57, f32[8192,64]{1,0:T(8,128)} %gather_fusion.2), kind=kLoop, calls=%fused_computation.8 | loop fusion | flops 1040384 | bytes 4227072 | tf_op jit(solution)/shard_map/reduce_sum | solution.py:218
  204.5 6.8 %all-to-all-start.2 = ((f32[32,1,256]{2,1,0:T(1,128)}), f32[32,1,256]{2,1,0:T(1,128)S(1)}, u32[]{:S(2)}, u32[]{:S(2)}) async-start(f32[32,1,256]{2,1,0:T(1,128)} %bitcast.78), calls=%async_computation.2 | async-start | bytes 65536 | tf_op jit(solution)/shard_map/all_to_all | solution.py:221
  211.3 8.6 %all-to-all-done.2 = f32[32,1,256]{2,1,0:T(1,128)S(1)} async-done(((f32[32,1,256]{2,1,0:T(1,128)}), f32[32,1,256]{2,1,0:T(1,128)S(1)}, u32[]{:S(2)}, u32[]{:S(2)}) %all-to-all-start.2) | async-done | bytes 32800 | tf_op jit(solution)/shard_map/all_to_all | solution.py:221
  219.9 30.5 %scatter_custom_fusion.1 = f32[4096]{0:T(1024)S(1)} fusion(s32[8192]{0:T(1024)S(1)} %bitcast.222, f32[8192]{0:T(1024)S(1)} %bitcast.221, f32[]{:T(128)} %constant.26.clone.1), kind=kCustom, calls=%fused_computation.135 | custom fusion | bytes 16388 | tf_op jit(solution)/shard_map/scatter | solution.py:224
  250.4 2.4 multiply_reduce_fusion
  252.8 0.5 fusion.44
  253.3 2.6 fusion.46
  256.4 0.3 reshape_reshape.6
  256.9 17.1 %all_to_all.47 = f32[64,8,65]{2,1,0:T(8,128)S(1)} all-to-all(f32[64,8,65]{2,1,0:T(8,128)S(1)} %copy.59), channel_id=1, replica_groups=mesh['grp_0'=8,'grp_1'=2,'dev_0'=8,'dev_1'=4] {'grp_1','dev_0','dev_1'}, dimensions={0} | all-to-all | bytes 266240 | tf_op jit(solution)/shard_map/all_to_all | solution.py:48
  274.0 20.0 %all_to_all.48 = f32[8,1,65]{2,1,0:T(1,128)S(1)} all-to-all(f32[8,1,65]{2,1,0:T(1,128)S(1)} %bitcast.223), channel_id=1, replica_groups=mesh['grp_0'=8,'grp_1'=2,'dev_0'=8,'dev_1'=4] {'grp_0'}, dimensions={0} | all-to-all | bytes 4160 | tf_op jit(solution)/shard_map/all_to_all | solution.py:56
  294.0 10.0 %all_to_all.49 = f32[8,1,65]{2,1,0:T(1,128)S(1)} all-to-all(f32[8,1,65]{2,1,0:T(1,128)S(1)} %broadcast_in_dim.72), channel_id=1, replica_groups=mesh['grp_0'=8,'grp_1'=2,'dev_0'=8,'dev_1'=4] {'grp_0'}, dimensions={0} | all-to-all | bytes 4160 | tf_op jit(solution)/shard_map/all_to_all | solution.py:69
  304.1 17.6 %all_to_all.50 = f32[64,8,65]{2,1,0:T(8,128)S(1)} all-to-all(f32[64,8,65]{2,1,0:T(8,128)S(1)} %broadcast_in_dim.73), channel_id=1, replica_groups=mesh['grp_0'=8,'grp_1'=2,'dev_0'=8,'dev_1'=4] {'grp_1','dev_0','dev_1'}, dimensions={0} | all-to-all | bytes 266240 | tf_op jit(solution)/shard_map/all_to_all | solution.py:69
  321.7 0.2 slice.100
  322.0 0.2 reshape_reshape.7
  322.2 0.5 slice.136
  322.7 0.5 slice.137
  323.2 0.7 fusion.88
  (97 shorter events, 2.7 us)
Async XLA Ops:
  0.6 13.9 %copy-start = (bf16[4096,128]{1,0:T(8,128)(2,1)S(1)}, bf16[4096,128]{1,0:T(8,128)(2,1)}, u32[]{:S(2)}) copy-start(bf16[4096,128]{1,0:T(8,128)(2,1)} %param.13) | copy-start | bytes 3145732
  2.1 24.8 %all-to-all-start.1 = ((s32[1,32,256]{2,0,1:T(1,128)}), s32[1,32,256]{2,0,1:T(1,128)S(1)}, u32[]{:S(2)}, u32[]{:S(2)}) async-start(s32[1,32,256]{2,0,1:T(1,128)} %broadcast_in_dim.69), calls=%async_computation.1 | async-start | bytes 65536 | tf_op jit(solution)/shard_map/all_to_all | solution.py:202
  14.5 2.8 copy-start.21
  14.5 2.8 copy-start.23
  14.6 3.0 copy-start.17
  14.6 3.0 copy-start.19
  17.4 2.2 copy-start.2
  17.6 2.0 copy-start.13
  19.6 0.9 copy-start.10
  19.7 4.5 %copy-start.18 = (s32[125]{0:T(128)S(1)}, s32[125]{0:T(128)}, u32[]{:S(2)}) copy-start(s32[125]{0:T(128)} %constant.84) | copy-start | bytes 1504
  21.8 2.3 copy-start.14
  55.3 13.5 %copy-start.1 = (f32[125,16,16]{2,1,0:T(8,128)S(1)}, f32[125,16,16]{2,1,0:T(8,128)}, u32[]{:S(2)}) copy-start(f32[125,16,16]{2,1,0:T(8,128)} %gather_fusion.1) | copy-start | bytes 384004
  59.0 19.3 %all-to-all-start = ((f32[4,32,256]{2,0,1:T(4,128)}), f32[4,32,256]{2,0,1:T(4,128)S(1)}, u32[]{:S(2)}, u32[]{:S(2)}) async-start(f32[4,32,256]{2,0,1:T(4,128)} %select_bitcast_fusion), calls=%async_computation | async-start | bytes 262144 | tf_op jit(solution)/shard_map/all_to_all | solution.py:201
  85.3 48.9 %copy-start.15 = (f32[64,16]{0,1:T(8,128)S(1)}, f32[64,16]{0,1:T(8,128)}, u32[]{:S(2)}) copy-start(f32[64,16]{0,1:T(8,128)} %param.22) | copy-start | bytes 12292
  136.6 2.6 collective-permute-start
  137.9 5.7 %collective-permute-start.1 = (f32[16,2,4,64]{3,0,2,1:T(8,128)S(1)}, f32[16,2,4,64]{3,0,2,1:T(8,128)S(1)}, u32[]{:S(2)}, u32[]{:S(2)}) collective-permute-start(f32[16,2,4,64]{3,0,2,1:T(8,128)S(1)} %get-tuple-element.17), channel_id=1, source_target_pairs={{32,0},{64,32},{96,64},{128,96},{160,128},{192,160},{224,192},{256... | collective-permute-start | bytes 98312 | tf_op jit(solution)/shard_map/ppermute | solution.py:34
  143.6 0.7 copy-start.8
  144.3 12.1 %collective-permute-start.2 = (f32[16,8,2,64]{3,0,2,1:T(8,128)}, f32[16,8,2,64]{3,0,2,1:T(8,128)}, u32[]{:S(2)}, u32[]{:S(2)}) collective-permute-start(f32[16,8,2,64]{3,0,2,1:T(8,128)} %get-tuple-element.12), channel_id=1, source_target_pairs={{0,1},{1,2},{2,3},{3,4},{4,5},{5,6},{6,7},{7,8},{8,9},{9,10},{10,1... | collective-permute-start | bytes 196616 | tf_op jit(solution)/shard_map/ppermute | solution.py:32
  146.9 9.6 %collective-permute-start.3 = (f32[16,8,2,64]{3,0,2,1:T(8,128)}, f32[16,8,2,64]{3,0,2,1:T(8,128)}, u32[]{:S(2)}, u32[]{:S(2)}) collective-permute-start(f32[16,8,2,64]{3,0,2,1:T(8,128)} %get-tuple-element.13), channel_id=1, source_target_pairs={{1,0},{2,1},{3,2},{4,3},{5,4},{6,5},{7,6},{8,7},{9,8},{10,9},{11,1... | collective-permute-start | bytes 196616 | tf_op jit(solution)/shard_map/ppermute | solution.py:34
  156.5 2.2 copy-start.7
  158.7 1.3 copy-start.6
  160.0 1.3 copy-start.5
  161.4 1.3 copy-start.4
  167.4 3.5 %copy-start.16 = (f32[64,16]{0,1:T(8,128)S(1)}, f32[64,16]{0,1:T(8,128)}, u32[]{:S(2)}) copy-start(f32[64,16]{0,1:T(8,128)} %param.21) | copy-start | bytes 12292
  168.4 3.1 copy-start.9
  199.2 12.0 %copy-start.11 = (s32[1,1,32,256]{3,1,2,0:T(1,128)S(1)}, s32[1,1,32,256]{3,1,2,0:T(1,128)}, u32[]{:S(2)}) copy-start(s32[1,1,32,256]{3,1,2,0:T(1,128)} %copy.87) | copy-start | bytes 98308
  204.5 48.3 %copy-start.3 = (bf16[4096,128]{1,0:T(8,128)(2,1)S(1)}, bf16[4096,128]{1,0:T(8,128)(2,1)}, u32[]{:S(2)}) copy-start(bf16[4096,128]{1,0:T(8,128)(2,1)} %copy-done.2) | copy-start | bytes 3145732
  204.5 15.4 %all-to-all-start.2 = ((f32[32,1,256]{2,1,0:T(1,128)}), f32[32,1,256]{2,1,0:T(1,128)S(1)}, u32[]{:S(2)}, u32[]{:S(2)}) async-start(f32[32,1,256]{2,1,0:T(1,128)} %bitcast.78), calls=%async_computation.2 | async-start | bytes 65536 | tf_op jit(solution)/shard_map/all_to_all | solution.py:221
  250.4 5.7 %copy-start.12 = (f32[4096]{0:T(1024)}, f32[4096]{0:T(1024)S(1)}, u32[]{:S(2)}) copy-start(f32[4096]{0:T(1024)S(1)} %scatter_custom_fusion.1) | copy-start | bytes 49156
  250.4 2.9 copy-start.20
  253.3 2.8 copy-start.22
where the time goes:
time: 326 us; the launch traced here: 324 us
  local copies, waits for them, and re-layouts  112 us (34%)
  blocking collectives  64.7 us (20%)
  other arithmetic  61.7 us (19%)
  starting transfers between devices  37.2 us (11%)
  matrix products  25.2 us (8%)
  waiting for transfers between devices  21.6 us (7%)
    scatter-add x1, other arithmetic, shards(): moments = jnp.zeros((NODES, BOXES), jnp.float32).at[:, slot_boxes].add(we...  45.1 us
    gather x2, local copies, waits for them, and re-layouts, shards(): picked = jnp.where(is_used[None], packed[:, safe_index], 0.0)  30.7 us
    scatter x1, local copies, waits for them, and re-layouts, shards(): jnp.zeros((atom_count,), jnp.float32).at[target_rows]  30.5 us
    gather x1, local copies, waits for them, and re-layouts, shards(): expansion[:, slot_boxes]  27.7 us
    all_to_all x2, blocking collectives, sent_to_all(): return lax.all_to_all(copies, axis, split_axis=0, concat_axis=0, tiled=True)  27.6 us
    all_to_all x1, blocking collectives, sum_in_two_steps(): lax.all_to_all(nearer, far, split_axis=0, concat_axis=0, tiled=True)  20 us
    all_to_all x1, blocking collectives, sent_and_summed(): lax.all_to_all(blocks, axis, split_axis=0, concat_axis=0, tiled=True)  17.1 us
    all_to_all x1, starting transfers between devices, shards(): lax.all_to_all(slot_box[None], DEV, split_axis=1, concat_axis=1, tiled=True)  10.2 us
  transfers between devices with their start and end apart: 7, of which 3 were waited for; matrix products, arithmetic and copies ran while one was open for 6% of the time, Pallas kernels for 0%

commit v1 on v0

--- a/solution.py
+++ b/solution.py
@@ -92,6 +92,14 @@
     for a in arrays:
         ends.append(ends[-1] + a.size)
     total = nested_sum(jnp.concatenate([a.ravel() for a in arrays]), axis)
+    return tuple((total[b:e].reshape(a.shape) for a, b, e in zip(arrays, ends, ends[1:])))
+
+
+def summed_everywhere(arrays, axes):
+    ends = [0]
+    for a in arrays:
+        ends.append(ends[-1] + a.size)
+    total = lax.psum(jnp.concatenate([a.ravel() for a in arrays]), axes)
     return tuple((total[b:e].reshape(a.shape) for a, b, e in zip(arrays, ends, ends[1:])))
 
 
@@ -242,8 +250,8 @@
         )
         * grad_scale
     )
-    grad_in, grad_mid, grad_head, grad_species = together(
-        (in_part, mid_part, head_part, species_part), ("grp_0", ("grp_1", "dev_0", "dev_1"))
+    grad_in, grad_mid, grad_head, grad_species = summed_everywhere(
+        (in_part, mid_part, head_part, species_part), GRP_DEV
     )
     return (potential, grad_in, grad_mid, grad_head, grad_species)
 

time: 326 us -> 539 us (1.65)
  the two profiles are of different devices: /device:TPU:8 before, /device:TPU:1 now
where the time goes in v1:
time: 539 us; the launch traced here: 538 us
  waiting for transfers between devices  283 us (53%)
  local copies, waits for them, and re-layouts  113 us (21%)
  other arithmetic  62.3 us (12%)
  starting transfers between devices  39.8 us (7%)
  matrix products  25.1 us (5%)
  between operations  14.6 us (3%)
    psum x1, waiting for transfers between devices, summed_everywhere(): total = lax.psum(jnp.concatenate([a.ravel() for a in arrays]), axes)  262 us
    scatter-add x1, other arithmetic, shards(): moments = jnp.zeros((NODES, BOXES), jnp.float32).at[:, slot_boxes].add(we...  45.1 us
    gather x2, local copies, waits for them, and re-layouts, shards(): picked = jnp.where(is_used[None], packed[:, safe_index], 0.0)  30.7 us
    scatter x1, local copies, waits for them, and re-layouts, shards(): jnp.zeros((atom_count,), jnp.float32).at[target_rows]  30.5 us
    gather x1, local copies, waits for them, and re-layouts, shards(): expansion[:, slot_boxes]  27.8 us
  transfers between devices with their start and end apart: 8, of which 5 were waited for; matrix products, arithmetic and copies ran while one was open for 4% of the time, Pallas kernels for 0%

profile of v1, /device:TPU:1, one launch (start us, length us, event | category | flops | bytes accessed | tf_op | source)
XLA Modules:
  0.0 538.1 jit_solution(3045653930925909940)
XLA Ops:
  7.2 1.5 broadcast_in_dim.60
  8.7 10.5 %all-to-all-start.1 = ((s32[1,32,256]{2,0,1:T(1,128)}), s32[1,32,256]{2,0,1:T(1,128)S(1)}, u32[]{:S(2)}, u32[]{:S(2)}) async-start(s32[1,32,256]{2,0,1:T(1,128)} %broadcast_in_dim.60), calls=%async_computation.1 | async-start | bytes 65536 | tf_op jit(solution)/shard_map/all_to_all | solution.py:210
  19.2 1.4 fusion.69
  20.5 0.8 broadcast_compare_fusion
  21.4 2.8 multiply_convert_fusion.1
  24.2 0.2 fusion.60
  24.4 2.0 multiply_reduce_fusion.1
  26.5 0.6 copy.33
  27.4 1.3 copy.37
  28.7 2.1 concatenate.18
  31.1 2.8 gather_fusion.1
  33.9 0.6 broadcast_clamp_fusion
  34.5 27.8 %gather_fusion = f32[8192,4]{1,0:T(8,128)} fusion(f32[4,4096]{0,1:T(8,128)S(1)} %copy.33, s32[8192]{0:T(1024)S(1)} %get-tuple-element.41), kind=kCustom, calls=%fused_computation | custom fusion | bytes 294912 | tf_op jit(solution)/shard_map/gather | solution.py:207
  62.3 2.9 copy.34
  65.2 0.7 select_bitcast_fusion
  65.9 9.2 %all-to-all-start = ((f32[4,32,256]{2,0,1:T(4,128)}), f32[4,32,256]{2,0,1:T(4,128)S(1)}, u32[]{:S(2)}, u32[]{:S(2)}) async-start(f32[4,32,256]{2,0,1:T(4,128)} %select_bitcast_fusion), calls=%async_computation | async-start | bytes 262144 | tf_op jit(solution)/shard_map/all_to_all | solution.py:209
  75.1 0.9 fusion.86
  76.1 8.4 %all-to-all-done = f32[4,32,256]{2,0,1:T(4,128)S(1)} async-done(((f32[4,32,256]{2,0,1:T(4,128)}), f32[4,32,256]{2,0,1:T(4,128)S(1)}, u32[]{:S(2)}, u32[]{:S(2)}) %all-to-all-start) | async-done | bytes 131104 | tf_op jit(solution)/shard_map/all_to_all | solution.py:209
  84.6 0.3 multiply_add_fusion.11
  84.9 0.3 multiply_add_fusion.7
  85.2 0.3 multiply_add_fusion.3
  86.0 1.9 broadcast_multiply_fusion
  87.9 2.0 mul.1040
  89.9 1.5 multiply_bitcast_fusion
  91.5 3.8 copy.35
  95.3 45.1 %scatter_custom_fusion = f32[64,1024]{0,1:T(8,128)} fusion(s32[8192]{0:T(1024)S(1)} %bitcast.212, f32[8192,64]{1,0:T(8,128)} %copy.35, f32[]{:T(128)} %constant.26.clone.1), kind=kCustom, calls=%fused_computation.69 | custom fusion | flops 524288 | bytes 262656 | tf_op jit(solution)/shard_map/scatter-add | solution.py:219
  140.4 2.4 convolution_bitcast_fusion.7
  142.8 6.6 %collective-permute-start = (f32[16,2,4,64]{3,0,2,1:T(8,128)S(1)}, f32[16,2,4,64]{3,0,2,1:T(8,128)S(1)}, u32[]{:S(2)}, u32[]{:S(2)}) collective-permute-start(f32[16,2,4,64]{3,0,2,1:T(8,128)S(1)} %get-tuple-element.16), channel_id=1, source_target_pairs={{0,32},{32,64},{64,96},{96,128},{128,160},{160,192},{192,224},{224... | collective-permute-start | bytes 98312 | tf_op jit(solution)/shard_map/ppermute | solution.py:32
  149.4 1.9 collective-permute-start.1
  151.3 3.6 collective-permute-done.1
  155.0 0.7 fusion.87
  155.7 2.4 collective-permute-start.2
  158.1 1.3 collective-permute-start.3
  159.4 1.4 copy.71
  160.8 2.7 copy.44
  163.6 0.5 collective-permute-done.3
  164.1 2.2 convolution_bitcast_fusion
  166.3 1.3 convolution_bitcast_fusion.2
  167.6 1.3 convolution_bitcast_fusion.3
  168.9 1.3 convolution_bitcast_fusion.4
  170.3 1.3 convolution_bitcast_fusion.5
  171.6 1.3 convolution_bitcast_fusion.1
  172.9 1.0 fusion.14
  173.9 1.0 fusion.41
  174.9 1.0 fusion.38
  176.0 1.0 fusion.35
  177.0 1.2 fusion.32
  178.3 0.2 reshape.1138
  178.4 0.4 convolution_bitcast_fusion.6
  178.8 0.2 copy.43
  179.0 27.8 %gather_fusion.2 = f32[8192,64]{1,0:T(8,128)} fusion(f32[64,1024]{0,1:T(8,128)S(1)} %copy.43, s32[8192]{0:T(1024)S(1)} %copy-done.9), kind=kCustom, calls=%fused_computation.2 | custom fusion | bytes 4227072 | tf_op jit(solution)/shard_map/gather | solution.py:226
  206.8 5.2 fusion.1
  212.1 7.9 %all-to-all-start.2 = ((f32[32,1,256]{2,1,0:T(1,128)}), f32[32,1,256]{2,1,0:T(1,128)S(1)}, u32[]{:S(2)}, u32[]{:S(2)}) async-start(f32[32,1,256]{2,1,0:T(1,128)} %bitcast.78), calls=%async_computation.2 | async-start | bytes 65536 | tf_op jit(solution)/shard_map/all_to_all | solution.py:229
  220.1 8.6 %all-to-all-done.2 = f32[32,1,256]{2,1,0:T(1,128)S(1)} async-done(((f32[32,1,256]{2,1,0:T(1,128)}), f32[32,1,256]{2,1,0:T(1,128)S(1)}, u32[]{:S(2)}, u32[]{:S(2)}) %all-to-all-start.2) | async-done | bytes 32800 | tf_op jit(solution)/shard_map/all_to_all | solution.py:229
  228.7 30.5 %scatter_custom_fusion.1 = f32[4096]{0:T(1024)S(1)} fusion(s32[8192]{0:T(1024)S(1)} %bitcast.220, f32[8192]{0:T(1024)S(1)} %bitcast.219, f32[]{:T(128)} %constant.26.clone.1), kind=kCustom, calls=%fused_computation.138 | custom fusion | bytes 16388 | tf_op jit(solution)/shard_map/scatter | solution.py:232
  259.2 2.4 multiply_convert_fusion
  261.6 0.5 fusion.44
  262.1 2.6 fusion.46
  264.9 0.2 fusion.47
  265.1 0.7 pad_maximum_fusion.1
  265.8 261.5 %all-reduce.3.cloned.1.call-done = f32[32902]{0:T(1024)} async-done(((f32[32902]{0:T(1024)}), f32[32902]{0:T(1024)}) %all-reduce.3.cloned.1.call-update) | async-done | bytes 131624 | tf_op jit(solution)/shard_map/psum | solution.py:102
  527.3 1.5 slice_bitcast_fusion.10
  528.9 1.2 slice.126
  530.0 1.2 slice.127
  (86 shorter events, 1.6 us)
Async XLA Ops:
  7.2 14.2 %copy-start = (bf16[4096,128]{1,0:T(8,128)(2,1)S(1)}, bf16[4096,128]{1,0:T(8,128)(2,1)}, u32[]{:S(2)}) copy-start(bf16[4096,128]{1,0:T(8,128)(2,1)} %param.13) | copy-start | bytes 3145732
  8.7 25.2 %all-to-all-start.1 = ((s32[1,32,256]{2,0,1:T(1,128)}), s32[1,32,256]{2,0,1:T(1,128)S(1)}, u32[]{:S(2)}, u32[]{:S(2)}) async-start(s32[1,32,256]{2,0,1:T(1,128)} %broadcast_in_dim.60), calls=%async_computation.1 | async-start | bytes 65536 | tf_op jit(solution)/shard_map/all_to_all | solution.py:210
  21.4 2.8 copy-start.21
  21.4 2.8 copy-start.23
  21.4 3.0 copy-start.17
  21.4 3.0 copy-start.19
  24.2 2.2 copy-start.2
  24.4 2.0 copy-start.13
  26.4 0.9 copy-start.10
  26.5 4.6 copy-start.18
  28.7 2.3 copy-start.14
  62.3 12.9 %copy-start.1 = (f32[125,16,16]{2,1,0:T(8,128)S(1)}, f32[125,16,16]{2,1,0:T(8,128)}, u32[]{:S(2)}) copy-start(f32[125,16,16]{2,1,0:T(8,128)} %gather_fusion.1) | copy-start | bytes 384004
  65.9 18.6 %all-to-all-start = ((f32[4,32,256]{2,0,1:T(4,128)}), f32[4,32,256]{2,0,1:T(4,128)S(1)}, u32[]{:S(2)}, u32[]{:S(2)}) async-start(f32[4,32,256]{2,0,1:T(4,128)} %select_bitcast_fusion), calls=%async_computation | async-start | bytes 262144 | tf_op jit(solution)/shard_map/all_to_all | solution.py:209
  91.5 48.9 %copy-start.15 = (f32[64,16]{0,1:T(8,128)S(1)}, f32[64,16]{0,1:T(8,128)}, u32[]{:S(2)}) copy-start(f32[64,16]{0,1:T(8,128)} %param.22) | copy-start | bytes 12292
  142.8 8.5 %collective-permute-start = (f32[16,2,4,64]{3,0,2,1:T(8,128)S(1)}, f32[16,2,4,64]{3,0,2,1:T(8,128)S(1)}, u32[]{:S(2)}, u32[]{:S(2)}) collective-permute-start(f32[16,2,4,64]{3,0,2,1:T(8,128)S(1)} %get-tuple-element.16), channel_id=1, source_target_pairs={{0,32},{32,64},{64,96},{96,128},{128,160},{160,192},{192,224},{224... | collective-permute-start | bytes 98312 | tf_op jit(solution)/shard_map/ppermute | solution.py:32
  149.4 5.6 %collective-permute-start.1 = (f32[16,2,4,64]{3,0,2,1:T(8,128)S(1)}, f32[16,2,4,64]{3,0,2,1:T(8,128)S(1)}, u32[]{:S(2)}, u32[]{:S(2)}) collective-permute-start(f32[16,2,4,64]{3,0,2,1:T(8,128)S(1)} %get-tuple-element.17), channel_id=1, source_target_pairs={{32,0},{64,32},{96,64},{128,96},{160,128},{192,160},{224,192},{256... | collective-permute-start | bytes 98312 | tf_op jit(solution)/shard_map/ppermute | solution.py:34
  154.9 0.7 copy-start.8
  155.7 7.9 %collective-permute-start.2 = (f32[16,8,2,64]{3,0,2,1:T(8,128)}, f32[16,8,2,64]{3,0,2,1:T(8,128)}, u32[]{:S(2)}, u32[]{:S(2)}) collective-permute-start(f32[16,8,2,64]{3,0,2,1:T(8,128)} %get-tuple-element.12), channel_id=1, source_target_pairs={{0,1},{1,2},{2,3},{3,4},{4,5},{5,6},{6,7},{7,8},{8,9},{9,10},{10,1... | collective-permute-start | bytes 196616 | tf_op jit(solution)/shard_map/ppermute | solution.py:32
  158.1 6.0 %collective-permute-start.3 = (f32[16,8,2,64]{3,0,2,1:T(8,128)}, f32[16,8,2,64]{3,0,2,1:T(8,128)}, u32[]{:S(2)}, u32[]{:S(2)}) collective-permute-start(f32[16,8,2,64]{3,0,2,1:T(8,128)} %get-tuple-element.13), channel_id=1, source_target_pairs={{1,0},{2,1},{3,2},{4,3},{5,4},{6,5},{7,6},{8,7},{9,8},{10,9},{11,1... | collective-permute-start | bytes 196616 | tf_op jit(solution)/shard_map/ppermute | solution.py:34
  163.6 2.7 copy-start.7
  166.3 1.3 copy-start.6
  167.6 1.3 copy-start.5
  168.9 1.3 copy-start.4
  174.9 3.5 copy-start.16
  176.0 3.1 copy-start.9
  206.8 13.2 %copy-start.11 = (s32[1,1,32,256]{3,1,2,0:T(1,128)S(1)}, s32[1,1,32,256]{3,1,2,0:T(1,128)}, u32[]{:S(2)}) copy-start(s32[1,1,32,256]{3,1,2,0:T(1,128)} %copy.71) | copy-start | bytes 98308
  212.1 49.5 %copy-start.3 = (bf16[4096,128]{1,0:T(8,128)(2,1)S(1)}, bf16[4096,128]{1,0:T(8,128)(2,1)}, u32[]{:S(2)}) copy-start(bf16[4096,128]{1,0:T(8,128)(2,1)} %copy-done.2) | copy-start | bytes 3145732
  212.1 16.6 %all-to-all-start.2 = ((f32[32,1,256]{2,1,0:T(1,128)}), f32[32,1,256]{2,1,0:T(1,128)S(1)}, u32[]{:S(2)}, u32[]{:S(2)}) async-start(f32[32,1,256]{2,1,0:T(1,128)} %bitcast.78), calls=%async_computation.2 | async-start | bytes 65536 | tf_op jit(solution)/shard_map/all_to_all | solution.py:229
  220.0 307.4 %all-reduce.3.cloned.1.call-start = ((), (), s32[]{:S(2)}) async-start(), calls=%async_computation.3 | async-start | bytes 270336 | tf_op jit(solution)/shard_map/psum | solution.py:102
  259.2 5.7 %copy-start.12 = (f32[4096]{0:T(1024)}, f32[4096]{0:T(1024)S(1)}, u32[]{:S(2)}) copy-start(f32[4096]{0:T(1024)S(1)} %scatter_custom_fusion.1) | copy-start | bytes 49156
  259.2 2.9 copy-start.20
  262.1 2.8 copy-start.22
Sparse Core Ops, SparseCore 0:
  265.9 261.3 all-reduce.2

commit v2 on v1

--- a/solution.py
+++ b/solution.py
@@ -4,6 +4,7 @@
 import jax.numpy as jnp
 import numpy as np
 from jax import lax
+from jax.experimental import pallas as pl
 from jax.sharding import Mesh
 from jax.sharding import PartitionSpec as P
 
@@ -101,6 +102,141 @@
         ends.append(ends[-1] + a.size)
     total = lax.psum(jnp.concatenate([a.ravel() for a in arrays]), axes)
     return tuple((total[b:e].reshape(a.shape) for a, b, e in zip(arrays, ends, ends[1:])))
+
+
+def split_three(x):
+    high = lax.reduce_precision(x, exponent_bits=8, mantissa_bits=7)
+    rest = x - high
+    middle = lax.reduce_precision(rest, exponent_bits=8, mantissa_bits=7)
+    return high, middle, rest - middle
+
+
+def pieces_bf16(x, axis):
+    return jnp.concatenate([p.astype(jnp.bfloat16) for p in split_three(x)], axis=axis)
+
+
+def atoms_to_slots_kernel(table_ref, high_ref, low_ref, out_ref):
+    rows, tile = out_ref.shape
+    side = table_ref.shape[1]
+    lines = lax.broadcasted_iota(jnp.int32, (side, tile), 0)
+    low = (lines == low_ref[...]).astype(jnp.bfloat16)
+    parts = jnp.dot(table_ref[...], low, preferred_element_type=jnp.float32)
+    block = rows * side
+    whole = parts[:block] + parts[block : 2 * block] + parts[2 * block :]
+    high = (lines == high_ref[...]).astype(jnp.float32)
+    for row in range(rows):
+        out_ref[row : row + 1, :] = jnp.sum(
+            whole[row * side : (row + 1) * side] * high, axis=0, keepdims=True
+        )
+
+
+def atoms_to_slots(values, high, low, tile=1024):
+    rows, count = values.shape
+    side = int(round(math.sqrt(count)))
+    table = pieces_bf16(values.reshape(rows * side, side), 0)
+    slots = high.shape[1]
+    return pl.pallas_call(
+        atoms_to_slots_kernel,
+        grid=(slots // tile,),
+        in_specs=[
+            pl.BlockSpec(table.shape, lambda i: (0, 0)),
+            pl.BlockSpec((1, tile), lambda i: (0, i)),
+            pl.BlockSpec((1, tile), lambda i: (0, i)),
+        ],
+        out_specs=pl.BlockSpec((rows, tile), lambda i: (0, i)),
+        out_shape=jax.ShapeDtypeStruct((rows, slots), jnp.float32),
+    )(table, high, low)
+
+
+def slots_to_atoms_kernel(value_ref, high_ref, low_ref, out_ref):
+    @pl.when(pl.program_id(0) == 0)
+    def _():
+        out_ref[...] = jnp.zeros_like(out_ref)
+
+    side = out_ref.shape[1]
+    tile = high_ref.shape[1]
+    lines = lax.broadcasted_iota(jnp.int32, (side, tile), 0)
+    hit = lines == high_ref[...]
+    low = (lines == low_ref[...]).astype(jnp.bfloat16)
+    stacked = jnp.concatenate(
+        [jnp.where(hit, value_ref[k : k + 1, :], 0.0).astype(jnp.bfloat16) for k in range(3)],
+        axis=0,
+    )
+    out_ref[...] += lax.dot_general(
+        stacked, low, (((1,), (1,)), ((), ())), preferred_element_type=jnp.float32
+    )
+
+
+def slots_to_atoms(values, high, low, count, tile=1024):
+    side = int(round(math.sqrt(count)))
+    pieces = jnp.stack(split_three(values), 0)
+    slots = values.shape[0]
+    parts = pl.pallas_call(
+        slots_to_atoms_kernel,
+        grid=(slots // tile,),
+        in_specs=[
+            pl.BlockSpec((3, tile), lambda i: (0, i)),
+            pl.BlockSpec((1, tile), lambda i: (0, i)),
+            pl.BlockSpec((1, tile), lambda i: (0, i)),
+        ],
+        out_specs=pl.BlockSpec((3 * side, side), lambda i: (0, 0)),
+        out_shape=jax.ShapeDtypeStruct((3 * side, side), jnp.float32),
+    )(pieces, high, low)
+    return (parts[:side] + parts[side : 2 * side] + parts[2 * side :]).reshape(count)
+
+
+def box_sum_kernel(value_ref, box_ref, out_ref):
+    @pl.when(pl.program_id(0) == 0)
+    def _():
+        out_ref[...] = jnp.zeros_like(out_ref)
+
+    boxes = out_ref.shape[1]
+    tile = box_ref.shape[1]
+    hot = (lax.broadcasted_iota(jnp.int32, (boxes, tile), 0) == box_ref[...]).astype(jnp.bfloat16)
+    out_ref[...] += lax.dot_general(
+        value_ref[...], hot, (((1,), (1,)), ((), ())), preferred_element_type=jnp.float32
+    )
+
+
+def box_sum(values, box, boxes, tile=1024):
+    rows, slots = values.shape
+    stacked = pieces_bf16(values, 0)
+    parts = pl.pallas_call(
+        box_sum_kernel,
+        grid=(slots // tile,),
+        in_specs=[
+            pl.BlockSpec((3 * rows, tile), lambda i: (0, i)),
+            pl.BlockSpec((1, tile), lambda i: (0, i)),
+        ],
+        out_specs=pl.BlockSpec((3 * rows, boxes), lambda i: (0, 0)),
+        out_shape=jax.ShapeDtypeStruct((3 * rows, boxes), jnp.float32),
+    )(stacked, box)
+    return parts[:rows] + parts[rows : 2 * rows] + parts[2 * rows :]
+
+
+def box_pick_kernel(table_ref, box_ref, weight_ref, out_ref):
+    boxes = table_ref.shape[1]
+    rows, tile = weight_ref.shape
+    hot = (lax.broadcasted_iota(jnp.int32, (boxes, tile), 0) == box_ref[...]).astype(jnp.bfloat16)
+    parts = jnp.dot(table_ref[...], hot, preferred_element_type=jnp.float32)
+    picked = parts[:rows] + parts[rows : 2 * rows] + parts[2 * rows :]
+    out_ref[...] = jnp.sum(weight_ref[...] * picked, axis=0, keepdims=True)
+
+
+def box_pick(table, box, weights, tile=1024):
+    rows, slots = weights.shape
+    stacked = pieces_bf16(table, 0)
+    return pl.pallas_call(
+        box_pick_kernel,
+        grid=(slots // tile,),
+        in_specs=[
+            pl.BlockSpec(stacked.shape, lambda i: (0, 0)),
+            pl.BlockSpec((1, tile), lambda i: (0, i)),
+            pl.BlockSpec((rows, tile), lambda i: (0, i)),
+        ],
+        out_specs=pl.BlockSpec((1, tile), lambda i: (0, i)),
+        out_shape=jax.ShapeDtypeStruct((1, slots), jnp.float32),
+    )(stacked, box, weights)[0]
 
 
 def shell_table():
@@ -202,9 +338,11 @@
         species_charge, species_hot, precision=lax.Precision.HIGHEST
     )
     is_used = send_list >= 0
-    safe_index = jnp.where(is_used, send_list, 0)
+    side = int(round(math.sqrt(atom_count)))
+    atom_high = jnp.where(is_used, send_list // side, -1).reshape(1, -1)
+    atom_low = (send_list % side).reshape(1, -1)
     packed = jnp.concatenate([charge[None, :], positions], axis=0)
-    picked = jnp.where(is_used[None], packed[:, safe_index], 0.0)
+    picked = atoms_to_slots(packed, atom_high, atom_low).reshape(4, *send_list.shape)
     arrived, box_ids = (
         lax.all_to_all(picked, DEV, split_axis=1, concat_axis=1, tiled=True),
         lax.all_to_all(slot_box[None], DEV, split_axis=1, concat_axis=1, tiled=True),
@@ -213,24 +351,17 @@
     arrived_coords = arrived[1:].reshape(3, -1)
     slot_boxes = box_ids.reshape(-1)
     weight_table = node_weights(arrived_coords)
-    moments = (
-        jnp.zeros((NODES, BOXES), jnp.float32)
-        .at[:, slot_boxes]
-        .add(weight_table * arrived_charge[None, :])
-    )
+    moments = box_sum(weight_table * arrived_charge[None, :], slot_boxes[None, :], BOXES)
     node_grid = moments.reshape(NODES, BZ, BX, BY)
     reduced = jnp.einsum("nr,nzxy->rzxy", compress_v, node_grid, precision=lax.Precision.HIGHEST)
     padded = extended_2(reduced, ((GRP, 1), (DEV, 2)), 2)
     local_terms = translate(padded, m2l_kernels)
     expansion = jnp.dot(expand_u, local_terms.reshape(RANK, BOXES), precision=lax.Precision.HIGHEST)
-    slot_potential = jnp.sum(weight_table * expansion[:, slot_boxes], axis=0).reshape(
+    slot_potential = box_pick(expansion, slot_boxes[None, :], weight_table).reshape(
         send_list.shape
     )
     returned = lax.all_to_all(slot_potential, DEV, split_axis=0, concat_axis=0, tiled=True)
-    target_rows = jnp.where(is_used, send_list, atom_count).reshape(-1)
-    potential = (
-        jnp.zeros((atom_count,), jnp.float32).at[target_rows].set(returned.reshape(-1), mode="drop")
-    )
+    potential = slots_to_atoms(returned.reshape(-1), atom_high, atom_low, atom_count)
     head_part = jnp.sum(potential[:, None] * hidden_two, axis=0) * grad_scale
     species_part = jnp.dot(species_hot, potential, precision=lax.Precision.HIGHEST) * grad_scale
     delta_two = (potential[:, None] * w_head[None, :] * silu_slope(pre_two)).astype(jnp.bfloat16)
@@ -250,8 +381,8 @@
         )
         * grad_scale
     )
-    grad_in, grad_mid, grad_head, grad_species = summed_everywhere(
-        (in_part, mid_part, head_part, species_part), GRP_DEV
+    grad_in, grad_mid, grad_head, grad_species = together(
+        (in_part, mid_part, head_part, species_part), ("grp_0", ("grp_1", "dev_0", "dev_1"))
     )
     return (potential, grad_in, grad_mid, grad_head, grad_species)
 

time: 539 us -> 204 us (0.38)
  waiting for transfers between devices: 283 us -> 9.31 us
  local copies, waits for them, and re-layouts: 113 us -> 11.7 us
  blocking collectives: 0 us -> 86.6 us
  other arithmetic: 62.3 us -> 13.7 us
  Pallas kernels: 0 us -> 28.5 us
  between operations: 14.6 us -> 1.34 us
  starting transfers between devices: 39.8 us -> 29 us
    psum x1 -> x0, waiting for transfers between devices: 262 us -> none  [summed_everywhere(): total = lax.psum(jnp.concatenate([a.ravel() for a in arrays]), axes)]
    all_to_all x0 -> x5, blocking collectives: none -> 86.6 us  [the longest x2 29.2 us: sent_to_all(): return lax.all_to_all(copies, axis, split_axis=0, concat_axis=0, tiled=True)]
    gather x3 -> x0, local copies, waits for them, and re-layouts: 58.5 us -> none  [the longest x2 30.7 us: shards(): picked = jnp.where(is_used[None], packed[:, safe_index], 0.0)]
    scatter-add x1 -> x0, other arithmetic: 45.1 us -> none  [shards(): moments = jnp.zeros((NODES, BOXES), jnp.float32).at[:, slot_boxes].add(we...]
    scatter x1 -> x0, local copies, waits for them, and re-layouts: 30.5 us -> none  [shards(): jnp.zeros((atom_count,), jnp.float32).at[target_rows]]
    pallas_call x0 -> x4, Pallas kernels: none -> 28.5 us  [the longest x1 9.29 us: box_sum(): pl.pallas_call(box_sum_kernel, grid=(slots // tile,), in_specs=[pl.BlockS...]
    all_to_all x1 -> x0, waiting for transfers between devices: 8.63 us -> none  [shards(): lax.all_to_all(slot_potential, DEV, split_axis=0, concat_axis=0, tiled=True)]
    all_to_all x1 -> x0, starting transfers between devices: 7.87 us -> none  [shards(): lax.all_to_all(slot_potential, DEV, split_axis=0, concat_axis=0, tiled=True)]
  transfers between devices with their start and end apart: 8 -> 6, of which waited for: 5 -> 4; matrix products, arithmetic and copies ran while one was open for 4% -> 6% of each run, Pallas kernels for 0% -> 0%
where the time goes in v2:
time: 204 us; the launch traced here: 202 us
  blocking collectives  86.6 us (42%)
  starting transfers between devices  29 us (14%)
  Pallas kernels  28.5 us (14%)
  matrix products  22.2 us (11%)
  other arithmetic  13.7 us (7%)
  local copies, waits for them, and re-layouts  11.7 us (6%)
  waiting for transfers between devices  9.31 us (5%)
    all_to_all x2, blocking collectives, sent_to_all(): return lax.all_to_all(copies, axis, split_axis=0, concat_axis=0, tiled=True)  29.2 us
    all_to_all x1, blocking collectives, shards(): lax.all_to_all(slot_potential, DEV, split_axis=0, concat_axis=0, tiled=True)  21.5 us
    all_to_all x1, blocking collectives, sum_in_two_steps(): lax.all_to_all(nearer, far, split_axis=0, concat_axis=0, tiled=True)  19.5 us
    all_to_all x1, blocking collectives, sent_and_summed(): lax.all_to_all(blocks, axis, split_axis=0, concat_axis=0, tiled=True)  16.4 us
    all_to_all x1, starting transfers between devices, shards(): lax.all_to_all(picked, DEV, split_axis=1, concat_axis=1, tiled=True)  10.5 us
    pallas_call x1, Pallas kernels, box_sum(): pl.pallas_call(box_sum_kernel, grid=(slots // tile,), in_specs=[pl.BlockS...  9.29 us
    ppermute x2, starting transfers between devices, extended_2(): lax.ppermute(tail, axis, [(i, (i + 1) % count) for i in range(ends)])  8.02 us
    pallas_call x1, Pallas kernels, box_pick(): pl.pallas_call(box_pick_kernel, grid=(slots // tile,), in_specs=[pl.Block...  7.76 us
  transfers between devices with their start and end apart: 6, of which 4 were waited for; matrix products, arithmetic and copies ran while one was open for 6% of the time, Pallas kernels for 0%

profile of v2, /device:TPU:1, one launch (start us, length us, event | category | flops | bytes accessed | tf_op | source)
XLA Modules:
  0.0 202.2 jit_solution(8685546550944649019)
XLA Ops:
  0.7 1.2 copy-done
  1.9 2.7 %multiply_convert_fusion.1 = (bf16[4096,128]{1,0:T(8,128)(2,1)S(1)}, f32[4096,128]{1,0:T(8,128)}) fusion(bf16[4096,128]{1,0:T(8,128)(2,1)S(1)} %copy-done, bf16[128,128]{1,0:T(8,128)(2,1)} %param.16), kind=kOutput, calls=%fused_computation.14 | convolution fusion | flops 136839168 | bytes 4227072 | tf_op jit(solution)/shard_map/dot_general | solution.py:330
  4.8 2.0 multiply_reduce_fusion.1
  7.1 0.6 copy.69
  7.7 0.6 copy.70
  8.4 0.7 pad_maximum_fusion.3.table_ref
  9.1 6.5 %shard_map.164 = f32[4,8192]{1,0:T(4,128)} custom-call(bf16[768,64]{1,0:T(8,128)(2,1)} %pad_maximum_fusion.3.table_ref, s32[1,8192]{1,0:T(1,128)} %bitcast.195, s32[1,8192]{1,0:T(1,128)} %bitcast.197), custom_call_target="tpu_custom_call" | custom-call | tf_op jit(solution)/shard_map/pallas_call | solution.py:138
  15.6 10.5 %all-to-all-start = ((f32[4,32,256]{2,0,1:T(4,128)}), f32[4,32,256]{2,0,1:T(4,128)S(1)}, u32[]{:S(2)}, u32[]{:S(2)}) async-start(f32[4,32,256]{2,0,1:T(4,128)} %bitcast.194), calls=%async_computation | async-start | bytes 262144 | tf_op jit(solution)/shard_map/all_to_all | solution.py:347
  26.2 0.4 copy.34
  26.7 0.6 broadcast_in_dim.15
  27.4 0.7 gather_fusion
  28.5 0.9 fusion.89
  29.3 6.1 %all-to-all-done = f32[4,32,256]{2,0,1:T(4,128)S(1)} async-done(((f32[4,32,256]{2,0,1:T(4,128)}), f32[4,32,256]{2,0,1:T(4,128)S(1)}, u32[]{:S(2)}, u32[]{:S(2)}) %all-to-all-start) | async-done | bytes 131104 | tf_op jit(solution)/shard_map/all_to_all | solution.py:347
  35.5 4.5 %all-to-all-start.1 = ((s32[1,32,256]{2,0,1:T(1,128)}), s32[1,32,256]{2,0,1:T(1,128)}, u32[]{:S(2)}, u32[]{:S(2)}) async-start(s32[1,32,256]{2,0,1:T(1,128)} %broadcast_in_dim.15), calls=%async_computation.1 | async-start | bytes 65536 | tf_op jit(solution)/shard_map/all_to_all | solution.py:348
  40.0 0.7 fusion.93
  40.7 0.3 multiply_add_fusion.3
  41.0 0.3 multiply_add_fusion.11
  41.3 0.3 multiply_add_fusion.7
  41.6 0.2 pad_maximum_fusion.4
  42.2 1.9 broadcast_multiply_fusion
  44.0 2.0 mul.1029.weight_ref
  46.0 1.3 reduce-precision_convert_fusion.1
  47.4 1.8 pad_maximum_fusion.value_ref
  49.2 9.3 %shard_map.165 = f32[192,1024]{1,0:T(8,128)} custom-call(bf16[192,8192]{1,0:T(8,128)(2,1)} %pad_maximum_fusion.value_ref, s32[1,8192]{1,0:T(1,128)} %bitcast.10.box_ref), custom_call_target="tpu_custom_call" | custom-call | tf_op jit(solution)/shard_map/pallas_call | solution.py:204
  58.5 1.2 slice_add_fusion
  59.7 0.3 reshape.1128
  60.0 0.5 convolution_bitcast_fusion.7
  60.6 4.6 %collective-permute-start.1 = (f32[16,2,4,64]{3,0,2,1:T(8,128)S(1)}, f32[16,2,4,64]{3,0,2,1:T(8,128)S(1)}, u32[]{:S(2)}, u32[]{:S(2)}) collective-permute-start(f32[16,2,4,64]{3,0,2,1:T(8,128)S(1)} %get-tuple-element.23), channel_id=1, source_target_pairs={{32,0},{64,32},{96,64},{128,96},{160,128},{192,160},{224,192},{256... | collective-permute-start | bytes 98312 | tf_op jit(solution)/shard_map/ppermute | solution.py:35
  65.2 3.8 %collective-permute-start = (f32[16,2,4,64]{3,0,2,1:T(8,128)S(1)}, f32[16,2,4,64]{3,0,2,1:T(8,128)S(1)}, u32[]{:S(2)}, u32[]{:S(2)}) collective-permute-start(f32[16,2,4,64]{3,0,2,1:T(8,128)S(1)} %get-tuple-element.22), channel_id=1, source_target_pairs={{0,32},{32,64},{64,96},{96,128},{128,160},{160,192},{192,224},{224... | collective-permute-start | bytes 98312 | tf_op jit(solution)/shard_map/ppermute | solution.py:33
  69.1 1.3 collective-permute-done
  70.4 1.3 collective-permute-start.3
  71.7 4.2 %collective-permute-start.2 = (f32[16,8,2,64]{3,0,2,1:T(8,128)S(1)}, f32[16,8,2,64]{3,0,2,1:T(8,128)S(1)}, u32[]{:S(2)}, u32[]{:S(2)}) collective-permute-start(f32[16,8,2,64]{3,0,2,1:T(8,128)S(1)} %get-tuple-element.18), channel_id=1, source_target_pairs={{0,1},{1,2},{2,3},{3,4},{4,5},{5,6},{6,7},{7,8},{8,9},{9,10},{10,1... | collective-permute-start | bytes 196616 | tf_op jit(solution)/shard_map/ppermute | solution.py:33
  76.1 1.8 collective-permute-done.2
  77.9 1.2 convolution_bitcast_fusion
  79.1 1.3 convolution_bitcast_fusion.5
  80.4 1.3 convolution_bitcast_fusion.4
  81.7 1.3 convolution_bitcast_fusion.3
  83.0 1.3 convolution_bitcast_fusion.2
  84.3 1.3 convolution_bitcast_fusion.1
  85.6 1.0 fusion.14
  86.7 1.0 fusion.41
  87.7 1.0 fusion.38
  88.7 1.0 fusion.35
  89.8 1.2 fusion.32
  91.2 0.4 reduce-precision_convert_fusion.3
  91.6 0.8 pad_maximum_fusion.1.table_ref
  92.4 7.8 %shard_map.166 = f32[1,8192]{1,0:T(1,128)} custom-call(bf16[192,1024]{1,0:T(8,128)(2,1)} %pad_maximum_fusion.1.table_ref, s32[1,8192]{1,0:T(1,128)} %bitcast.10.box_ref, f32[64,8192]{1,0:T(8,128)} %copy-done.1), custom_call_target="tpu_custom_call" | custom-call | tf_op jit(solution)/shard_map/pallas_call | solution.py:229
  100.2 21.5 %all_to_all.47 = f32[32,1,256]{2,1,0:T(1,128)S(1)} all-to-all(f32[32,1,256]{2,1,0:T(1,128)} %bitcast.200), channel_id=1, replica_groups=mesh['grp_0'=8,'grp_1'=2,'dev_0'=8,'dev_1'=4] {'dev_0','dev_1'}, dimensions={0} | all-to-all | bytes 65536 | tf_op jit(solution)/shard_map/all_to_all | solution.py:363
  121.8 0.7 pad_maximum_fusion.7.value_ref
  122.5 4.9 %shard_map.167 = f32[192,64]{1,0:T(8,128)} custom-call(f32[3,8192]{1,0:T(4,128)} %pad_maximum_fusion.7.value_ref, s32[1,8192]{1,0:T(1,128)} %bitcast.196, s32[1,8192]{1,0:T(1,128)} %bitcast.198), custom_call_target="tpu_custom_call" | custom-call | tf_op jit(solution)/shard_map/pallas_call | solution.py:174
  127.4 0.8 slice_add_fusion.2
  128.4 2.4 %multiply_reduce_fusion = (f32[128]{0:T(128)S(1)}, bf16[4096,128]{1,0:T(8,128)(2,1)S(1)}) fusion(f32[4096]{0:T(1024)S(1)} %reshape.1131, f32[4096,128]{1,0:T(8,128)} %get-tuple-element.51, f32[128]{0:T(128)S(1)} %copy-done.19), kind=kLoop, calls=%fused_computation.9 | loop fusion | flops 6815616 | bytes 3163136 | tf_op jit(solution)/shard_map/reduce_sum | solution.py:365
  130.8 0.5 fusion.44
  131.3 2.6 %fusion.46 = f32[128,128]{0,1:T(8,128)S(1)} fusion(bf16[4096,128]{1,0:T(8,128)(2,1)S(1)} %copy-done, bf16[4096,128]{1,0:T(8,128)(2,1)S(1)} %get-tuple-element.9, bf16[128,128]{1,0:T(8,128)(2,1)S(1)} %copy-done.22, f32[4096,128]{1,0:T(8,128)} %get-tuple-element.49), kind=kOutput, calls=%fused_computation.53 | convolution fusion | flops 273170432 | bytes 4292608 | tf_op jit(solution)/shard_map/dot_general | solution.py:379
  134.4 0.3 reshape_reshape.6
  134.9 16.4 %all_to_all.48 = f32[64,8,65]{2,1,0:T(8,128)S(1)} all-to-all(f32[64,8,65]{2,1,0:T(8,128)S(1)} %copy.42), channel_id=1, replica_groups=mesh['grp_0'=8,'grp_1'=2,'dev_0'=8,'dev_1'=4] {'grp_1','dev_0','dev_1'}, dimensions={0} | all-to-all | bytes 266240 | tf_op jit(solution)/shard_map/all_to_all | solution.py:49
  151.3 19.5 %all_to_all.49 = f32[8,1,65]{2,1,0:T(1,128)S(1)} all-to-all(f32[8,1,65]{2,1,0:T(1,128)S(1)} %bitcast.207), channel_id=1, replica_groups=mesh['grp_0'=8,'grp_1'=2,'dev_0'=8,'dev_1'=4] {'grp_0'}, dimensions={0} | all-to-all | bytes 4160 | tf_op jit(solution)/shard_map/all_to_all | solution.py:57
  170.9 8.9 %all_to_all.50 = f32[8,1,65]{2,1,0:T(1,128)S(1)} all-to-all(f32[8,1,65]{2,1,0:T(1,128)S(1)} %broadcast_in_dim.18), channel_id=1, replica_groups=mesh['grp_0'=8,'grp_1'=2,'dev_0'=8,'dev_1'=4] {'grp_0'}, dimensions={0} | all-to-all | bytes 4160 | tf_op jit(solution)/shard_map/all_to_all | solution.py:70
  179.8 20.3 %all_to_all.51 = f32[64,8,65]{2,1,0:T(8,128)S(1)} all-to-all(f32[64,8,65]{2,1,0:T(8,128)S(1)} %broadcast_in_dim.19), channel_id=1, replica_groups=mesh['grp_0'=8,'grp_1'=2,'dev_0'=8,'dev_1'=4] {'grp_1','dev_0','dev_1'}, dimensions={0} | all-to-all | bytes 266240 | tf_op jit(solution)/shard_map/all_to_all | solution.py:70
  200.1 0.2 slice.124
  200.3 0.2 reshape_reshape.7
  200.5 0.5 slice.162
  201.1 0.5 slice.163
  201.6 0.7 fusion.91
  (100 shorter events, 2.7 us)
Async XLA Ops:
  0.6 1.2 copy-start
  0.6 3.9 %copy-start.23 = (s32[4096]{0:T(1024)S(1)}, s32[4096]{0:T(1024)}, u32[]{:S(2)}) copy-start(s32[4096]{0:T(1024)} %param.15) | copy-start | bytes 49156
  0.7 3.9 %copy-start.25 = (f32[6]{0:T(128)S(1)}, f32[6]{0:T(128)}, u32[]{:S(2)}) copy-start(f32[6]{0:T(128)} %param.19) | copy-start | bytes 76
  0.7 4.1 %copy-start.18 = (f32[128]{0:T(128)S(1)}, f32[128]{0:T(128)}, u32[]{:S(2)}) copy-start(f32[128]{0:T(128)} %param.18) | copy-start | bytes 1540
  0.7 4.1 %copy-start.21 = (bf16[128,128]{1,0:T(8,128)(2,1)S(1)}, bf16[128,128]{1,0:T(8,128)(2,1)}, u32[]{:S(2)}) copy-start(bf16[128,128]{1,0:T(8,128)(2,1)} %param.17) | copy-start | bytes 98308
  4.6 2.2 %copy-start.2 = (bf16[4096,128]{1,0:T(8,128)(2,1)}, bf16[4096,128]{1,0:T(8,128)(2,1)S(1)}, u32[]{:S(2)}) copy-start(bf16[4096,128]{1,0:T(8,128)(2,1)S(1)} %get-tuple-element.48) | copy-start | bytes 3145732
  4.8 2.0 copy-start.9
  4.8 2.2 %copy-start.14 = (s32[32,256]{1,0:T(8,128)S(1)}, s32[32,256]{1,0:T(8,128)}, u32[]{:S(2)}) copy-start(s32[32,256]{1,0:T(8,128)} %param.23) | copy-start | bytes 98308
  6.8 19.4 %copy-start.7 = (f32[98,16,16]{0,2,1:T(8,128)S(1)}, f32[98,16,16]{0,2,1:T(8,128)}, u32[]{:S(2)}) copy-start(f32[98,16,16]{0,2,1:T(8,128)} %param.20) | copy-start | bytes 301060
  6.8 19.9 %copy-start.20 = (s32[125]{0:T(128)S(1)}, s32[125]{0:T(128)}, u32[]{:S(2)}) copy-start(s32[125]{0:T(128)} %constant.100) | copy-start | bytes 1504
  6.8 19.9 %copy-start.15 = (s32[32,256]{1,0:T(8,128)S(1)}, s32[32,256]{1,0:T(8,128)}, u32[]{:S(2)}) copy-start(s32[32,256]{1,0:T(8,128)} %param.24) | copy-start | bytes 98308
  15.6 19.9 %all-to-all-start = ((f32[4,32,256]{2,0,1:T(4,128)}), f32[4,32,256]{2,0,1:T(4,128)S(1)}, u32[]{:S(2)}, u32[]{:S(2)}) async-start(f32[4,32,256]{2,0,1:T(4,128)} %bitcast.194), calls=%async_computation | async-start | bytes 262144 | tf_op jit(solution)/shard_map/all_to_all | solution.py:347
  28.2 13.8 %copy-start.12 = (pred[5,64,64]{2,1,0:T(8,128)(4,1)}, pred[5,64,64]{2,1,0:T(8,128)(4,1)S(1)}, u32[]{:S(2)}) copy-start(pred[5,64,64]{2,1,0:T(8,128)(4,1)S(1)} %fusion.78) | copy-start | bytes 61444
  28.5 13.6 %copy-start.10 = (pred[5,8,4]{1,2,0:T(4,128)(4,1)}, pred[5,8,4]{1,2,0:T(4,128)(4,1)S(1)}, u32[]{:S(2)}) copy-start(pred[5,8,4]{1,2,0:T(4,128)(4,1)S(1)} %constant_dynamic-update-slice_fusion.1) | copy-start | bytes 484
  35.5 13.7 %all-to-all-start.1 = ((s32[1,32,256]{2,0,1:T(1,128)}), s32[1,32,256]{2,0,1:T(1,128)}, u32[]{:S(2)}, u32[]{:S(2)}) async-start(s32[1,32,256]{2,0,1:T(1,128)} %broadcast_in_dim.15), calls=%async_computation.1 | async-start | bytes 65536 | tf_op jit(solution)/shard_map/all_to_all | solution.py:348
  46.0 1.4 copy-start.1
  49.2 10.8 %copy-start.17 = (f32[64,16]{0,1:T(8,128)S(1)}, f32[64,16]{0,1:T(8,128)}, u32[]{:S(2)}) copy-start(f32[64,16]{0,1:T(8,128)} %param.22) | copy-start | bytes 12292
  58.5 17.4 %copy-start.11 = (pred[5,8,4]{1,2,0:T(4,128)(4,1)S(1)}, pred[5,8,4]{1,2,0:T(4,128)(4,1)}, u32[]{:S(2)}) copy-start(pred[5,8,4]{1,2,0:T(4,128)(4,1)} %copy-done.10) | copy-start | bytes 484
  58.5 19.4 %copy-start.13 = (pred[5,64,64]{2,1,0:T(8,128)(4,1)S(1)}, pred[5,64,64]{2,1,0:T(8,128)(4,1)}, u32[]{:S(2)}) copy-start(pred[5,64,64]{2,1,0:T(8,128)(4,1)} %copy-done.12) | copy-start | bytes 61444
  60.6 8.5 %collective-permute-start.1 = (f32[16,2,4,64]{3,0,2,1:T(8,128)S(1)}, f32[16,2,4,64]{3,0,2,1:T(8,128)S(1)}, u32[]{:S(2)}, u32[]{:S(2)}) collective-permute-start(f32[16,2,4,64]{3,0,2,1:T(8,128)S(1)} %get-tuple-element.23), channel_id=1, source_target_pairs={{32,0},{64,32},{96,64},{128,96},{160,128},{192,160},{224,192},{256... | collective-permute-start | bytes 98312 | tf_op jit(solution)/shard_map/ppermute | solution.py:35
  65.2 5.2 %collective-permute-start = (f32[16,2,4,64]{3,0,2,1:T(8,128)S(1)}, f32[16,2,4,64]{3,0,2,1:T(8,128)S(1)}, u32[]{:S(2)}, u32[]{:S(2)}) collective-permute-start(f32[16,2,4,64]{3,0,2,1:T(8,128)S(1)} %get-tuple-element.22), channel_id=1, source_target_pairs={{0,32},{32,64},{64,96},{96,128},{128,160},{160,192},{192,224},{224... | collective-permute-start | bytes 98312 | tf_op jit(solution)/shard_map/ppermute | solution.py:33
  69.0 10.0 %copy-start.6 = (f32[25,16,16]{2,1,0:T(8,128)S(1)}, f32[25,16,16]{2,1,0:T(8,128)}, u32[]{:S(2)}) copy-start(f32[25,16,16]{2,1,0:T(8,128)} %get-tuple-element.14) | copy-start | bytes 76804
  70.4 5.7 %collective-permute-start.3 = (f32[16,8,2,64]{3,0,2,1:T(8,128)S(1)}, f32[16,8,2,64]{3,0,2,1:T(8,128)S(1)}, u32[]{:S(2)}, u32[]{:S(2)}) collective-permute-start(f32[16,8,2,64]{3,0,2,1:T(8,128)S(1)} %get-tuple-element.19), channel_id=1, source_target_pairs={{1,0},{2,1},{3,2},{4,3},{5,4},{6,5},{7,6},{8,7},{9,8},{10,9},{11,1... | collective-permute-start | bytes 196616 | tf_op jit(solution)/shard_map/ppermute | solution.py:35
  71.7 6.2 %collective-permute-start.2 = (f32[16,8,2,64]{3,0,2,1:T(8,128)S(1)}, f32[16,8,2,64]{3,0,2,1:T(8,128)S(1)}, u32[]{:S(2)}, u32[]{:S(2)}) collective-permute-start(f32[16,8,2,64]{3,0,2,1:T(8,128)S(1)} %get-tuple-element.18), channel_id=1, source_target_pairs={{0,1},{1,2},{2,3},{3,4},{4,5},{5,6},{6,7},{7,8},{8,9},{9,10},{10,1... | collective-permute-start | bytes 196616 | tf_op jit(solution)/shard_map/ppermute | solution.py:33
  79.0 1.3 copy-start.5
  80.4 1.3 copy-start.4
  87.7 3.5 %copy-start.16 = (f32[64,16]{0,1:T(8,128)S(1)}, f32[64,16]{0,1:T(8,128)}, u32[]{:S(2)}) copy-start(f32[64,16]{0,1:T(8,128)} %param.21) | copy-start | bytes 12292
  91.6 36.8 %copy-start.19 = (f32[128]{0:T(128)S(1)}, f32[128]{0:T(128)}, u32[]{:S(2)}) copy-start(f32[128]{0:T(128)} %param.18) | copy-start | bytes 1540
  100.2 30.6 %copy-start.3 = (bf16[4096,128]{1,0:T(8,128)(2,1)S(1)}, bf16[4096,128]{1,0:T(8,128)(2,1)}, u32[]{:S(2)}) copy-start(bf16[4096,128]{1,0:T(8,128)(2,1)} %copy-done.2) | copy-start | bytes 3145732
  128.3 3.0 %copy-start.8 = (f32[4096]{0:T(1024)}, f32[4096]{0:T(1024)S(1)}, u32[]{:S(2)}) copy-start(f32[4096]{0:T(1024)S(1)} %reshape.1131) | copy-start | bytes 49156
  128.4 2.9 %copy-start.22 = (bf16[128,128]{1,0:T(8,128)(2,1)S(1)}, bf16[128,128]{1,0:T(8,128)(2,1)}, u32[]{:S(2)}) copy-start(bf16[128,128]{1,0:T(8,128)(2,1)} %param.17) | copy-start | bytes 98308
  131.3 2.8 %copy-start.24 = (s32[4096]{0:T(1024)S(1)}, s32[4096]{0:T(1024)}, u32[]{:S(2)}) copy-start(s32[4096]{0:T(1024)} %param.15) | copy-start | bytes 49156

commit v3 on v2

--- a/solution.py
+++ b/solution.py
@@ -96,11 +96,36 @@
     return tuple((total[b:e].reshape(a.shape) for a, b, e in zip(arrays, ends, ends[1:])))
 
 
-def summed_everywhere(arrays, axes):
+def swapped(x, axis, step):
+    count = lax.axis_size(axis)
+    return lax.ppermute(x, axis, [(i, i ^ step) for i in range(count)])
+
+
+def butterfly_sum(x, axis):
+    step = 1
+    while step < lax.axis_size(axis):
+        x = x + swapped(x, axis, step)
+        step *= 2
+    return x
+
+
+def hybrid_sum(x, pair, plane, stack):
+    length = x.shape[0]
+    x = butterfly_sum(x, pair)
+    peers = lax.axis_size(plane)
+    lines = padded_to(x, peers).reshape(peers, -1)
+    own = lax.all_to_all(lines, plane, 0, 0, tiled=True).reshape(peers, -1).sum(axis=0)
+    own = butterfly_sum(own, stack)
+    copies = jnp.broadcast_to(own, (peers, *own.shape))
+    return lax.all_to_all(copies, plane, 0, 0, tiled=True).reshape(-1)[:length]
+
+
+def summed_everywhere(arrays):
     ends = [0]
     for a in arrays:
         ends.append(ends[-1] + a.size)
-    total = lax.psum(jnp.concatenate([a.ravel() for a in arrays]), axes)
+    flat = jnp.concatenate([a.ravel() for a in arrays])
+    total = hybrid_sum(flat, "grp_1", DEV, "grp_0")
     return tuple((total[b:e].reshape(a.shape) for a, b, e in zip(arrays, ends, ends[1:])))
 
 
@@ -343,13 +368,11 @@
     atom_low = (send_list % side).reshape(1, -1)
     packed = jnp.concatenate([charge[None, :], positions], axis=0)
     picked = atoms_to_slots(packed, atom_high, atom_low).reshape(4, *send_list.shape)
-    arrived, box_ids = (
-        lax.all_to_all(picked, DEV, split_axis=1, concat_axis=1, tiled=True),
-        lax.all_to_all(slot_box[None], DEV, split_axis=1, concat_axis=1, tiled=True),
-    )
+    outgoing = jnp.concatenate([picked, slot_box[None].astype(jnp.float32)], axis=0)
+    arrived = lax.all_to_all(outgoing, DEV, split_axis=1, concat_axis=1, tiled=True)
     arrived_charge = arrived[0].reshape(-1)
-    arrived_coords = arrived[1:].reshape(3, -1)
-    slot_boxes = box_ids.reshape(-1)
+    arrived_coords = arrived[1:4].reshape(3, -1)
+    slot_boxes = arrived[4].reshape(-1).astype(jnp.int32)
     weight_table = node_weights(arrived_coords)
     moments = box_sum(weight_table * arrived_charge[None, :], slot_boxes[None, :], BOXES)
     node_grid = moments.reshape(NODES, BZ, BX, BY)
@@ -381,8 +404,8 @@
         )
         * grad_scale
     )
-    grad_in, grad_mid, grad_head, grad_species = together(
-        (in_part, mid_part, head_part, species_part), ("grp_0", ("grp_1", "dev_0", "dev_1"))
+    grad_in, grad_mid, grad_head, grad_species = summed_everywhere(
+        (in_part, mid_part, head_part, species_part)
     )
     return (potential, grad_in, grad_mid, grad_head, grad_species)
 

time: 204 us -> 193 us (0.946)
  the two profiles are of different devices: /device:TPU:1 before, /device:TPU:8 now
where the time goes in v3:
time: 193 us; the launch traced here: 191 us
  starting transfers between devices  45.4 us (24%)
  blocking collectives  43.9 us (23%)
  Pallas kernels  28.4 us (15%)
  waiting for transfers between devices  22.7 us (12%)
  matrix products  22.2 us (12%)
  other arithmetic  17.3 us (9%)
  local copies, waits for them, and re-layouts  9.48 us (5%)
    ppermute x4, starting transfers between devices, swapped(): return lax.ppermute(x, axis, [(i, i ^ step) for i in range(count)])  24.9 us
    all_to_all x1, blocking collectives, shards(): lax.all_to_all(slot_potential, DEV, split_axis=0, concat_axis=0, tiled=True)  15.5 us
    all_to_all x1, blocking collectives, hybrid_sum(): lax.all_to_all(lines, plane, 0, 0, tiled=True).reshape(peers, -1)  14.5 us
    all_to_all x1, blocking collectives, hybrid_sum(): return lax.all_to_all(copies, plane, 0, 0, tiled=True).reshape(-1)[:length]  13.9 us
    all_to_all x1, starting transfers between devices, shards(): lax.all_to_all(outgoing, DEV, split_axis=1, concat_axis=1, tiled=True)  10.2 us
    pallas_call x1, Pallas kernels, box_sum(): pl.pallas_call(box_sum_kernel, grid=(slots // tile,), in_specs=[pl.BlockS...  9.28 us
    all_to_all x1, waiting for transfers between devices, shards(): lax.all_to_all(outgoing, DEV, split_axis=1, concat_axis=1, tiled=True)  9.02 us
    pallas_call x1, Pallas kernels, box_pick(): pl.pallas_call(box_pick_kernel, grid=(slots // tile,), in_specs=[pl.Block...  7.76 us
  transfers between devices with their start and end apart: 9, of which 8 were waited for; matrix products, arithmetic and copies ran while one was open for 1% of the time, Pallas kernels for 0%

profile of v3, /device:TPU:8, one launch (start us, length us, event | category | flops | bytes accessed | tf_op | source)
XLA Modules:
  0.0 190.9 jit_solution(16431292881529914342)
XLA Ops:
  0.6 0.8 convert_element_type.140
  1.5 0.4 copy-done
  1.9 2.7 %multiply_convert_fusion.1 = (bf16[4096,128]{1,0:T(8,128)(2,1)S(1)}, f32[4096,128]{1,0:T(8,128)}) fusion(bf16[4096,128]{1,0:T(8,128)(2,1)S(1)} %copy-done, bf16[128,128]{1,0:T(8,128)(2,1)} %param.16), kind=kOutput, calls=%fused_computation.14 | convolution fusion | flops 136839168 | bytes 4227072 | tf_op jit(solution)/shard_map/dot_general | solution.py:355
  4.9 2.0 %multiply_reduce_fusion.1 = (f32[4096]{0:T(1024)S(1)}, f32[4096,128]{1,0:T(8,128)}) fusion(f32[128]{0:T(128)S(1)} %copy-done.17, bf16[4096,128]{1,0:T(8,128)(2,1)S(1)} %get-tuple-element.49, bf16[128,128]{1,0:T(8,128)(2,1)S(1)} %copy-done.20), kind=kOutput, calls=%fused_computation.11 | convolution fusion | flops 137359360 | bytes 3195392 | tf_op jit(solution)/shard_map/dot_general | solution.py:357
  7.1 0.6 copy.78
  7.8 0.6 copy.79
  8.4 0.7 pad_maximum_fusion.4.table_ref
  9.1 6.5 %shard_map.164 = f32[4,8192]{1,0:T(4,128)} custom-call(bf16[768,64]{1,0:T(8,128)(2,1)} %pad_maximum_fusion.4.table_ref, s32[1,8192]{1,0:T(1,128)} %bitcast.197, s32[1,8192]{1,0:T(1,128)} %bitcast.199), custom_call_target="tpu_custom_call" | custom-call | tf_op jit(solution)/shard_map/pallas_call | solution.py:163
  15.6 1.7 pad_maximum_fusion.2
  17.3 10.2 %all-to-all-start = ((f32[5,32,256]{2,0,1:T(8,128)}), f32[5,32,256]{2,0,1:T(8,128)S(1)}, u32[]{:S(2)}, u32[]{:S(2)}) async-start(f32[5,32,256]{2,0,1:T(8,128)} %pad_maximum_fusion.2), calls=%async_computation | async-start | bytes 524288 | tf_op jit(solution)/shard_map/all_to_all | solution.py:372
  27.6 0.4 copy.44
  28.4 0.4 copy-done.12
  29.0 0.7 gather_fusion
  29.7 0.9 fusion.90
  30.6 9.0 %all-to-all-done = f32[5,32,256]{2,0,1:T(8,128)S(1)} async-done(((f32[5,32,256]{2,0,1:T(8,128)}), f32[5,32,256]{2,0,1:T(8,128)S(1)}, u32[]{:S(2)}, u32[]{:S(2)}) %all-to-all-start) | async-done | bytes 163872 | tf_op jit(solution)/shard_map/all_to_all | solution.py:372
  39.6 0.7 slice_convert_fusion
  41.8 1.9 broadcast_multiply_fusion
  43.7 2.0 %mul.1029.weight_ref = f32[64,8192]{1,0:T(8,128)S(1)} reshape(f32[4,4,4,8192]{3,2,1,0:T(4,128)} %broadcast_multiply_fusion) | data formatting | bytes 4194304 | tf_op jit(solution)/shard_map/mul | solution.py:296
  45.7 1.3 reduce-precision_convert_fusion.1
  47.1 1.7 pad_maximum_fusion.value_ref
  48.8 9.3 %shard_map.165 = f32[192,1024]{1,0:T(8,128)} custom-call(bf16[192,8192]{1,0:T(8,128)(2,1)} %pad_maximum_fusion.value_ref, s32[1,8192]{1,0:T(1,128)} %bitcast.195), custom_call_target="tpu_custom_call" | custom-call | tf_op jit(solution)/shard_map/pallas_call | solution.py:229
  58.1 1.2 slice_add_fusion
  59.6 0.5 convolution_bitcast_fusion.7
  60.2 1.3 collective-permute-start.1
  61.5 3.0 %collective-permute-start = (f32[16,2,4,64]{3,0,2,1:T(8,128)S(1)}, f32[16,2,4,64]{3,0,2,1:T(8,128)S(1)}, u32[]{:S(2)}, u32[]{:S(2)}) collective-permute-start(f32[16,2,4,64]{3,0,2,1:T(8,128)S(1)} %get-tuple-element.27), channel_id=1, source_target_pairs={{0,32},{32,64},{64,96},{96,128},{128,160},{160,192},{192,224},{224... | collective-permute-start | bytes 98312 | tf_op jit(solution)/shard_map/ppermute | solution.py:33
  64.5 0.8 collective-permute-done
  65.4 3.7 %collective-permute-start.3 = (f32[16,8,2,64]{3,0,2,1:T(8,128)S(1)}, f32[16,8,2,64]{3,0,2,1:T(8,128)S(1)}, u32[]{:S(2)}, u32[]{:S(2)}) collective-permute-start(f32[16,8,2,64]{3,0,2,1:T(8,128)S(1)} %get-tuple-element.19), channel_id=1, source_target_pairs={{1,0},{2,1},{3,2},{4,3},{5,4},{6,5},{7,6},{8,7},{9,8},{10,9},{11,1... | collective-permute-start | bytes 196616 | tf_op jit(solution)/shard_map/ppermute | solution.py:35
  69.1 2.4 %collective-permute-start.2 = (f32[16,8,2,64]{3,0,2,1:T(8,128)S(1)}, f32[16,8,2,64]{3,0,2,1:T(8,128)S(1)}, u32[]{:S(2)}, u32[]{:S(2)}) collective-permute-start(f32[16,8,2,64]{3,0,2,1:T(8,128)S(1)} %get-tuple-element.18), channel_id=1, source_target_pairs={{0,1},{1,2},{2,3},{3,4},{4,5},{5,6},{6,7},{7,8},{8,9},{9,10},{10,1... | collective-permute-start | bytes 196616 | tf_op jit(solution)/shard_map/ppermute | solution.py:33
  71.6 0.7 collective-permute-done.3
  72.3 6.0 %collective-permute-done.2 = f32[16,8,2,64]{3,0,2,1:T(8,128)S(1)} collective-permute-done((f32[16,8,2,64]{3,0,2,1:T(8,128)S(1)}, f32[16,8,2,64]{3,0,2,1:T(8,128)S(1)}, u32[]{:S(2)}, u32[]{:S(2)}) %collective-permute-start.2) | collective-permute-done | bytes 65568 | tf_op jit(solution)/shard_map/ppermute | solution.py:33
  78.3 1.2 convolution_bitcast_fusion
  79.5 1.3 convolution_bitcast_fusion.5
  80.8 1.3 convolution_bitcast_fusion.4
  82.1 1.3 convolution_bitcast_fusion.3
  83.5 1.3 convolution_bitcast_fusion.2
  84.8 1.3 convolution_bitcast_fusion.1
  86.1 1.0 fusion.14
  87.1 1.0 fusion.41
  88.1 1.0 fusion.38
  89.2 1.0 fusion.35
  90.2 1.2 fusion.32
  91.6 0.4 reduce-precision_convert_fusion.3
  92.1 0.8 pad_maximum_fusion.1.table_ref
  92.9 7.8 %shard_map.166 = f32[1,8192]{1,0:T(1,128)} custom-call(bf16[192,1024]{1,0:T(8,128)(2,1)} %pad_maximum_fusion.1.table_ref, s32[1,8192]{1,0:T(1,128)} %bitcast.196, f32[64,8192]{1,0:T(8,128)} %copy-done.1), custom_call_target="tpu_custom_call" | custom-call | tf_op jit(solution)/shard_map/pallas_call | solution.py:254
  100.6 15.5 %all_to_all.29 = f32[32,1,256]{2,1,0:T(1,128)S(1)} all-to-all(f32[32,1,256]{2,1,0:T(1,128)} %bitcast.202), channel_id=1, replica_groups=mesh['grp_0'=8,'grp_1'=2,'dev_0'=8,'dev_1'=4] {'dev_0','dev_1'}, dimensions={0} | all-to-all | bytes 65536 | tf_op jit(solution)/shard_map/all_to_all | solution.py:386
  116.2 0.8 pad_maximum_fusion.9.value_ref
  117.0 4.9 %shard_map.167 = f32[192,64]{1,0:T(8,128)} custom-call(f32[3,8192]{1,0:T(4,128)} %pad_maximum_fusion.9.value_ref, s32[1,8192]{1,0:T(1,128)} %bitcast.198, s32[1,8192]{1,0:T(1,128)} %bitcast.200), custom_call_target="tpu_custom_call" | custom-call | tf_op jit(solution)/shard_map/pallas_call | solution.py:199
  121.9 0.8 slice_add_fusion.2
  123.1 2.4 %multiply_convert_fusion = (bf16[4096,128]{1,0:T(8,128)(2,1)S(1)}, f32[128]{0:T(128)S(1)}) fusion(f32[4096,128]{1,0:T(8,128)} %get-tuple-element.52, f32[4096]{0:T(1024)S(1)} %reshape.1149, f32[128]{0:T(128)S(1)} %copy-done.18), kind=kLoop, calls=%fused_computation.10 | loop fusion | flops 6815616 | bytes 3163136 | tf_op jit(solution)/shard_map/convert_element_type | solution.py:390
  125.5 0.5 fusion.44
  126.0 2.6 %fusion.46 = f32[128,128]{0,1:T(8,128)S(1)} fusion(bf16[4096,128]{1,0:T(8,128)(2,1)S(1)} %copy-done, bf16[4096,128]{1,0:T(8,128)(2,1)S(1)} %get-tuple-element.8, bf16[128,128]{1,0:T(8,128)(2,1)S(1)} %copy-done.21, f32[4096,128]{1,0:T(8,128)} %get-tuple-element.50), kind=kOutput, calls=%fused_computation.53 | convolution fusion | flops 273170432 | bytes 4292608 | tf_op jit(solution)/shard_map/dot_general | solution.py:402
  128.8 1.9 %collective-permute-start.4 = (f32[32902]{0:T(1024)S(1)}, f32[32902]{0:T(1024)S(1)}, u32[]{:S(2)}, u32[]{:S(2)}) collective-permute-start(f32[32902]{0:T(1024)S(1)} %pad_maximum_fusion.5), channel_id=1, source_target_pairs={{0,32},{32,0},{1,33},{33,1},{2,34},{34,2},{3,35},{35,3},{4,36},{36... | collective-permute-start | bytes 394832 | tf_op jit(solution)/shard_map/ppermute | solution.py:101
  130.7 1.3 collective-permute-done.4
  132.3 14.5 %all_to_all.30 = f32[32,1,1029]{2,1,0:T(1,128)S(1)} all-to-all(f32[32,1,1029]{2,1,0:T(1,128)S(1)} %all_to_all.22), channel_id=1, replica_groups=mesh['grp_0'=8,'grp_1'=2,'dev_0'=8,'dev_1'=4] {'dev_0','dev_1'}, dimensions={0} | all-to-all | bytes 263424 | tf_op jit(solution)/shard_map/all_to_all | solution.py:117
  146.9 6.7 %collective-permute-start.5 = (f32[1029]{0:T(1024)S(1)}, f32[1029]{0:T(1024)S(1)}, u32[]{:S(2)}, u32[]{:S(2)}) collective-permute-start(f32[1029]{0:T(1024)S(1)} %reduce_sum.29), channel_id=1, source_target_pairs={{0,64},{64,0},{128,192},{192,128},{256,320},{320,256},{384,448},{4... | collective-permute-start | bytes 12356 | tf_op jit(solution)/shard_map/ppermute | solution.py:101
  153.6 1.6 collective-permute-done.5
  155.2 7.1 %collective-permute-start.6 = (f32[1029]{0:T(1024)S(1)}, f32[1029]{0:T(1024)S(1)}, u32[]{:S(2)}, u32[]{:S(2)}) collective-permute-start(f32[1029]{0:T(1024)S(1)} %add.663), channel_id=1, source_target_pairs={{0,128},{64,192},{128,0},{192,64},{256,384},{320,448},{384,256},{4... | collective-permute-start | bytes 12356 | tf_op jit(solution)/shard_map/ppermute | solution.py:101
  162.3 1.6 collective-permute-done.6
  163.9 9.3 %collective-permute-start.7 = (f32[1029]{0:T(1024)S(1)}, f32[1029]{0:T(1024)S(1)}, u32[]{:S(2)}, u32[]{:S(2)}) collective-permute-start(f32[1029]{0:T(1024)S(1)} %add.664), channel_id=1, source_target_pairs={{0,256},{64,320},{128,384},{192,448},{256,0},{320,64},{384,128},{4... | collective-permute-start | bytes 12356 | tf_op jit(solution)/shard_map/ppermute | solution.py:101
  173.2 1.6 collective-permute-done.7
  174.9 13.9 %all_to_all.31 = f32[32,1,1029]{2,1,0:T(1,128)S(1)} all-to-all(f32[32,1,1029]{2,1,0:T(1,128)S(1)} %broadcast_in_dim.10), channel_id=1, replica_groups=mesh['grp_0'=8,'grp_1'=2,'dev_0'=8,'dev_1'=4] {'dev_0','dev_1'}, dimensions={0} | all-to-all | bytes 263424 | tf_op jit(solution)/shard_map/all_to_all | solution.py:120
  189.2 0.7 slice_bitcast_fusion.10
  189.9 0.5 slice.162
  190.4 0.5 slice.163
  (104 shorter events, 4.7 us)
Async XLA Ops:
  0.6 1.2 copy-start
  1.9 2.8 %copy-start.22 = (s32[4096]{0:T(1024)S(1)}, s32[4096]{0:T(1024)}, u32[]{:S(2)}) copy-start(s32[4096]{0:T(1024)} %param.15) | copy-start | bytes 49156
  1.9 2.8 %copy-start.24 = (f32[6]{0:T(128)S(1)}, f32[6]{0:T(128)}, u32[]{:S(2)}) copy-start(f32[6]{0:T(128)} %param.19) | copy-start | bytes 76
  1.9 3.0 %copy-start.17 = (f32[128]{0:T(128)S(1)}, f32[128]{0:T(128)}, u32[]{:S(2)}) copy-start(f32[128]{0:T(128)} %param.18) | copy-start | bytes 1540
  1.9 3.0 %copy-start.20 = (bf16[128,128]{1,0:T(8,128)(2,1)S(1)}, bf16[128,128]{1,0:T(8,128)(2,1)}, u32[]{:S(2)}) copy-start(bf16[128,128]{1,0:T(8,128)(2,1)} %param.17) | copy-start | bytes 98308
  4.6 2.2 %copy-start.2 = (bf16[4096,128]{1,0:T(8,128)(2,1)}, bf16[4096,128]{1,0:T(8,128)(2,1)S(1)}, u32[]{:S(2)}) copy-start(bf16[4096,128]{1,0:T(8,128)(2,1)S(1)} %get-tuple-element.49) | copy-start | bytes 3145732
  4.9 2.0 %copy-start.9 = (f32[3,4096]{1,0:T(4,128)S(1)}, f32[3,4096]{1,0:T(4,128)}, u32[]{:S(2)}) copy-start(f32[3,4096]{1,0:T(4,128)} %param.14) | copy-start | bytes 147460
  4.9 2.2 %copy-start.14 = (s32[32,256]{1,0:T(8,128)S(1)}, s32[32,256]{1,0:T(8,128)}, u32[]{:S(2)}) copy-start(s32[32,256]{1,0:T(8,128)} %param.23) | copy-start | bytes 98308
  6.9 20.7 %copy-start.7 = (f32[98,16,16]{0,2,1:T(8,128)S(1)}, f32[98,16,16]{0,2,1:T(8,128)}, u32[]{:S(2)}) copy-start(f32[98,16,16]{0,2,1:T(8,128)} %param.20) | copy-start | bytes 301060
  8.4 20.0 %copy-start.19 = (s32[125]{0:T(128)S(1)}, s32[125]{0:T(128)}, u32[]{:S(2)}) copy-start(s32[125]{0:T(128)} %constant.102) | copy-start | bytes 1504
  17.3 22.3 %all-to-all-start = ((f32[5,32,256]{2,0,1:T(8,128)}), f32[5,32,256]{2,0,1:T(8,128)S(1)}, u32[]{:S(2)}, u32[]{:S(2)}) async-start(f32[5,32,256]{2,0,1:T(8,128)} %pad_maximum_fusion.2), calls=%async_computation | async-start | bytes 524288 | tf_op jit(solution)/shard_map/all_to_all | solution.py:372
  28.1 0.6 copy-start.12
  28.4 0.6 copy-start.10
  45.7 1.4 copy-start.1
  48.8 10.8 %copy-start.16 = (f32[64,16]{0,1:T(8,128)S(1)}, f32[64,16]{0,1:T(8,128)}, u32[]{:S(2)}) copy-start(f32[64,16]{0,1:T(8,128)} %param.22) | copy-start | bytes 12292
  58.1 13.4 %copy-start.11 = (pred[5,8,4]{1,2,0:T(4,128)(4,1)S(1)}, pred[5,8,4]{1,2,0:T(4,128)(4,1)}, u32[]{:S(2)}) copy-start(pred[5,8,4]{1,2,0:T(4,128)(4,1)} %copy-done.10) | copy-start | bytes 484
  58.1 20.2 %copy-start.13 = (pred[5,64,64]{2,1,0:T(8,128)(4,1)S(1)}, pred[5,64,64]{2,1,0:T(8,128)(4,1)}, u32[]{:S(2)}) copy-start(pred[5,64,64]{2,1,0:T(8,128)(4,1)} %copy-done.12) | copy-start | bytes 61444
  60.2 4.4 %collective-permute-start.1 = (f32[16,2,4,64]{3,0,2,1:T(8,128)S(1)}, f32[16,2,4,64]{3,0,2,1:T(8,128)S(1)}, u32[]{:S(2)}, u32[]{:S(2)}) collective-permute-start(f32[16,2,4,64]{3,0,2,1:T(8,128)S(1)} %get-tuple-element.28), channel_id=1, source_target_pairs={{32,0},{64,32},{96,64},{128,96},{160,128},{192,160},{224,192},{256... | collective-permute-start | bytes 98312 | tf_op jit(solution)/shard_map/ppermute | solution.py:35
  61.5 3.9 %collective-permute-start = (f32[16,2,4,64]{3,0,2,1:T(8,128)S(1)}, f32[16,2,4,64]{3,0,2,1:T(8,128)S(1)}, u32[]{:S(2)}, u32[]{:S(2)}) collective-permute-start(f32[16,2,4,64]{3,0,2,1:T(8,128)S(1)} %get-tuple-element.27), channel_id=1, source_target_pairs={{0,32},{32,64},{64,96},{96,128},{128,160},{160,192},{192,224},{224... | collective-permute-start | bytes 98312 | tf_op jit(solution)/shard_map/ppermute | solution.py:33
  64.5 15.0 %copy-start.6 = (f32[25,16,16]{2,1,0:T(8,128)S(1)}, f32[25,16,16]{2,1,0:T(8,128)}, u32[]{:S(2)}) copy-start(f32[25,16,16]{2,1,0:T(8,128)} %get-tuple-element.14) | copy-start | bytes 76804
  65.4 6.9 %collective-permute-start.3 = (f32[16,8,2,64]{3,0,2,1:T(8,128)S(1)}, f32[16,8,2,64]{3,0,2,1:T(8,128)S(1)}, u32[]{:S(2)}, u32[]{:S(2)}) collective-permute-start(f32[16,8,2,64]{3,0,2,1:T(8,128)S(1)} %get-tuple-element.19), channel_id=1, source_target_pairs={{1,0},{2,1},{3,2},{4,3},{5,4},{6,5},{7,6},{8,7},{9,8},{10,9},{11,1... | collective-permute-start | bytes 196616 | tf_op jit(solution)/shard_map/ppermute | solution.py:35
  69.1 9.2 %collective-permute-start.2 = (f32[16,8,2,64]{3,0,2,1:T(8,128)S(1)}, f32[16,8,2,64]{3,0,2,1:T(8,128)S(1)}, u32[]{:S(2)}, u32[]{:S(2)}) collective-permute-start(f32[16,8,2,64]{3,0,2,1:T(8,128)S(1)} %get-tuple-element.18), channel_id=1, source_target_pairs={{0,1},{1,2},{2,3},{3,4},{4,5},{5,6},{6,7},{7,8},{8,9},{9,10},{10,1... | collective-permute-start | bytes 196616 | tf_op jit(solution)/shard_map/ppermute | solution.py:33
  79.5 1.3 copy-start.5
  80.8 1.3 copy-start.4
  88.1 3.5 %copy-start.15 = (f32[64,16]{0,1:T(8,128)S(1)}, f32[64,16]{0,1:T(8,128)}, u32[]{:S(2)}) copy-start(f32[64,16]{0,1:T(8,128)} %param.21) | copy-start | bytes 12292
  92.1 30.8 %copy-start.23 = (s32[4096]{0:T(1024)S(1)}, s32[4096]{0:T(1024)}, u32[]{:S(2)}) copy-start(s32[4096]{0:T(1024)} %param.15) | copy-start | bytes 49156
  92.1 31.0 %copy-start.18 = (f32[128]{0:T(128)S(1)}, f32[128]{0:T(128)}, u32[]{:S(2)}) copy-start(f32[128]{0:T(128)} %param.18) | copy-start | bytes 1540
  100.6 24.9 %copy-start.3 = (bf16[4096,128]{1,0:T(8,128)(2,1)S(1)}, bf16[4096,128]{1,0:T(8,128)(2,1)}, u32[]{:S(2)}) copy-start(bf16[4096,128]{1,0:T(8,128)(2,1)} %copy-done.2) | copy-start | bytes 3145732
  122.8 3.3 %copy-start.8 = (f32[4096]{0:T(1024)}, f32[4096]{0:T(1024)S(1)}, u32[]{:S(2)}) copy-start(f32[4096]{0:T(1024)S(1)} %reshape.1149) | copy-start | bytes 49156
  123.1 3.0 %copy-start.21 = (bf16[128,128]{1,0:T(8,128)(2,1)S(1)}, bf16[128,128]{1,0:T(8,128)(2,1)}, u32[]{:S(2)}) copy-start(bf16[128,128]{1,0:T(8,128)(2,1)} %param.17) | copy-start | bytes 98308
  128.8 3.2 %collective-permute-start.4 = (f32[32902]{0:T(1024)S(1)}, f32[32902]{0:T(1024)S(1)}, u32[]{:S(2)}, u32[]{:S(2)}) collective-permute-start(f32[32902]{0:T(1024)S(1)} %pad_maximum_fusion.5), channel_id=1, source_target_pairs={{0,32},{32,0},{1,33},{33,1},{2,34},{34,2},{3,35},{35,3},{4,36},{36... | collective-permute-start | bytes 394832 | tf_op jit(solution)/shard_map/ppermute | solution.py:101
  146.9 8.3 %collective-permute-start.5 = (f32[1029]{0:T(1024)S(1)}, f32[1029]{0:T(1024)S(1)}, u32[]{:S(2)}, u32[]{:S(2)}) collective-permute-start(f32[1029]{0:T(1024)S(1)} %reduce_sum.29), channel_id=1, source_target_pairs={{0,64},{64,0},{128,192},{192,128},{256,320},{320,256},{384,448},{4... | collective-permute-start | bytes 12356 | tf_op jit(solution)/shard_map/ppermute | solution.py:101
  155.2 8.7 %collective-permute-start.6 = (f32[1029]{0:T(1024)S(1)}, f32[1029]{0:T(1024)S(1)}, u32[]{:S(2)}, u32[]{:S(2)}) collective-permute-start(f32[1029]{0:T(1024)S(1)} %add.663), channel_id=1, source_target_pairs={{0,128},{64,192},{128,0},{192,64},{256,384},{320,448},{384,256},{4... | collective-permute-start | bytes 12356 | tf_op jit(solution)/shard_map/ppermute | solution.py:101
  163.9 10.9 %collective-permute-start.7 = (f32[1029]{0:T(1024)S(1)}, f32[1029]{0:T(1024)S(1)}, u32[]{:S(2)}, u32[]{:S(2)}) collective-permute-start(f32[1029]{0:T(1024)S(1)} %add.664), channel_id=1, source_target_pairs={{0,256},{64,320},{128,384},{192,448},{256,0},{320,64},{384,128},{4... | collective-permute-start | bytes 12356 | tf_op jit(solution)/shard_map/ppermute | solution.py:101

commit v4 on v3

--- a/solution.py
+++ b/solution.py
@@ -210,58 +210,85 @@
     return (parts[:side] + parts[side : 2 * side] + parts[2 * side :]).reshape(count)
 
 
-def box_sum_kernel(value_ref, box_ref, out_ref):
+def node_rows(data_ref, tile):
+    nodes = lax.broadcasted_iota(jnp.int32, (NODES, tile), 0)
+    spread = []
+    for axis, shift in ((0, 4), (1, 2), (2, 0)):
+        u = data_ref[1 + axis : 2 + axis, :]
+        order_two = 2.0 * u * u - 1.0
+        order_three = 4.0 * u * u * u - 3.0 * u
+        rows = []
+        for node_point in NODE_POINTS:
+            cheb_two = 2.0 * node_point * node_point - 1.0
+            cheb_three = 4.0 * node_point * node_point * node_point - 3.0 * node_point
+            rows.append(0.25 + 0.5 * (node_point * u + cheb_two * order_two + cheb_three * order_three))
+        pick = jnp.bitwise_and(jnp.right_shift(nodes, shift), 3)
+        full = jnp.broadcast_to(rows[3], (NODES, tile))
+        for p in range(3):
+            full = jnp.where(pick == p, rows[p], full)
+        spread.append(full)
+    return spread[0] * spread[1] * spread[2]
+
+
+def bf16_pieces_in_kernel(x):
+    high = x.astype(jnp.bfloat16)
+    rest = x - high.astype(jnp.float32)
+    middle = rest.astype(jnp.bfloat16)
+    low = (rest - middle.astype(jnp.float32)).astype(jnp.bfloat16)
+    return jnp.concatenate([high, middle, low], axis=0)
+
+
+def box_sum_kernel(data_ref, out_ref):
     @pl.when(pl.program_id(0) == 0)
     def _():
         out_ref[...] = jnp.zeros_like(out_ref)
 
     boxes = out_ref.shape[1]
-    tile = box_ref.shape[1]
-    hot = (lax.broadcasted_iota(jnp.int32, (boxes, tile), 0) == box_ref[...]).astype(jnp.bfloat16)
+    tile = data_ref.shape[1]
+    box = data_ref[4:5, :].astype(jnp.int32)
+    weighted = node_rows(data_ref, tile) * data_ref[0:1, :]
+    hot = (lax.broadcasted_iota(jnp.int32, (boxes, tile), 0) == box).astype(jnp.bfloat16)
     out_ref[...] += lax.dot_general(
-        value_ref[...], hot, (((1,), (1,)), ((), ())), preferred_element_type=jnp.float32
-    )
-
-
-def box_sum(values, box, boxes, tile=1024):
-    rows, slots = values.shape
-    stacked = pieces_bf16(values, 0)
+        bf16_pieces_in_kernel(weighted), hot, (((1,), (1,)), ((), ())),
+        preferred_element_type=jnp.float32,
+    )
+
+
+def box_sum(data, boxes, tile=1024):
+    rows, slots = data.shape
     parts = pl.pallas_call(
         box_sum_kernel,
         grid=(slots // tile,),
-        in_specs=[
-            pl.BlockSpec((3 * rows, tile), lambda i: (0, i)),
-            pl.BlockSpec((1, tile), lambda i: (0, i)),
-        ],
-        out_specs=pl.BlockSpec((3 * rows, boxes), lambda i: (0, 0)),
-        out_shape=jax.ShapeDtypeStruct((3 * rows, boxes), jnp.float32),
-    )(stacked, box)
-    return parts[:rows] + parts[rows : 2 * rows] + parts[2 * rows :]
-
-
-def box_pick_kernel(table_ref, box_ref, weight_ref, out_ref):
+        in_specs=[pl.BlockSpec((rows, tile), lambda i: (0, i))],
+        out_specs=pl.BlockSpec((3 * NODES, boxes), lambda i: (0, 0)),
+        out_shape=jax.ShapeDtypeStruct((3 * NODES, boxes), jnp.float32),
+    )(data)
+    return parts[:NODES] + parts[NODES : 2 * NODES] + parts[2 * NODES :]
+
+
+def box_pick_kernel(table_ref, data_ref, out_ref):
     boxes = table_ref.shape[1]
-    rows, tile = weight_ref.shape
-    hot = (lax.broadcasted_iota(jnp.int32, (boxes, tile), 0) == box_ref[...]).astype(jnp.bfloat16)
+    tile = data_ref.shape[1]
+    box = data_ref[4:5, :].astype(jnp.int32)
+    hot = (lax.broadcasted_iota(jnp.int32, (boxes, tile), 0) == box).astype(jnp.bfloat16)
     parts = jnp.dot(table_ref[...], hot, preferred_element_type=jnp.float32)
-    picked = parts[:rows] + parts[rows : 2 * rows] + parts[2 * rows :]
-    out_ref[...] = jnp.sum(weight_ref[...] * picked, axis=0, keepdims=True)
-
-
-def box_pick(table, box, weights, tile=1024):
-    rows, slots = weights.shape
+    picked = parts[:NODES] + parts[NODES : 2 * NODES] + parts[2 * NODES :]
+    out_ref[...] = jnp.sum(node_rows(data_ref, tile) * picked, axis=0, keepdims=True)
+
+
+def box_pick(table, data, tile=1024):
+    rows, slots = data.shape
     stacked = pieces_bf16(table, 0)
     return pl.pallas_call(
         box_pick_kernel,
         grid=(slots // tile,),
         in_specs=[
             pl.BlockSpec(stacked.shape, lambda i: (0, 0)),
-            pl.BlockSpec((1, tile), lambda i: (0, i)),
             pl.BlockSpec((rows, tile), lambda i: (0, i)),
         ],
         out_specs=pl.BlockSpec((1, tile), lambda i: (0, i)),
         out_shape=jax.ShapeDtypeStruct((1, slots), jnp.float32),
-    )(stacked, box, weights)[0]
+    )(stacked, data)[0]
 
 
 def shell_table():
@@ -370,19 +397,14 @@
     picked = atoms_to_slots(packed, atom_high, atom_low).reshape(4, *send_list.shape)
     outgoing = jnp.concatenate([picked, slot_box[None].astype(jnp.float32)], axis=0)
     arrived = lax.all_to_all(outgoing, DEV, split_axis=1, concat_axis=1, tiled=True)
-    arrived_charge = arrived[0].reshape(-1)
-    arrived_coords = arrived[1:4].reshape(3, -1)
-    slot_boxes = arrived[4].reshape(-1).astype(jnp.int32)
-    weight_table = node_weights(arrived_coords)
-    moments = box_sum(weight_table * arrived_charge[None, :], slot_boxes[None, :], BOXES)
+    arrived = arrived.reshape(arrived.shape[0], -1)
+    moments = box_sum(arrived, BOXES)
     node_grid = moments.reshape(NODES, BZ, BX, BY)
     reduced = jnp.einsum("nr,nzxy->rzxy", compress_v, node_grid, precision=lax.Precision.HIGHEST)
     padded = extended_2(reduced, ((GRP, 1), (DEV, 2)), 2)
     local_terms = translate(padded, m2l_kernels)
     expansion = jnp.dot(expand_u, local_terms.reshape(RANK, BOXES), precision=lax.Precision.HIGHEST)
-    slot_potential = box_pick(expansion, slot_boxes[None, :], weight_table).reshape(
-        send_list.shape
-    )
+    slot_potential = box_pick(expansion, arrived).reshape(send_list.shape)
     returned = lax.all_to_all(slot_potential, DEV, split_axis=0, concat_axis=0, tiled=True)
     potential = slots_to_atoms(returned.reshape(-1), atom_high, atom_low, atom_count)
     head_part = jnp.sum(potential[:, None] * hidden_two, axis=0) * grad_scale

time: 193 us -> 185 us (0.959)
  other arithmetic: 17.3 us -> 10.3 us
    mul x2 -> x0, other arithmetic: 1.99 us -> none  [node_weights(): along_z[:, None, None, :] * along_x[None, :, None, :]]
    mul x1 -> x0, local copies, waits for them, and re-layouts: 1.97 us -> none  [node_weights(): along_z[:, None, None, :] * along_x[None, :, None, :]]
where the time goes in v4:
time: 185 us; the launch traced here: 183 us
  starting transfers between devices  45.4 us (25%)
  blocking collectives  43.9 us (24%)
  Pallas kernels  29.1 us (16%)
  waiting for transfers between devices  22.4 us (12%)
  matrix products  22.3 us (12%)
  other arithmetic  10.3 us (6%)
  local copies, waits for them, and re-layouts  8.54 us (5%)
    ppermute x4, starting transfers between devices, swapped(): return lax.ppermute(x, axis, [(i, i ^ step) for i in range(count)])  24.9 us
    all_to_all x1, blocking collectives, shards(): lax.all_to_all(slot_potential, DEV, split_axis=0, concat_axis=0, tiled=True)  15.6 us
    all_to_all x1, blocking collectives, hybrid_sum(): lax.all_to_all(lines, plane, 0, 0, tiled=True).reshape(peers, -1)  14.4 us
    all_to_all x1, blocking collectives, hybrid_sum(): return lax.all_to_all(copies, plane, 0, 0, tiled=True).reshape(-1)[:length]  13.9 us
    all_to_all x1, starting transfers between devices, shards(): lax.all_to_all(outgoing, DEV, split_axis=1, concat_axis=1, tiled=True)  10.2 us
    pallas_call x1, Pallas kernels, box_sum(): pl.pallas_call(box_sum_kernel, grid=(slots // tile,), in_specs=[pl.BlockS...  9.87 us
    all_to_all x1, waiting for transfers between devices, shards(): lax.all_to_all(outgoing, DEV, split_axis=1, concat_axis=1, tiled=True)  8.64 us
    pallas_call x1, Pallas kernels, box_pick(): pl.pallas_call(box_pick_kernel, grid=(slots // tile,), in_specs=[pl.Block...  7.79 us
  transfers between devices with their start and end apart: 9, of which 8 were waited for; matrix products, arithmetic and copies ran while one was open for 1% of the time, Pallas kernels for 0%

profile of v4, /device:TPU:8, one launch (start us, length us, event | category | flops | bytes accessed | tf_op | source)
XLA Modules:
  0.0 183.1 jit_solution(12497677022548798216)
XLA Ops:
  0.6 0.8 convert_element_type.118
  1.5 0.4 copy-done
  1.9 2.8 %multiply_convert_fusion.1 = (bf16[4096,128]{1,0:T(8,128)(2,1)S(1)}, f32[4096,128]{1,0:T(8,128)}) fusion(bf16[4096,128]{1,0:T(8,128)(2,1)S(1)} %copy-done, bf16[128,128]{1,0:T(8,128)(2,1)} %param.16), kind=kOutput, calls=%fused_computation.8 | convolution fusion | flops 136839168 | bytes 4227072 | tf_op jit(solution)/shard_map/dot_general | solution.py:382
  4.9 2.0 %multiply_reduce_fusion.1 = (f32[4096]{0:T(1024)S(1)}, f32[4096,128]{1,0:T(8,128)}) fusion(f32[128]{0:T(128)S(1)} %copy-done.16, bf16[4096,128]{1,0:T(8,128)(2,1)S(1)} %get-tuple-element.29, bf16[128,128]{1,0:T(8,128)(2,1)S(1)} %copy-done.19), kind=kOutput, calls=%fused_computation.5 | convolution fusion | flops 137359360 | bytes 3195392 | tf_op jit(solution)/shard_map/dot_general | solution.py:384
  7.2 0.6 copy.78
  7.8 0.6 copy.79
  8.5 0.7 pad_maximum_fusion.3.table_ref
  9.2 6.5 %shard_map.164 = f32[4,8192]{1,0:T(4,128)} custom-call(bf16[768,64]{1,0:T(8,128)(2,1)} %pad_maximum_fusion.3.table_ref, s32[1,8192]{1,0:T(1,128)} %bitcast.193, s32[1,8192]{1,0:T(1,128)} %bitcast.195), custom_call_target="tpu_custom_call" | custom-call | tf_op jit(solution)/shard_map/pallas_call | solution.py:163
  15.7 1.7 pad_maximum_fusion.1
  17.3 10.2 %all-to-all-start = ((f32[5,32,256]{2,0,1:T(8,128)}), f32[5,32,256]{2,0,1:T(8,128)S(1)}, u32[]{:S(2)}, u32[]{:S(2)}) async-start(f32[5,32,256]{2,0,1:T(8,128)} %pad_maximum_fusion.1), calls=%async_computation | async-start | bytes 524288 | tf_op jit(solution)/shard_map/all_to_all | solution.py:399
  27.6 0.4 copy.44
  28.5 0.4 copy-done.11
  28.8 0.6 copy-done.9
  29.4 0.7 gather_fusion
  30.2 0.9 fusion.83
  31.0 8.6 %all-to-all-done = f32[5,32,256]{2,0,1:T(8,128)S(1)} async-done(((f32[5,32,256]{2,0,1:T(8,128)}), f32[5,32,256]{2,0,1:T(8,128)S(1)}, u32[]{:S(2)}, u32[]{:S(2)}) %all-to-all-start) | async-done | bytes 163872 | tf_op jit(solution)/shard_map/all_to_all | solution.py:399
  39.7 0.7 copy-done.1
  40.4 9.9 %shard_map.165 = f32[192,1024]{1,0:T(8,128)} custom-call(f32[5,8192]{1,0:T(8,128)} %bitcast.183), custom_call_target="tpu_custom_call" | custom-call | tf_op jit(solution)/shard_map/pallas_call | solution.py:259
  50.3 1.2 slice_add_fusion
  51.4 0.3 reshape.458
  51.8 0.5 convolution_bitcast_fusion.7
  52.3 1.3 collective-permute-start.1
  53.6 3.0 %collective-permute-start = (f32[16,2,4,64]{3,0,2,1:T(8,128)S(1)}, f32[16,2,4,64]{3,0,2,1:T(8,128)S(1)}, u32[]{:S(2)}, u32[]{:S(2)}) collective-permute-start(f32[16,2,4,64]{3,0,2,1:T(8,128)S(1)} %get-tuple-element.19), channel_id=1, source_target_pairs={{0,32},{32,64},{64,96},{96,128},{128,160},{160,192},{192,224},{224... | collective-permute-start | bytes 98312 | tf_op jit(solution)/shard_map/ppermute | solution.py:33
  56.7 0.8 collective-permute-done
  57.6 3.7 %collective-permute-start.3 = (f32[16,8,2,64]{3,0,2,1:T(8,128)S(1)}, f32[16,8,2,64]{3,0,2,1:T(8,128)S(1)}, u32[]{:S(2)}, u32[]{:S(2)}) collective-permute-start(f32[16,8,2,64]{3,0,2,1:T(8,128)S(1)} %get-tuple-element.16), channel_id=1, source_target_pairs={{1,0},{2,1},{3,2},{4,3},{5,4},{6,5},{7,6},{8,7},{9,8},{10,9},{11,1... | collective-permute-start | bytes 196616 | tf_op jit(solution)/shard_map/ppermute | solution.py:35
  61.3 2.4 %collective-permute-start.2 = (f32[16,8,2,64]{3,0,2,1:T(8,128)S(1)}, f32[16,8,2,64]{3,0,2,1:T(8,128)S(1)}, u32[]{:S(2)}, u32[]{:S(2)}) collective-permute-start(f32[16,8,2,64]{3,0,2,1:T(8,128)S(1)} %get-tuple-element.15), channel_id=1, source_target_pairs={{0,1},{1,2},{2,3},{3,4},{4,5},{5,6},{6,7},{7,8},{8,9},{9,10},{10,1... | collective-permute-start | bytes 196616 | tf_op jit(solution)/shard_map/ppermute | solution.py:33
  63.7 0.7 collective-permute-done.3
  64.5 6.0 %collective-permute-done.2 = f32[16,8,2,64]{3,0,2,1:T(8,128)S(1)} collective-permute-done((f32[16,8,2,64]{3,0,2,1:T(8,128)S(1)}, f32[16,8,2,64]{3,0,2,1:T(8,128)S(1)}, u32[]{:S(2)}, u32[]{:S(2)}) %collective-permute-start.2) | collective-permute-done | bytes 65568 | tf_op jit(solution)/shard_map/ppermute | solution.py:33
  70.5 1.2 convolution_bitcast_fusion
  71.6 1.3 convolution_bitcast_fusion.5
  73.0 1.3 convolution_bitcast_fusion.4
  74.3 1.3 convolution_bitcast_fusion.3
  75.6 1.3 convolution_bitcast_fusion.2
  76.9 1.3 convolution_bitcast_fusion.1
  78.2 1.0 fusion.13
  79.2 1.0 fusion.40
  80.3 1.0 fusion.37
  81.3 1.0 fusion.34
  82.4 1.2 fusion.31
  83.8 0.4 reduce-precision_convert_fusion.1
  84.2 0.8 pad_maximum_fusion.table_ref
  85.0 7.8 %shard_map.166 = f32[1,8192]{1,0:T(1,128)} custom-call(bf16[192,1024]{1,0:T(8,128)(2,1)} %pad_maximum_fusion.table_ref, f32[5,8192]{1,0:T(8,128)} %bitcast.184), custom_call_target="tpu_custom_call" | custom-call | tf_op jit(solution)/shard_map/pallas_call | solution.py:282
  92.8 15.6 %all_to_all.29 = f32[32,1,256]{2,1,0:T(1,128)S(1)} all-to-all(f32[32,1,256]{2,1,0:T(1,128)} %bitcast.198), channel_id=1, replica_groups=mesh['grp_0'=8,'grp_1'=2,'dev_0'=8,'dev_1'=4] {'dev_0','dev_1'}, dimensions={0} | all-to-all | bytes 65536 | tf_op jit(solution)/shard_map/all_to_all | solution.py:408
  108.4 0.7 pad_maximum_fusion.5.value_ref
  109.2 4.9 %shard_map.167 = f32[192,64]{1,0:T(8,128)} custom-call(f32[3,8192]{1,0:T(4,128)} %pad_maximum_fusion.5.value_ref, s32[1,8192]{1,0:T(1,128)} %bitcast.194, s32[1,8192]{1,0:T(1,128)} %bitcast.196), custom_call_target="tpu_custom_call" | custom-call | tf_op jit(solution)/shard_map/pallas_call | solution.py:199
  114.1 0.8 slice_add_fusion.2
  115.3 2.4 %multiply_convert_fusion = (bf16[4096,128]{1,0:T(8,128)(2,1)S(1)}, f32[128]{0:T(128)S(1)}) fusion(f32[4096,128]{1,0:T(8,128)} %get-tuple-element.32, f32[4096]{0:T(1024)S(1)} %reshape.461, f32[128]{0:T(128)S(1)} %copy-done.17), kind=kLoop, calls=%fused_computation.4 | loop fusion | flops 6815616 | bytes 3163136 | tf_op jit(solution)/shard_map/convert_element_type | solution.py:412
  117.7 0.5 fusion.43
  118.2 2.6 %fusion.45 = f32[128,128]{0,1:T(8,128)S(1)} fusion(bf16[4096,128]{1,0:T(8,128)(2,1)S(1)} %copy-done, bf16[4096,128]{1,0:T(8,128)(2,1)S(1)} %get-tuple-element.5, bf16[128,128]{1,0:T(8,128)(2,1)S(1)} %copy-done.20, f32[4096,128]{1,0:T(8,128)} %get-tuple-element.30), kind=kOutput, calls=%fused_computation.47 | convolution fusion | flops 273170432 | bytes 4292608 | tf_op jit(solution)/shard_map/dot_general | solution.py:424
  121.0 1.9 %collective-permute-start.4 = (f32[32902]{0:T(1024)S(1)}, f32[32902]{0:T(1024)S(1)}, u32[]{:S(2)}, u32[]{:S(2)}) collective-permute-start(f32[32902]{0:T(1024)S(1)} %pad_maximum_fusion.4), channel_id=1, source_target_pairs={{0,32},{32,0},{1,33},{33,1},{2,34},{34,2},{3,35},{35,3},{4,36},{36... | collective-permute-start | bytes 394832 | tf_op jit(solution)/shard_map/ppermute | solution.py:101
  122.9 1.3 collective-permute-done.4
  124.3 0.2 all_to_all.22
  124.5 14.4 %all_to_all.30 = f32[32,1,1029]{2,1,0:T(1,128)S(1)} all-to-all(f32[32,1,1029]{2,1,0:T(1,128)S(1)} %all_to_all.22), channel_id=1, replica_groups=mesh['grp_0'=8,'grp_1'=2,'dev_0'=8,'dev_1'=4] {'dev_0','dev_1'}, dimensions={0} | all-to-all | bytes 263424 | tf_op jit(solution)/shard_map/all_to_all | solution.py:117
  139.1 6.7 %collective-permute-start.5 = (f32[1029]{0:T(1024)S(1)}, f32[1029]{0:T(1024)S(1)}, u32[]{:S(2)}, u32[]{:S(2)}) collective-permute-start(f32[1029]{0:T(1024)S(1)} %reduce_sum.29), channel_id=1, source_target_pairs={{0,64},{64,0},{128,192},{192,128},{256,320},{320,256},{384,448},{4... | collective-permute-start | bytes 12356 | tf_op jit(solution)/shard_map/ppermute | solution.py:101
  145.8 1.6 collective-permute-done.5
  147.4 7.0 %collective-permute-start.6 = (f32[1029]{0:T(1024)S(1)}, f32[1029]{0:T(1024)S(1)}, u32[]{:S(2)}, u32[]{:S(2)}) collective-permute-start(f32[1029]{0:T(1024)S(1)} %add.207), channel_id=1, source_target_pairs={{0,128},{64,192},{128,0},{192,64},{256,384},{320,448},{384,256},{4... | collective-permute-start | bytes 12356 | tf_op jit(solution)/shard_map/ppermute | solution.py:101
  154.4 1.6 collective-permute-done.6
  156.1 9.3 %collective-permute-start.7 = (f32[1029]{0:T(1024)S(1)}, f32[1029]{0:T(1024)S(1)}, u32[]{:S(2)}, u32[]{:S(2)}) collective-permute-start(f32[1029]{0:T(1024)S(1)} %add.208), channel_id=1, source_target_pairs={{0,256},{64,320},{128,384},{192,448},{256,0},{320,64},{384,128},{4... | collective-permute-start | bytes 12356 | tf_op jit(solution)/shard_map/ppermute | solution.py:101
  165.3 1.6 collective-permute-done.7
  167.0 13.9 %all_to_all.31 = f32[32,1,1029]{2,1,0:T(1,128)S(1)} all-to-all(f32[32,1,1029]{2,1,0:T(1,128)S(1)} %broadcast_in_dim.10), channel_id=1, replica_groups=mesh['grp_0'=8,'grp_1'=2,'dev_0'=8,'dev_1'=4] {'dev_0','dev_1'}, dimensions={0} | all-to-all | bytes 263424 | tf_op jit(solution)/shard_map/all_to_all | solution.py:120
  180.9 0.3 reduce.1
  181.4 0.7 slice_bitcast_fusion.10
  182.1 0.5 slice.130
  182.6 0.5 slice.131
  (91 shorter events, 2.1 us)
Async XLA Ops:
  0.6 1.2 copy-start
  1.9 2.8 %copy-start.21 = (s32[4096]{0:T(1024)S(1)}, s32[4096]{0:T(1024)}, u32[]{:S(2)}) copy-start(s32[4096]{0:T(1024)} %param.15) | copy-start | bytes 49156
  1.9 2.8 %copy-start.23 = (f32[6]{0:T(128)S(1)}, f32[6]{0:T(128)}, u32[]{:S(2)}) copy-start(f32[6]{0:T(128)} %param.19) | copy-start | bytes 76
  1.9 3.0 %copy-start.16 = (f32[128]{0:T(128)S(1)}, f32[128]{0:T(128)}, u32[]{:S(2)}) copy-start(f32[128]{0:T(128)} %param.18) | copy-start | bytes 1540
  1.9 3.0 %copy-start.19 = (bf16[128,128]{1,0:T(8,128)(2,1)S(1)}, bf16[128,128]{1,0:T(8,128)(2,1)}, u32[]{:S(2)}) copy-start(bf16[128,128]{1,0:T(8,128)(2,1)} %param.17) | copy-start | bytes 98308
  4.7 2.2 %copy-start.2 = (bf16[4096,128]{1,0:T(8,128)(2,1)}, bf16[4096,128]{1,0:T(8,128)(2,1)S(1)}, u32[]{:S(2)}) copy-start(bf16[4096,128]{1,0:T(8,128)(2,1)S(1)} %get-tuple-element.29) | copy-start | bytes 3145732
  4.9 2.0 %copy-start.8 = (f32[3,4096]{1,0:T(4,128)S(1)}, f32[3,4096]{1,0:T(4,128)}, u32[]{:S(2)}) copy-start(f32[3,4096]{1,0:T(4,128)} %param.14) | copy-start | bytes 147460
  4.9 2.2 %copy-start.13 = (s32[32,256]{1,0:T(8,128)S(1)}, s32[32,256]{1,0:T(8,128)}, u32[]{:S(2)}) copy-start(s32[32,256]{1,0:T(8,128)} %param.23) | copy-start | bytes 98308
  6.9 20.7 %copy-start.6 = (f32[98,16,16]{0,2,1:T(8,128)S(1)}, f32[98,16,16]{0,2,1:T(8,128)}, u32[]{:S(2)}) copy-start(f32[98,16,16]{0,2,1:T(8,128)} %param.20) | copy-start | bytes 301060
  8.5 20.9 %copy-start.18 = (s32[125]{0:T(128)S(1)}, s32[125]{0:T(128)}, u32[]{:S(2)}) copy-start(s32[125]{0:T(128)} %constant.75) | copy-start | bytes 1504
  17.3 22.3 %all-to-all-start = ((f32[5,32,256]{2,0,1:T(8,128)}), f32[5,32,256]{2,0,1:T(8,128)S(1)}, u32[]{:S(2)}, u32[]{:S(2)}) async-start(f32[5,32,256]{2,0,1:T(8,128)} %pad_maximum_fusion.1), calls=%async_computation | async-start | bytes 524288 | tf_op jit(solution)/shard_map/all_to_all | solution.py:399
  28.2 0.6 copy-start.11
  28.8 0.6 copy-start.9
  30.2 21.6 %copy-start.15 = (f32[64,16]{0,1:T(8,128)S(1)}, f32[64,16]{0,1:T(8,128)}, u32[]{:S(2)}) copy-start(f32[64,16]{0,1:T(8,128)} %param.22) | copy-start | bytes 12292
  39.7 0.7 copy-start.1
  50.3 13.4 %copy-start.10 = (pred[5,8,4]{1,2,0:T(4,128)(4,1)S(1)}, pred[5,8,4]{1,2,0:T(4,128)(4,1)}, u32[]{:S(2)}) copy-start(pred[5,8,4]{1,2,0:T(4,128)(4,1)} %copy-done.9) | copy-start | bytes 484
  50.3 20.2 %copy-start.12 = (pred[5,64,64]{2,1,0:T(8,128)(4,1)S(1)}, pred[5,64,64]{2,1,0:T(8,128)(4,1)}, u32[]{:S(2)}) copy-start(pred[5,64,64]{2,1,0:T(8,128)(4,1)} %copy-done.11) | copy-start | bytes 61444
  52.3 4.4 %collective-permute-start.1 = (f32[16,2,4,64]{3,0,2,1:T(8,128)S(1)}, f32[16,2,4,64]{3,0,2,1:T(8,128)S(1)}, u32[]{:S(2)}, u32[]{:S(2)}) collective-permute-start(f32[16,2,4,64]{3,0,2,1:T(8,128)S(1)} %get-tuple-element.20), channel_id=1, source_target_pairs={{32,0},{64,32},{96,64},{128,96},{160,128},{192,160},{224,192},{256... | collective-permute-start | bytes 98312 | tf_op jit(solution)/shard_map/ppermute | solution.py:35
  53.6 3.9 %collective-permute-start = (f32[16,2,4,64]{3,0,2,1:T(8,128)S(1)}, f32[16,2,4,64]{3,0,2,1:T(8,128)S(1)}, u32[]{:S(2)}, u32[]{:S(2)}) collective-permute-start(f32[16,2,4,64]{3,0,2,1:T(8,128)S(1)} %get-tuple-element.19), channel_id=1, source_target_pairs={{0,32},{32,64},{64,96},{96,128},{128,160},{160,192},{192,224},{224... | collective-permute-start | bytes 98312 | tf_op jit(solution)/shard_map/ppermute | solution.py:33
  56.7 14.9 %copy-start.5 = (f32[25,16,16]{2,1,0:T(8,128)S(1)}, f32[25,16,16]{2,1,0:T(8,128)}, u32[]{:S(2)}) copy-start(f32[25,16,16]{2,1,0:T(8,128)} %get-tuple-element.11) | copy-start | bytes 76804
  57.6 6.9 %collective-permute-start.3 = (f32[16,8,2,64]{3,0,2,1:T(8,128)S(1)}, f32[16,8,2,64]{3,0,2,1:T(8,128)S(1)}, u32[]{:S(2)}, u32[]{:S(2)}) collective-permute-start(f32[16,8,2,64]{3,0,2,1:T(8,128)S(1)} %get-tuple-element.16), channel_id=1, source_target_pairs={{1,0},{2,1},{3,2},{4,3},{5,4},{6,5},{7,6},{8,7},{9,8},{10,9},{11,1... | collective-permute-start | bytes 196616 | tf_op jit(solution)/shard_map/ppermute | solution.py:35
  61.3 9.2 %collective-permute-start.2 = (f32[16,8,2,64]{3,0,2,1:T(8,128)S(1)}, f32[16,8,2,64]{3,0,2,1:T(8,128)S(1)}, u32[]{:S(2)}, u32[]{:S(2)}) collective-permute-start(f32[16,8,2,64]{3,0,2,1:T(8,128)S(1)} %get-tuple-element.15), channel_id=1, source_target_pairs={{0,1},{1,2},{2,3},{3,4},{4,5},{5,6},{6,7},{7,8},{8,9},{9,10},{10,1... | collective-permute-start | bytes 196616 | tf_op jit(solution)/shard_map/ppermute | solution.py:33
  71.6 1.3 copy-start.4
  80.3 3.5 %copy-start.14 = (f32[64,16]{0,1:T(8,128)S(1)}, f32[64,16]{0,1:T(8,128)}, u32[]{:S(2)}) copy-start(f32[64,16]{0,1:T(8,128)} %param.21) | copy-start | bytes 12292
  82.3 32.7 %copy-start.22 = (s32[4096]{0:T(1024)S(1)}, s32[4096]{0:T(1024)}, u32[]{:S(2)}) copy-start(s32[4096]{0:T(1024)} %param.15) | copy-start | bytes 49156
  82.3 32.9 %copy-start.17 = (f32[128]{0:T(128)S(1)}, f32[128]{0:T(128)}, u32[]{:S(2)}) copy-start(f32[128]{0:T(128)} %param.18) | copy-start | bytes 1540
  92.8 24.9 %copy-start.3 = (bf16[4096,128]{1,0:T(8,128)(2,1)S(1)}, bf16[4096,128]{1,0:T(8,128)(2,1)}, u32[]{:S(2)}) copy-start(bf16[4096,128]{1,0:T(8,128)(2,1)} %copy-done.2) | copy-start | bytes 3145732
  114.9 3.3 %copy-start.7 = (f32[4096]{0:T(1024)}, f32[4096]{0:T(1024)S(1)}, u32[]{:S(2)}) copy-start(f32[4096]{0:T(1024)S(1)} %reshape.461) | copy-start | bytes 49156
  115.3 3.0 %copy-start.20 = (bf16[128,128]{1,0:T(8,128)(2,1)S(1)}, bf16[128,128]{1,0:T(8,128)(2,1)}, u32[]{:S(2)}) copy-start(bf16[128,128]{1,0:T(8,128)(2,1)} %param.17) | copy-start | bytes 98308
  121.0 3.2 %collective-permute-start.4 = (f32[32902]{0:T(1024)S(1)}, f32[32902]{0:T(1024)S(1)}, u32[]{:S(2)}, u32[]{:S(2)}) collective-permute-start(f32[32902]{0:T(1024)S(1)} %pad_maximum_fusion.4), channel_id=1, source_target_pairs={{0,32},{32,0},{1,33},{33,1},{2,34},{34,2},{3,35},{35,3},{4,36},{36... | collective-permute-start | bytes 394832 | tf_op jit(solution)/shard_map/ppermute | solution.py:101
  139.1 8.3 %collective-permute-start.5 = (f32[1029]{0:T(1024)S(1)}, f32[1029]{0:T(1024)S(1)}, u32[]{:S(2)}, u32[]{:S(2)}) collective-permute-start(f32[1029]{0:T(1024)S(1)} %reduce_sum.29), channel_id=1, source_target_pairs={{0,64},{64,0},{128,192},{192,128},{256,320},{320,256},{384,448},{4... | collective-permute-start | bytes 12356 | tf_op jit(solution)/shard_map/ppermute | solution.py:101
  147.4 8.7 %collective-permute-start.6 = (f32[1029]{0:T(1024)S(1)}, f32[1029]{0:T(1024)S(1)}, u32[]{:S(2)}, u32[]{:S(2)}) collective-permute-start(f32[1029]{0:T(1024)S(1)} %add.207), channel_id=1, source_target_pairs={{0,128},{64,192},{128,0},{192,64},{256,384},{320,448},{384,256},{4... | collective-permute-start | bytes 12356 | tf_op jit(solution)/shard_map/ppermute | solution.py:101
  156.1 10.9 %collective-permute-start.7 = (f32[1029]{0:T(1024)S(1)}, f32[1029]{0:T(1024)S(1)}, u32[]{:S(2)}, u32[]{:S(2)}) collective-permute-start(f32[1029]{0:T(1024)S(1)} %add.208), channel_id=1, source_target_pairs={{0,256},{64,320},{128,384},{192,448},{256,0},{320,64},{384,128},{4... | collective-permute-start | bytes 12356 | tf_op jit(solution)/shard_map/ppermute | solution.py:101

commit v5 on v4

--- a/solution.py
+++ b/solution.py
@@ -140,8 +140,10 @@
     return jnp.concatenate([p.astype(jnp.bfloat16) for p in split_three(x)], axis=axis)
 
 
-def atoms_to_slots_kernel(table_ref, high_ref, low_ref, out_ref):
+def atoms_to_slots_kernel(table_ref, high_ref, low_ref, box_ref, out_ref):
     rows, tile = out_ref.shape
+    rows -= 1
+    out_ref[rows : rows + 1, :] = box_ref[...].astype(jnp.float32)
     side = table_ref.shape[1]
     lines = lax.broadcasted_iota(jnp.int32, (side, tile), 0)
     low = (lines == low_ref[...]).astype(jnp.bfloat16)
@@ -155,7 +157,7 @@
         )
 
 
-def atoms_to_slots(values, high, low, tile=1024):
+def atoms_to_slots(values, high, low, box, tile=1024):
     rows, count = values.shape
     side = int(round(math.sqrt(count)))
     table = pieces_bf16(values.reshape(rows * side, side), 0)
@@ -167,10 +169,11 @@
             pl.BlockSpec(table.shape, lambda i: (0, 0)),
             pl.BlockSpec((1, tile), lambda i: (0, i)),
             pl.BlockSpec((1, tile), lambda i: (0, i)),
+            pl.BlockSpec((1, tile), lambda i: (0, i)),
         ],
-        out_specs=pl.BlockSpec((rows, tile), lambda i: (0, i)),
-        out_shape=jax.ShapeDtypeStruct((rows, slots), jnp.float32),
-    )(table, high, low)
+        out_specs=pl.BlockSpec((rows + 1, tile), lambda i: (0, i)),
+        out_shape=jax.ShapeDtypeStruct((rows + 1, slots), jnp.float32),
+    )(table, high, low, box)
 
 
 def slots_to_atoms_kernel(value_ref, high_ref, low_ref, out_ref):
@@ -183,8 +186,13 @@
     lines = lax.broadcasted_iota(jnp.int32, (side, tile), 0)
     hit = lines == high_ref[...]
     low = (lines == low_ref[...]).astype(jnp.bfloat16)
+    value = value_ref[...]
+    high_part = value.astype(jnp.bfloat16).astype(jnp.float32)
+    rest = value - high_part
+    middle_part = rest.astype(jnp.bfloat16).astype(jnp.float32)
+    low_part = rest - middle_part
     stacked = jnp.concatenate(
-        [jnp.where(hit, value_ref[k : k + 1, :], 0.0).astype(jnp.bfloat16) for k in range(3)],
+        [jnp.where(hit, p, 0.0).astype(jnp.bfloat16) for p in (high_part, middle_part, low_part)],
         axis=0,
     )
     out_ref[...] += lax.dot_general(
@@ -194,13 +202,13 @@
 
 def slots_to_atoms(values, high, low, count, tile=1024):
     side = int(round(math.sqrt(count)))
-    pieces = jnp.stack(split_three(values), 0)
+    pieces = values.reshape(1, -1)
     slots = values.shape[0]
     parts = pl.pallas_call(
         slots_to_atoms_kernel,
         grid=(slots // tile,),
         in_specs=[
-            pl.BlockSpec((3, tile), lambda i: (0, i)),
+            pl.BlockSpec((1, tile), lambda i: (0, i)),
             pl.BlockSpec((1, tile), lambda i: (0, i)),
             pl.BlockSpec((1, tile), lambda i: (0, i)),
         ],
@@ -394,8 +402,8 @@
     atom_high = jnp.where(is_used, send_list // side, -1).reshape(1, -1)
     atom_low = (send_list % side).reshape(1, -1)
     packed = jnp.concatenate([charge[None, :], positions], axis=0)
-    picked = atoms_to_slots(packed, atom_high, atom_low).reshape(4, *send_list.shape)
-    outgoing = jnp.concatenate([picked, slot_box[None].astype(jnp.float32)], axis=0)
+    outgoing = atoms_to_slots(packed, atom_high, atom_low, slot_box.reshape(1, -1))
+    outgoing = outgoing.reshape(outgoing.shape[0], *send_list.shape)
     arrived = lax.all_to_all(outgoing, DEV, split_axis=1, concat_axis=1, tiled=True)
     arrived = arrived.reshape(arrived.shape[0], -1)
     moments = box_sum(arrived, BOXES)

time: 185 us -> 183 us (0.989)
  other arithmetic: 10.3 us -> 6.94 us
    unnamed x51 -> x54, local copies, waits for them, and re-layouts: 3.8 us -> 5.28 us
where the time goes in v5:
time: 183 us; the launch traced here: 181 us
  starting transfers between devices  45.4 us (25%)
  blocking collectives  43.9 us (24%)
  Pallas kernels  29.1 us (16%)
  waiting for transfers between devices  22.4 us (12%)
  matrix products  22.3 us (12%)
  local copies, waits for them, and re-layouts  10 us (5%)
  other arithmetic  6.94 us (4%)
    ppermute x4, starting transfers between devices, swapped(): return lax.ppermute(x, axis, [(i, i ^ step) for i in range(count)])  24.9 us
    all_to_all x1, blocking collectives, shards(): lax.all_to_all(slot_potential, DEV, split_axis=0, concat_axis=0, tiled=True)  15.5 us
    all_to_all x1, blocking collectives, hybrid_sum(): lax.all_to_all(lines, plane, 0, 0, tiled=True).reshape(peers, -1)  14.4 us
    all_to_all x1, blocking collectives, hybrid_sum(): return lax.all_to_all(copies, plane, 0, 0, tiled=True).reshape(-1)[:length]  13.9 us
    all_to_all x1, starting transfers between devices, shards(): lax.all_to_all(outgoing, DEV, split_axis=1, concat_axis=1, tiled=True)  10.2 us
    pallas_call x1, Pallas kernels, box_sum(): pl.pallas_call(box_sum_kernel, grid=(slots // tile,), in_specs=[pl.BlockS...  9.87 us
    all_to_all x1, waiting for transfers between devices, shards(): lax.all_to_all(outgoing, DEV, split_axis=1, concat_axis=1, tiled=True)  8.63 us
    pallas_call x1, Pallas kernels, box_pick(): pl.pallas_call(box_pick_kernel, grid=(slots // tile,), in_specs=[pl.Block...  7.88 us
  transfers between devices with their start and end apart: 9, of which 8 were waited for; matrix products, arithmetic and copies ran while one was open for 1% of the time, Pallas kernels for 0%

profile of v5, /device:TPU:8, one launch (start us, length us, event | category | flops | bytes accessed | tf_op | source)
XLA Modules:
  0.0 181.3 jit_solution(12743492371577496520)
XLA Ops:
  0.7 1.2 copy-done
  1.9 2.7 %multiply_convert_fusion.1 = (bf16[4096,128]{1,0:T(8,128)(2,1)S(1)}, f32[4096,128]{1,0:T(8,128)}) fusion(bf16[4096,128]{1,0:T(8,128)(2,1)S(1)} %copy-done, bf16[128,128]{1,0:T(8,128)(2,1)} %param.16), kind=kOutput, calls=%fused_computation.8 | convolution fusion | flops 136839168 | bytes 4227072 | tf_op jit(solution)/shard_map/dot_general | solution.py:390
  4.6 0.2 fusion.60
  4.9 2.0 %multiply_reduce_fusion.1 = (f32[4096]{0:T(1024)S(1)}, f32[4096,128]{1,0:T(8,128)}) fusion(f32[128]{0:T(128)S(1)} %copy-done.17, bf16[4096,128]{1,0:T(8,128)(2,1)S(1)} %get-tuple-element.26, bf16[128,128]{1,0:T(8,128)(2,1)S(1)} %copy-done.20), kind=kOutput, calls=%fused_computation.5 | convolution fusion | flops 137359360 | bytes 3195392 | tf_op jit(solution)/shard_map/dot_general | solution.py:392
  7.1 0.6 copy.78
  7.8 0.6 copy.79
  8.4 0.6 copy.80
  9.1 0.7 pad_maximum_fusion.2.table_ref
  9.8 6.6 %shard_map.164 = f32[5,8192]{1,0:T(8,128)} custom-call(bf16[768,64]{1,0:T(8,128)(2,1)} %pad_maximum_fusion.2.table_ref, s32[1,8192]{1,0:T(1,128)} %bitcast.196, s32[1,8192]{1,0:T(1,128)} %bitcast.198, s32[1,8192]{1,0:T(1,128)} %bitcast.200), custom_call_target="tpu_custom_call" | custom-call | tf_op jit(solution)/shard_map/pallas_call | solution.py:165
  16.4 10.2 %all-to-all-start = ((f32[5,32,256]{2,0,1:T(8,128)}), f32[5,32,256]{2,0,1:T(8,128)S(1)}, u32[]{:S(2)}, u32[]{:S(2)}) async-start(f32[5,32,256]{2,0,1:T(8,128)} %bitcast.188), calls=%async_computation | async-start | bytes 524288 | tf_op jit(solution)/shard_map/all_to_all | solution.py:407
  26.7 0.4 copy.44
  27.5 0.4 copy-done.11
  27.9 0.6 copy-done.9
  28.5 0.7 gather_fusion
  29.2 0.9 fusion.83
  30.1 8.6 %all-to-all-done = f32[5,32,256]{2,0,1:T(8,128)S(1)} async-done(((f32[5,32,256]{2,0,1:T(8,128)}), f32[5,32,256]{2,0,1:T(8,128)S(1)}, u32[]{:S(2)}, u32[]{:S(2)}) %all-to-all-start) | async-done | bytes 163872 | tf_op jit(solution)/shard_map/all_to_all | solution.py:407
  38.7 0.7 copy-done.1
  39.4 9.9 %shard_map.165 = f32[192,1024]{1,0:T(8,128)} custom-call(f32[5,8192]{1,0:T(8,128)} %bitcast.186), custom_call_target="tpu_custom_call" | custom-call | tf_op jit(solution)/shard_map/pallas_call | solution.py:267
  49.3 1.2 slice_add_fusion
  50.5 0.3 reshape.420
  50.8 0.5 convolution_bitcast_fusion.7
  51.4 1.3 collective-permute-start.1
  52.7 3.0 %collective-permute-start = (f32[16,2,4,64]{3,0,2,1:T(8,128)S(1)}, f32[16,2,4,64]{3,0,2,1:T(8,128)S(1)}, u32[]{:S(2)}, u32[]{:S(2)}) collective-permute-start(f32[16,2,4,64]{3,0,2,1:T(8,128)S(1)} %get-tuple-element.19), channel_id=1, source_target_pairs={{0,32},{32,64},{64,96},{96,128},{128,160},{160,192},{192,224},{224... | collective-permute-start | bytes 98312 | tf_op jit(solution)/shard_map/ppermute | solution.py:33
  55.8 0.8 collective-permute-done
  56.7 3.7 %collective-permute-start.3 = (f32[16,8,2,64]{3,0,2,1:T(8,128)S(1)}, f32[16,8,2,64]{3,0,2,1:T(8,128)S(1)}, u32[]{:S(2)}, u32[]{:S(2)}) collective-permute-start(f32[16,8,2,64]{3,0,2,1:T(8,128)S(1)} %get-tuple-element.16), channel_id=1, source_target_pairs={{1,0},{2,1},{3,2},{4,3},{5,4},{6,5},{7,6},{8,7},{9,8},{10,9},{11,1... | collective-permute-start | bytes 196616 | tf_op jit(solution)/shard_map/ppermute | solution.py:35
  60.3 2.4 %collective-permute-start.2 = (f32[16,8,2,64]{3,0,2,1:T(8,128)S(1)}, f32[16,8,2,64]{3,0,2,1:T(8,128)S(1)}, u32[]{:S(2)}, u32[]{:S(2)}) collective-permute-start(f32[16,8,2,64]{3,0,2,1:T(8,128)S(1)} %get-tuple-element.15), channel_id=1, source_target_pairs={{0,1},{1,2},{2,3},{3,4},{4,5},{5,6},{6,7},{7,8},{8,9},{9,10},{10,1... | collective-permute-start | bytes 196616 | tf_op jit(solution)/shard_map/ppermute | solution.py:33
  62.8 0.7 collective-permute-done.3
  63.5 6.0 %collective-permute-done.2 = f32[16,8,2,64]{3,0,2,1:T(8,128)S(1)} collective-permute-done((f32[16,8,2,64]{3,0,2,1:T(8,128)S(1)}, f32[16,8,2,64]{3,0,2,1:T(8,128)S(1)}, u32[]{:S(2)}, u32[]{:S(2)}) %collective-permute-start.2) | collective-permute-done | bytes 65568 | tf_op jit(solution)/shard_map/ppermute | solution.py:33
  69.5 1.2 convolution_bitcast_fusion
  70.7 1.3 convolution_bitcast_fusion.5
  72.0 1.3 convolution_bitcast_fusion.4
  73.3 1.3 convolution_bitcast_fusion.3
  74.6 1.3 convolution_bitcast_fusion.2
  75.9 1.3 convolution_bitcast_fusion.1
  77.3 1.0 fusion.13
  78.3 1.0 fusion.40
  79.3 1.0 fusion.37
  80.4 1.0 fusion.34
  81.4 1.2 fusion.31
  82.8 0.4 reduce-precision_convert_fusion.1
  83.3 0.8 pad_maximum_fusion.table_ref
  84.0 7.9 %shard_map.166 = f32[1,8192]{1,0:T(1,128)} custom-call(bf16[192,1024]{1,0:T(8,128)(2,1)} %pad_maximum_fusion.table_ref, f32[5,8192]{1,0:T(8,128)} %bitcast.187), custom_call_target="tpu_custom_call" | custom-call | tf_op jit(solution)/shard_map/pallas_call | solution.py:290
  91.9 15.5 %all_to_all.29 = f32[32,1,256]{2,1,0:T(1,128)} all-to-all(f32[32,1,256]{2,1,0:T(1,128)} %bitcast.202), channel_id=1, replica_groups=mesh['grp_0'=8,'grp_1'=2,'dev_0'=8,'dev_1'=4] {'dev_0','dev_1'}, dimensions={0} | all-to-all | bytes 65536 | tf_op jit(solution)/shard_map/all_to_all | solution.py:416
  107.5 4.8 %shard_map.167 = f32[192,64]{1,0:T(8,128)} custom-call(f32[1,8192]{1,0:T(1,128)} %bitcast.201, s32[1,8192]{1,0:T(1,128)} %bitcast.197, s32[1,8192]{1,0:T(1,128)} %bitcast.199), custom_call_target="tpu_custom_call" | custom-call | tf_op jit(solution)/shard_map/pallas_call | solution.py:207
  112.2 0.8 slice_add_fusion.2
  113.2 0.2 fusion.46
  113.5 2.4 %multiply_convert_fusion = (bf16[4096,128]{1,0:T(8,128)(2,1)S(1)}, f32[128]{0:T(128)S(1)}) fusion(f32[4096,128]{1,0:T(8,128)} %get-tuple-element.29, f32[4096]{0:T(1024)S(1)} %reshape.422, f32[128]{0:T(128)S(1)} %copy-done.18), kind=kLoop, calls=%fused_computation.4 | loop fusion | flops 6815616 | bytes 3163136 | tf_op jit(solution)/shard_map/convert_element_type | solution.py:420
  115.9 0.5 fusion.43
  116.4 2.6 %fusion.45 = f32[128,128]{0,1:T(8,128)S(1)} fusion(bf16[4096,128]{1,0:T(8,128)(2,1)S(1)} %copy-done, bf16[4096,128]{1,0:T(8,128)(2,1)S(1)} %get-tuple-element.5, bf16[128,128]{1,0:T(8,128)(2,1)S(1)} %copy-done.21, f32[4096,128]{1,0:T(8,128)} %get-tuple-element.27), kind=kOutput, calls=%fused_computation.47 | convolution fusion | flops 273170432 | bytes 4292608 | tf_op jit(solution)/shard_map/dot_general | solution.py:432
  119.1 1.9 %collective-permute-start.4 = (f32[32902]{0:T(1024)S(1)}, f32[32902]{0:T(1024)S(1)}, u32[]{:S(2)}, u32[]{:S(2)}) collective-permute-start(f32[32902]{0:T(1024)S(1)} %pad_maximum_fusion.3), channel_id=1, source_target_pairs={{0,32},{32,0},{1,33},{33,1},{2,34},{34,2},{3,35},{35,3},{4,36},{36... | collective-permute-start | bytes 394832 | tf_op jit(solution)/shard_map/ppermute | solution.py:101
  121.1 1.3 collective-permute-done.4
  122.4 0.2 all_to_all.22
  122.7 14.4 %all_to_all.30 = f32[32,1,1029]{2,1,0:T(1,128)S(1)} all-to-all(f32[32,1,1029]{2,1,0:T(1,128)S(1)} %all_to_all.22), channel_id=1, replica_groups=mesh['grp_0'=8,'grp_1'=2,'dev_0'=8,'dev_1'=4] {'dev_0','dev_1'}, dimensions={0} | all-to-all | bytes 263424 | tf_op jit(solution)/shard_map/all_to_all | solution.py:117
  137.2 6.7 %collective-permute-start.5 = (f32[1029]{0:T(1024)S(1)}, f32[1029]{0:T(1024)S(1)}, u32[]{:S(2)}, u32[]{:S(2)}) collective-permute-start(f32[1029]{0:T(1024)S(1)} %reduce_sum.29), channel_id=1, source_target_pairs={{0,64},{64,0},{128,192},{192,128},{256,320},{320,256},{384,448},{4... | collective-permute-start | bytes 12356 | tf_op jit(solution)/shard_map/ppermute | solution.py:101
  143.9 1.6 collective-permute-done.5
  145.6 7.1 %collective-permute-start.6 = (f32[1029]{0:T(1024)S(1)}, f32[1029]{0:T(1024)S(1)}, u32[]{:S(2)}, u32[]{:S(2)}) collective-permute-start(f32[1029]{0:T(1024)S(1)} %add.207), channel_id=1, source_target_pairs={{0,128},{64,192},{128,0},{192,64},{256,384},{320,448},{384,256},{4... | collective-permute-start | bytes 12356 | tf_op jit(solution)/shard_map/ppermute | solution.py:101
  152.6 1.6 collective-permute-done.6
  154.2 9.2 %collective-permute-start.7 = (f32[1029]{0:T(1024)S(1)}, f32[1029]{0:T(1024)S(1)}, u32[]{:S(2)}, u32[]{:S(2)}) collective-permute-start(f32[1029]{0:T(1024)S(1)} %add.208), channel_id=1, source_target_pairs={{0,256},{64,320},{128,384},{192,448},{256,0},{320,64},{384,128},{4... | collective-permute-start | bytes 12356 | tf_op jit(solution)/shard_map/ppermute | solution.py:101
  163.5 1.6 collective-permute-done.7
  165.2 13.9 %all_to_all.31 = f32[32,1,1029]{2,1,0:T(1,128)S(1)} all-to-all(f32[32,1,1029]{2,1,0:T(1,128)S(1)} %broadcast_in_dim.10), channel_id=1, replica_groups=mesh['grp_0'=8,'grp_1'=2,'dev_0'=8,'dev_1'=4] {'dev_0','dev_1'}, dimensions={0} | all-to-all | bytes 263424 | tf_op jit(solution)/shard_map/all_to_all | solution.py:120
  179.1 0.3 reduce.1
  179.6 0.7 slice_bitcast_fusion.10
  180.2 0.5 slice.130
  180.7 0.5 slice.131
  (89 shorter events, 1.7 us)
Async XLA Ops:
  0.6 1.2 copy-start
  0.6 4.0 %copy-start.22 = (s32[4096]{0:T(1024)S(1)}, s32[4096]{0:T(1024)}, u32[]{:S(2)}) copy-start(s32[4096]{0:T(1024)} %param.15) | copy-start | bytes 49156
  0.7 3.9 %copy-start.24 = (f32[6]{0:T(128)S(1)}, f32[6]{0:T(128)}, u32[]{:S(2)}) copy-start(f32[6]{0:T(128)} %param.19) | copy-start | bytes 76
  0.7 4.1 %copy-start.17 = (f32[128]{0:T(128)S(1)}, f32[128]{0:T(128)}, u32[]{:S(2)}) copy-start(f32[128]{0:T(128)} %param.18) | copy-start | bytes 1540
  0.7 4.1 %copy-start.20 = (bf16[128,128]{1,0:T(8,128)(2,1)S(1)}, bf16[128,128]{1,0:T(8,128)(2,1)}, u32[]{:S(2)}) copy-start(bf16[128,128]{1,0:T(8,128)(2,1)} %param.17) | copy-start | bytes 98308
  4.6 2.2 %copy-start.2 = (bf16[4096,128]{1,0:T(8,128)(2,1)}, bf16[4096,128]{1,0:T(8,128)(2,1)S(1)}, u32[]{:S(2)}) copy-start(bf16[4096,128]{1,0:T(8,128)(2,1)S(1)} %get-tuple-element.26) | copy-start | bytes 3145732
  4.8 2.0 %copy-start.8 = (f32[3,4096]{1,0:T(4,128)S(1)}, f32[3,4096]{1,0:T(4,128)}, u32[]{:S(2)}) copy-start(f32[3,4096]{1,0:T(4,128)} %param.14) | copy-start | bytes 147460
  4.8 2.2 %copy-start.13 = (s32[32,256]{1,0:T(8,128)S(1)}, s32[32,256]{1,0:T(8,128)}, u32[]{:S(2)}) copy-start(s32[32,256]{1,0:T(8,128)} %param.23) | copy-start | bytes 98308
  4.9 3.6 %copy-start.14 = (s32[32,256]{1,0:T(8,128)S(1)}, s32[32,256]{1,0:T(8,128)}, u32[]{:S(2)}) copy-start(s32[32,256]{1,0:T(8,128)} %param.24) | copy-start | bytes 98308
  6.8 19.8 %copy-start.6 = (f32[98,16,16]{0,2,1:T(8,128)S(1)}, f32[98,16,16]{0,2,1:T(8,128)}, u32[]{:S(2)}) copy-start(f32[98,16,16]{0,2,1:T(8,128)} %param.20) | copy-start | bytes 301060
  8.4 20.0 %copy-start.19 = (s32[125]{0:T(128)S(1)}, s32[125]{0:T(128)}, u32[]{:S(2)}) copy-start(s32[125]{0:T(128)} %constant.75) | copy-start | bytes 1504
  16.4 22.3 %all-to-all-start = ((f32[5,32,256]{2,0,1:T(8,128)}), f32[5,32,256]{2,0,1:T(8,128)S(1)}, u32[]{:S(2)}, u32[]{:S(2)}) async-start(f32[5,32,256]{2,0,1:T(8,128)} %bitcast.188), calls=%async_computation | async-start | bytes 524288 | tf_op jit(solution)/shard_map/all_to_all | solution.py:407
  27.3 0.6 copy-start.11
  27.9 0.6 copy-start.9
  29.2 21.6 %copy-start.16 = (f32[64,16]{0,1:T(8,128)S(1)}, f32[64,16]{0,1:T(8,128)}, u32[]{:S(2)}) copy-start(f32[64,16]{0,1:T(8,128)} %param.22) | copy-start | bytes 12292
  38.7 0.7 copy-start.1
  49.3 13.4 %copy-start.10 = (pred[5,8,4]{1,2,0:T(4,128)(4,1)S(1)}, pred[5,8,4]{1,2,0:T(4,128)(4,1)}, u32[]{:S(2)}) copy-start(pred[5,8,4]{1,2,0:T(4,128)(4,1)} %copy-done.9) | copy-start | bytes 484
  49.3 20.2 %copy-start.12 = (pred[5,64,64]{2,1,0:T(8,128)(4,1)S(1)}, pred[5,64,64]{2,1,0:T(8,128)(4,1)}, u32[]{:S(2)}) copy-start(pred[5,64,64]{2,1,0:T(8,128)(4,1)} %copy-done.11) | copy-start | bytes 61444
  51.4 4.4 %collective-permute-start.1 = (f32[16,2,4,64]{3,0,2,1:T(8,128)S(1)}, f32[16,2,4,64]{3,0,2,1:T(8,128)S(1)}, u32[]{:S(2)}, u32[]{:S(2)}) collective-permute-start(f32[16,2,4,64]{3,0,2,1:T(8,128)S(1)} %get-tuple-element.20), channel_id=1, source_target_pairs={{32,0},{64,32},{96,64},{128,96},{160,128},{192,160},{224,192},{256... | collective-permute-start | bytes 98312 | tf_op jit(solution)/shard_map/ppermute | solution.py:35
  52.7 3.9 %collective-permute-start = (f32[16,2,4,64]{3,0,2,1:T(8,128)S(1)}, f32[16,2,4,64]{3,0,2,1:T(8,128)S(1)}, u32[]{:S(2)}, u32[]{:S(2)}) collective-permute-start(f32[16,2,4,64]{3,0,2,1:T(8,128)S(1)} %get-tuple-element.19), channel_id=1, source_target_pairs={{0,32},{32,64},{64,96},{96,128},{128,160},{160,192},{192,224},{224... | collective-permute-start | bytes 98312 | tf_op jit(solution)/shard_map/ppermute | solution.py:33
  55.7 14.9 %copy-start.5 = (f32[25,16,16]{2,1,0:T(8,128)S(1)}, f32[25,16,16]{2,1,0:T(8,128)}, u32[]{:S(2)}) copy-start(f32[25,16,16]{2,1,0:T(8,128)} %get-tuple-element.11) | copy-start | bytes 76804
  56.7 6.9 %collective-permute-start.3 = (f32[16,8,2,64]{3,0,2,1:T(8,128)S(1)}, f32[16,8,2,64]{3,0,2,1:T(8,128)S(1)}, u32[]{:S(2)}, u32[]{:S(2)}) collective-permute-start(f32[16,8,2,64]{3,0,2,1:T(8,128)S(1)} %get-tuple-element.16), channel_id=1, source_target_pairs={{1,0},{2,1},{3,2},{4,3},{5,4},{6,5},{7,6},{8,7},{9,8},{10,9},{11,1... | collective-permute-start | bytes 196616 | tf_op jit(solution)/shard_map/ppermute | solution.py:35
  60.3 9.2 %collective-permute-start.2 = (f32[16,8,2,64]{3,0,2,1:T(8,128)S(1)}, f32[16,8,2,64]{3,0,2,1:T(8,128)S(1)}, u32[]{:S(2)}, u32[]{:S(2)}) collective-permute-start(f32[16,8,2,64]{3,0,2,1:T(8,128)S(1)} %get-tuple-element.15), channel_id=1, source_target_pairs={{0,1},{1,2},{2,3},{3,4},{4,5},{5,6},{6,7},{7,8},{8,9},{9,10},{10,1... | collective-permute-start | bytes 196616 | tf_op jit(solution)/shard_map/ppermute | solution.py:33
  70.7 1.3 copy-start.4
  79.3 3.5 %copy-start.15 = (f32[64,16]{0,1:T(8,128)S(1)}, f32[64,16]{0,1:T(8,128)}, u32[]{:S(2)}) copy-start(f32[64,16]{0,1:T(8,128)} %param.21) | copy-start | bytes 12292
  81.4 31.8 %copy-start.23 = (s32[4096]{0:T(1024)S(1)}, s32[4096]{0:T(1024)}, u32[]{:S(2)}) copy-start(s32[4096]{0:T(1024)} %param.15) | copy-start | bytes 49156
  81.4 32.0 %copy-start.18 = (f32[128]{0:T(128)S(1)}, f32[128]{0:T(128)}, u32[]{:S(2)}) copy-start(f32[128]{0:T(128)} %param.18) | copy-start | bytes 1540
  84.0 31.8 %copy-start.3 = (bf16[4096,128]{1,0:T(8,128)(2,1)S(1)}, bf16[4096,128]{1,0:T(8,128)(2,1)}, u32[]{:S(2)}) copy-start(bf16[4096,128]{1,0:T(8,128)(2,1)} %copy-done.2) | copy-start | bytes 3145732
  113.1 3.3 %copy-start.7 = (f32[4096]{0:T(1024)}, f32[4096]{0:T(1024)S(1)}, u32[]{:S(2)}) copy-start(f32[4096]{0:T(1024)S(1)} %reshape.422) | copy-start | bytes 49156
  113.4 3.0 %copy-start.21 = (bf16[128,128]{1,0:T(8,128)(2,1)S(1)}, bf16[128,128]{1,0:T(8,128)(2,1)}, u32[]{:S(2)}) copy-start(bf16[128,128]{1,0:T(8,128)(2,1)} %param.17) | copy-start | bytes 98308
  119.1 3.2 %collective-permute-start.4 = (f32[32902]{0:T(1024)S(1)}, f32[32902]{0:T(1024)S(1)}, u32[]{:S(2)}, u32[]{:S(2)}) collective-permute-start(f32[32902]{0:T(1024)S(1)} %pad_maximum_fusion.3), channel_id=1, source_target_pairs={{0,32},{32,0},{1,33},{33,1},{2,34},{34,2},{3,35},{35,3},{4,36},{36... | collective-permute-start | bytes 394832 | tf_op jit(solution)/shard_map/ppermute | solution.py:101
  137.2 8.3 %collective-permute-start.5 = (f32[1029]{0:T(1024)S(1)}, f32[1029]{0:T(1024)S(1)}, u32[]{:S(2)}, u32[]{:S(2)}) collective-permute-start(f32[1029]{0:T(1024)S(1)} %reduce_sum.29), channel_id=1, source_target_pairs={{0,64},{64,0},{128,192},{192,128},{256,320},{320,256},{384,448},{4... | collective-permute-start | bytes 12356 | tf_op jit(solution)/shard_map/ppermute | solution.py:101
  145.6 8.7 %collective-permute-start.6 = (f32[1029]{0:T(1024)S(1)}, f32[1029]{0:T(1024)S(1)}, u32[]{:S(2)}, u32[]{:S(2)}) collective-permute-start(f32[1029]{0:T(1024)S(1)} %add.207), channel_id=1, source_target_pairs={{0,128},{64,192},{128,0},{192,64},{256,384},{320,448},{384,256},{4... | collective-permute-start | bytes 12356 | tf_op jit(solution)/shard_map/ppermute | solution.py:101
  154.2 10.9 %collective-permute-start.7 = (f32[1029]{0:T(1024)S(1)}, f32[1029]{0:T(1024)S(1)}, u32[]{:S(2)}, u32[]{:S(2)}) collective-permute-start(f32[1029]{0:T(1024)S(1)} %add.208), channel_id=1, source_target_pairs={{0,256},{64,320},{128,384},{192,448},{256,0},{320,64},{384,128},{4... | collective-permute-start | bytes 12356 | tf_op jit(solution)/shard_map/ppermute | solution.py:101

commit v6 on v5

--- a/solution.py
+++ b/solution.py
@@ -157,7 +157,7 @@
         )
 
 
-def atoms_to_slots(values, high, low, box, tile=1024):
+def atoms_to_slots(values, high, low, box, tile=2048):
     rows, count = values.shape
     side = int(round(math.sqrt(count)))
     table = pieces_bf16(values.reshape(rows * side, side), 0)
@@ -200,7 +200,7 @@
     )
 
 
-def slots_to_atoms(values, high, low, count, tile=1024):
+def slots_to_atoms(values, high, low, count, tile=2048):
     side = int(round(math.sqrt(count)))
     pieces = values.reshape(1, -1)
     slots = values.shape[0]
@@ -240,10 +240,15 @@
 
 def bf16_pieces_in_kernel(x):
     high = x.astype(jnp.bfloat16)
-    rest = x - high.astype(jnp.float32)
-    middle = rest.astype(jnp.bfloat16)
-    low = (rest - middle.astype(jnp.float32)).astype(jnp.bfloat16)
-    return jnp.concatenate([high, middle, low], axis=0)
+    low = (x - high.astype(jnp.float32)).astype(jnp.bfloat16)
+    return jnp.concatenate([high, low], axis=0)
+
+
+def split_two(x):
+    high = lax.reduce_precision(x, exponent_bits=8, mantissa_bits=7)
+    return jnp.concatenate(
+        [high.astype(jnp.bfloat16), (x - high).astype(jnp.bfloat16)], axis=0
+    )
 
 
 def box_sum_kernel(data_ref, out_ref):
@@ -262,16 +267,16 @@
     )
 
 
-def box_sum(data, boxes, tile=1024):
+def box_sum(data, boxes, tile=2048):
     rows, slots = data.shape
     parts = pl.pallas_call(
         box_sum_kernel,
         grid=(slots // tile,),
         in_specs=[pl.BlockSpec((rows, tile), lambda i: (0, i))],
-        out_specs=pl.BlockSpec((3 * NODES, boxes), lambda i: (0, 0)),
-        out_shape=jax.ShapeDtypeStruct((3 * NODES, boxes), jnp.float32),
+        out_specs=pl.BlockSpec((2 * NODES, boxes), lambda i: (0, 0)),
+        out_shape=jax.ShapeDtypeStruct((2 * NODES, boxes), jnp.float32),
     )(data)
-    return parts[:NODES] + parts[NODES : 2 * NODES] + parts[2 * NODES :]
+    return parts[:NODES] + parts[NODES:]
 
 
 def box_pick_kernel(table_ref, data_ref, out_ref):
@@ -280,13 +285,13 @@
     box = data_ref[4:5, :].astype(jnp.int32)
     hot = (lax.broadcasted_iota(jnp.int32, (boxes, tile), 0) == box).astype(jnp.bfloat16)
     parts = jnp.dot(table_ref[...], hot, preferred_element_type=jnp.float32)
-    picked = parts[:NODES] + parts[NODES : 2 * NODES] + parts[2 * NODES :]
+    picked = parts[:NODES] + parts[NODES:]
     out_ref[...] = jnp.sum(node_rows(data_ref, tile) * picked, axis=0, keepdims=True)
 
 
-def box_pick(table, data, tile=1024):
+def box_pick(table, data, tile=2048):
     rows, slots = data.shape
-    stacked = pieces_bf16(table, 0)
+    stacked = split_two(table)
     return pl.pallas_call(
         box_pick_kernel,
         grid=(slots // tile,),

time: 183 us -> 177 us (0.967)
  Pallas kernels: 29.1 us -> 24.4 us
where the time goes in v6:
time: 177 us; the launch traced here: 176 us
  starting transfers between devices  45.4 us (26%)
  blocking collectives  43.9 us (25%)
  Pallas kernels  24.4 us (14%)
  waiting for transfers between devices  22.4 us (13%)
  matrix products  22.2 us (13%)
  local copies, waits for them, and re-layouts  10 us (6%)
  other arithmetic  6.79 us (4%)
    ppermute x4, starting transfers between devices, swapped(): return lax.ppermute(x, axis, [(i, i ^ step) for i in range(count)])  24.9 us
    all_to_all x1, blocking collectives, shards(): lax.all_to_all(slot_potential, DEV, split_axis=0, concat_axis=0, tiled=True)  15.5 us
    all_to_all x1, blocking collectives, hybrid_sum(): lax.all_to_all(lines, plane, 0, 0, tiled=True).reshape(peers, -1)  14.5 us
    all_to_all x1, blocking collectives, hybrid_sum(): return lax.all_to_all(copies, plane, 0, 0, tiled=True).reshape(-1)[:length]  13.9 us
    all_to_all x1, starting transfers between devices, shards(): lax.all_to_all(outgoing, DEV, split_axis=1, concat_axis=1, tiled=True)  10.2 us
    pallas_call x1, Pallas kernels, box_sum(): pl.pallas_call(box_sum_kernel, grid=(slots // tile,), in_specs=[pl.BlockS...  8.85 us
    all_to_all x1, waiting for transfers between devices, shards(): lax.all_to_all(outgoing, DEV, split_axis=1, concat_axis=1, tiled=True)  8.62 us
    ppermute x2, waiting for transfers between devices, extended_2(): lax.ppermute(tail, axis, [(i, (i + 1) % count) for i in range(ends)])  6.84 us
  transfers between devices with their start and end apart: 9, of which 8 were waited for; matrix products, arithmetic and copies ran while one was open for 1% of the time, Pallas kernels for 0%

profile of v6, /device:TPU:8, one launch (start us, length us, event | category | flops | bytes accessed | tf_op | source)
XLA Modules:
  0.0 176.4 jit_solution(13409072856888190752)
XLA Ops:
  0.7 1.2 copy-done
  1.9 2.7 %multiply_convert_fusion.1 = (bf16[4096,128]{1,0:T(8,128)(2,1)S(1)}, f32[4096,128]{1,0:T(8,128)}) fusion(bf16[4096,128]{1,0:T(8,128)(2,1)S(1)} %copy-done, bf16[128,128]{1,0:T(8,128)(2,1)} %param.16), kind=kOutput, calls=%fused_computation.8 | convolution fusion | flops 136839168 | bytes 4227072 | tf_op jit(solution)/shard_map/dot_general | solution.py:395
  4.6 0.2 fusion.60
  4.9 2.0 %multiply_reduce_fusion.1 = (f32[4096]{0:T(1024)S(1)}, f32[4096,128]{1,0:T(8,128)}) fusion(f32[128]{0:T(128)S(1)} %copy-done.17, bf16[4096,128]{1,0:T(8,128)(2,1)S(1)} %get-tuple-element.25, bf16[128,128]{1,0:T(8,128)(2,1)S(1)} %copy-done.20), kind=kOutput, calls=%fused_computation.5 | convolution fusion | flops 137359360 | bytes 3195392 | tf_op jit(solution)/shard_map/dot_general | solution.py:397
  7.1 0.6 copy.78
  7.8 0.6 copy.79
  8.4 0.6 copy.80
  9.1 0.7 pad_maximum_fusion.2.table_ref
  9.8 5.6 %shard_map.164 = f32[5,8192]{1,0:T(8,128)} custom-call(bf16[768,64]{1,0:T(8,128)(2,1)} %pad_maximum_fusion.2.table_ref, s32[1,8192]{1,0:T(1,128)} %bitcast.196, s32[1,8192]{1,0:T(1,128)} %bitcast.198, s32[1,8192]{1,0:T(1,128)} %bitcast.200), custom_call_target="tpu_custom_call" | custom-call | tf_op jit(solution)/shard_map/pallas_call | solution.py:165
  15.4 10.2 %all-to-all-start = ((f32[5,32,256]{2,0,1:T(8,128)}), f32[5,32,256]{2,0,1:T(8,128)S(1)}, u32[]{:S(2)}, u32[]{:S(2)}) async-start(f32[5,32,256]{2,0,1:T(8,128)} %bitcast.188), calls=%async_computation | async-start | bytes 524288 | tf_op jit(solution)/shard_map/all_to_all | solution.py:412
  25.7 0.4 copy.44
  26.5 0.4 copy-done.11
  26.9 0.6 copy-done.9
  27.5 0.7 gather_fusion
  28.2 0.9 fusion.83
  29.1 8.6 %all-to-all-done = f32[5,32,256]{2,0,1:T(8,128)S(1)} async-done(((f32[5,32,256]{2,0,1:T(8,128)}), f32[5,32,256]{2,0,1:T(8,128)S(1)}, u32[]{:S(2)}, u32[]{:S(2)}) %all-to-all-start) | async-done | bytes 163872 | tf_op jit(solution)/shard_map/all_to_all | solution.py:412
  37.7 0.7 copy-done.1
  38.5 8.8 %shard_map.165 = f32[128,1024]{1,0:T(8,128)} custom-call(f32[5,8192]{1,0:T(8,128)} %bitcast.186), custom_call_target="tpu_custom_call" | custom-call | tf_op jit(solution)/shard_map/pallas_call | solution.py:272
  47.3 1.1 slice_add_fusion
  48.4 0.3 reshape.420
  48.7 0.5 convolution_bitcast_fusion.7
  49.3 1.3 collective-permute-start.1
  50.6 3.0 %collective-permute-start = (f32[16,2,4,64]{3,0,2,1:T(8,128)S(1)}, f32[16,2,4,64]{3,0,2,1:T(8,128)S(1)}, u32[]{:S(2)}, u32[]{:S(2)}) collective-permute-start(f32[16,2,4,64]{3,0,2,1:T(8,128)S(1)} %get-tuple-element.18), channel_id=1, source_target_pairs={{0,32},{32,64},{64,96},{96,128},{128,160},{160,192},{192,224},{224... | collective-permute-start | bytes 98312 | tf_op jit(solution)/shard_map/ppermute | solution.py:33
  53.6 0.8 collective-permute-done
  54.5 3.7 %collective-permute-start.3 = (f32[16,8,2,64]{3,0,2,1:T(8,128)S(1)}, f32[16,8,2,64]{3,0,2,1:T(8,128)S(1)}, u32[]{:S(2)}, u32[]{:S(2)}) collective-permute-start(f32[16,8,2,64]{3,0,2,1:T(8,128)S(1)} %get-tuple-element.15), channel_id=1, source_target_pairs={{1,0},{2,1},{3,2},{4,3},{5,4},{6,5},{7,6},{8,7},{9,8},{10,9},{11,1... | collective-permute-start | bytes 196616 | tf_op jit(solution)/shard_map/ppermute | solution.py:35
  58.2 2.4 %collective-permute-start.2 = (f32[16,8,2,64]{3,0,2,1:T(8,128)S(1)}, f32[16,8,2,64]{3,0,2,1:T(8,128)S(1)}, u32[]{:S(2)}, u32[]{:S(2)}) collective-permute-start(f32[16,8,2,64]{3,0,2,1:T(8,128)S(1)} %get-tuple-element.14), channel_id=1, source_target_pairs={{0,1},{1,2},{2,3},{3,4},{4,5},{5,6},{6,7},{7,8},{8,9},{9,10},{10,1... | collective-permute-start | bytes 196616 | tf_op jit(solution)/shard_map/ppermute | solution.py:33
  60.7 0.7 collective-permute-done.3
  61.4 6.0 %collective-permute-done.2 = f32[16,8,2,64]{3,0,2,1:T(8,128)S(1)} collective-permute-done((f32[16,8,2,64]{3,0,2,1:T(8,128)S(1)}, f32[16,8,2,64]{3,0,2,1:T(8,128)S(1)}, u32[]{:S(2)}, u32[]{:S(2)}) %collective-permute-start.2) | collective-permute-done | bytes 65568 | tf_op jit(solution)/shard_map/ppermute | solution.py:33
  67.4 1.2 convolution_bitcast_fusion
  68.6 1.3 convolution_bitcast_fusion.5
  69.9 1.3 convolution_bitcast_fusion.4
  71.2 1.3 convolution_bitcast_fusion.3
  72.5 1.3 convolution_bitcast_fusion.2
  73.8 1.3 convolution_bitcast_fusion.1
  75.2 1.0 fusion.13
  76.2 1.0 fusion.40
  77.2 1.0 fusion.37
  78.3 1.0 fusion.34
  79.3 1.2 fusion.31
  80.7 0.4 reduce-precision_convert_fusion
  81.1 0.7 pad_maximum_fusion.1.table_ref
  81.9 6.8 %shard_map.166 = f32[1,8192]{1,0:T(1,128)} custom-call(bf16[128,1024]{1,0:T(8,128)(2,1)} %pad_maximum_fusion.1.table_ref, f32[5,8192]{1,0:T(8,128)} %bitcast.187), custom_call_target="tpu_custom_call" | custom-call | tf_op jit(solution)/shard_map/pallas_call | solution.py:295
  88.7 15.5 %all_to_all.29 = f32[32,1,256]{2,1,0:T(1,128)} all-to-all(f32[32,1,256]{2,1,0:T(1,128)} %bitcast.201), channel_id=1, replica_groups=mesh['grp_0'=8,'grp_1'=2,'dev_0'=8,'dev_1'=4] {'dev_0','dev_1'}, dimensions={0} | all-to-all | bytes 65536 | tf_op jit(solution)/shard_map/all_to_all | solution.py:421
  104.2 3.2 %shard_map.167 = f32[192,64]{1,0:T(8,128)} custom-call(f32[1,8192]{1,0:T(1,128)} %bitcast.202, s32[1,8192]{1,0:T(1,128)} %bitcast.197, s32[1,8192]{1,0:T(1,128)} %bitcast.199), custom_call_target="tpu_custom_call" | custom-call | tf_op jit(solution)/shard_map/pallas_call | solution.py:207
  107.4 0.8 slice_add_fusion.1
  108.4 0.2 fusion.46
  108.6 2.4 %multiply_convert_fusion = (bf16[4096,128]{1,0:T(8,128)(2,1)S(1)}, f32[128]{0:T(128)S(1)}) fusion(f32[4096,128]{1,0:T(8,128)} %get-tuple-element.28, f32[4096]{0:T(1024)S(1)} %reshape.422, f32[128]{0:T(128)S(1)} %copy-done.18), kind=kLoop, calls=%fused_computation.4 | loop fusion | flops 6815616 | bytes 3163136 | tf_op jit(solution)/shard_map/convert_element_type | solution.py:425
  111.0 0.5 fusion.43
  111.5 2.6 %fusion.45 = f32[128,128]{0,1:T(8,128)S(1)} fusion(bf16[4096,128]{1,0:T(8,128)(2,1)S(1)} %copy-done, bf16[4096,128]{1,0:T(8,128)(2,1)S(1)} %get-tuple-element.5, bf16[128,128]{1,0:T(8,128)(2,1)S(1)} %copy-done.21, f32[4096,128]{1,0:T(8,128)} %get-tuple-element.26), kind=kOutput, calls=%fused_computation.47 | convolution fusion | flops 273170432 | bytes 4292608 | tf_op jit(solution)/shard_map/dot_general | solution.py:437
  114.3 1.9 %collective-permute-start.4 = (f32[32902]{0:T(1024)S(1)}, f32[32902]{0:T(1024)S(1)}, u32[]{:S(2)}, u32[]{:S(2)}) collective-permute-start(f32[32902]{0:T(1024)S(1)} %pad_maximum_fusion.3), channel_id=1, source_target_pairs={{0,32},{32,0},{1,33},{33,1},{2,34},{34,2},{3,35},{35,3},{4,36},{36... | collective-permute-start | bytes 394832 | tf_op jit(solution)/shard_map/ppermute | solution.py:101
  116.2 1.3 collective-permute-done.4
  117.6 0.2 all_to_all.22
  117.8 14.5 %all_to_all.30 = f32[32,1,1029]{2,1,0:T(1,128)S(1)} all-to-all(f32[32,1,1029]{2,1,0:T(1,128)S(1)} %all_to_all.22), channel_id=1, replica_groups=mesh['grp_0'=8,'grp_1'=2,'dev_0'=8,'dev_1'=4] {'dev_0','dev_1'}, dimensions={0} | all-to-all | bytes 263424 | tf_op jit(solution)/shard_map/all_to_all | solution.py:117
  132.4 6.7 %collective-permute-start.5 = (f32[1029]{0:T(1024)S(1)}, f32[1029]{0:T(1024)S(1)}, u32[]{:S(2)}, u32[]{:S(2)}) collective-permute-start(f32[1029]{0:T(1024)S(1)} %reduce_sum.29), channel_id=1, source_target_pairs={{0,64},{64,0},{128,192},{192,128},{256,320},{320,256},{384,448},{4... | collective-permute-start | bytes 12356 | tf_op jit(solution)/shard_map/ppermute | solution.py:101
  139.1 1.6 collective-permute-done.5
  140.7 7.1 %collective-permute-start.6 = (f32[1029]{0:T(1024)S(1)}, f32[1029]{0:T(1024)S(1)}, u32[]{:S(2)}, u32[]{:S(2)}) collective-permute-start(f32[1029]{0:T(1024)S(1)} %add.203), channel_id=1, source_target_pairs={{0,128},{64,192},{128,0},{192,64},{256,384},{320,448},{384,256},{4... | collective-permute-start | bytes 12356 | tf_op jit(solution)/shard_map/ppermute | solution.py:101
  147.8 1.6 collective-permute-done.6
  149.4 9.2 %collective-permute-start.7 = (f32[1029]{0:T(1024)S(1)}, f32[1029]{0:T(1024)S(1)}, u32[]{:S(2)}, u32[]{:S(2)}) collective-permute-start(f32[1029]{0:T(1024)S(1)} %add.204), channel_id=1, source_target_pairs={{0,256},{64,320},{128,384},{192,448},{256,0},{320,64},{384,128},{4... | collective-permute-start | bytes 12356 | tf_op jit(solution)/shard_map/ppermute | solution.py:101
  158.6 1.6 collective-permute-done.7
  160.3 13.9 %all_to_all.31 = f32[32,1,1029]{2,1,0:T(1,128)S(1)} all-to-all(f32[32,1,1029]{2,1,0:T(1,128)S(1)} %broadcast_in_dim.10), channel_id=1, replica_groups=mesh['grp_0'=8,'grp_1'=2,'dev_0'=8,'dev_1'=4] {'dev_0','dev_1'}, dimensions={0} | all-to-all | bytes 263424 | tf_op jit(solution)/shard_map/all_to_all | solution.py:120
  174.2 0.3 reduce.1
  174.7 0.7 slice_bitcast_fusion.10
  175.4 0.5 slice.125
  175.9 0.5 slice.126
  (89 shorter events, 1.7 us)
Async XLA Ops:
  0.6 1.2 copy-start
  0.6 4.0 %copy-start.22 = (s32[4096]{0:T(1024)S(1)}, s32[4096]{0:T(1024)}, u32[]{:S(2)}) copy-start(s32[4096]{0:T(1024)} %param.15) | copy-start | bytes 49156
  0.7 3.9 %copy-start.24 = (f32[6]{0:T(128)S(1)}, f32[6]{0:T(128)}, u32[]{:S(2)}) copy-start(f32[6]{0:T(128)} %param.19) | copy-start | bytes 76
  0.7 4.1 %copy-start.17 = (f32[128]{0:T(128)S(1)}, f32[128]{0:T(128)}, u32[]{:S(2)}) copy-start(f32[128]{0:T(128)} %param.18) | copy-start | bytes 1540
  0.7 4.1 %copy-start.20 = (bf16[128,128]{1,0:T(8,128)(2,1)S(1)}, bf16[128,128]{1,0:T(8,128)(2,1)}, u32[]{:S(2)}) copy-start(bf16[128,128]{1,0:T(8,128)(2,1)} %param.17) | copy-start | bytes 98308
  4.6 2.2 %copy-start.2 = (bf16[4096,128]{1,0:T(8,128)(2,1)}, bf16[4096,128]{1,0:T(8,128)(2,1)S(1)}, u32[]{:S(2)}) copy-start(bf16[4096,128]{1,0:T(8,128)(2,1)S(1)} %get-tuple-element.25) | copy-start | bytes 3145732
  4.8 2.0 %copy-start.8 = (f32[3,4096]{1,0:T(4,128)S(1)}, f32[3,4096]{1,0:T(4,128)}, u32[]{:S(2)}) copy-start(f32[3,4096]{1,0:T(4,128)} %param.14) | copy-start | bytes 147460
  4.8 2.2 %copy-start.13 = (s32[32,256]{1,0:T(8,128)S(1)}, s32[32,256]{1,0:T(8,128)}, u32[]{:S(2)}) copy-start(s32[32,256]{1,0:T(8,128)} %param.23) | copy-start | bytes 98308
  4.9 3.6 %copy-start.14 = (s32[32,256]{1,0:T(8,128)S(1)}, s32[32,256]{1,0:T(8,128)}, u32[]{:S(2)}) copy-start(s32[32,256]{1,0:T(8,128)} %param.24) | copy-start | bytes 98308
  6.8 18.8 %copy-start.6 = (f32[98,16,16]{0,2,1:T(8,128)S(1)}, f32[98,16,16]{0,2,1:T(8,128)}, u32[]{:S(2)}) copy-start(f32[98,16,16]{0,2,1:T(8,128)} %param.20) | copy-start | bytes 301060
  8.4 19.0 %copy-start.19 = (s32[125]{0:T(128)S(1)}, s32[125]{0:T(128)}, u32[]{:S(2)}) copy-start(s32[125]{0:T(128)} %constant.75) | copy-start | bytes 1504
  15.4 22.3 %all-to-all-start = ((f32[5,32,256]{2,0,1:T(8,128)}), f32[5,32,256]{2,0,1:T(8,128)S(1)}, u32[]{:S(2)}, u32[]{:S(2)}) async-start(f32[5,32,256]{2,0,1:T(8,128)} %bitcast.188), calls=%async_computation | async-start | bytes 524288 | tf_op jit(solution)/shard_map/all_to_all | solution.py:412
  26.2 0.6 copy-start.11
  26.9 0.6 copy-start.9
  28.2 20.5 %copy-start.15 = (f32[64,16]{0,1:T(8,128)S(1)}, f32[64,16]{0,1:T(8,128)}, u32[]{:S(2)}) copy-start(f32[64,16]{0,1:T(8,128)} %param.22) | copy-start | bytes 12292
  37.7 0.7 copy-start.1
  38.4 22.1 %copy-start.10 = (pred[5,8,4]{1,2,0:T(4,128)(4,1)S(1)}, pred[5,8,4]{1,2,0:T(4,128)(4,1)}, u32[]{:S(2)}) copy-start(pred[5,8,4]{1,2,0:T(4,128)(4,1)} %copy-done.9) | copy-start | bytes 484
  38.4 28.9 %copy-start.12 = (pred[5,64,64]{2,1,0:T(8,128)(4,1)S(1)}, pred[5,64,64]{2,1,0:T(8,128)(4,1)}, u32[]{:S(2)}) copy-start(pred[5,64,64]{2,1,0:T(8,128)(4,1)} %copy-done.11) | copy-start | bytes 61444
  49.3 4.4 %collective-permute-start.1 = (f32[16,2,4,64]{3,0,2,1:T(8,128)S(1)}, f32[16,2,4,64]{3,0,2,1:T(8,128)S(1)}, u32[]{:S(2)}, u32[]{:S(2)}) collective-permute-start(f32[16,2,4,64]{3,0,2,1:T(8,128)S(1)} %get-tuple-element.19), channel_id=1, source_target_pairs={{32,0},{64,32},{96,64},{128,96},{160,128},{192,160},{224,192},{256... | collective-permute-start | bytes 98312 | tf_op jit(solution)/shard_map/ppermute | solution.py:35
  50.6 3.9 %collective-permute-start = (f32[16,2,4,64]{3,0,2,1:T(8,128)S(1)}, f32[16,2,4,64]{3,0,2,1:T(8,128)S(1)}, u32[]{:S(2)}, u32[]{:S(2)}) collective-permute-start(f32[16,2,4,64]{3,0,2,1:T(8,128)S(1)} %get-tuple-element.18), channel_id=1, source_target_pairs={{0,32},{32,64},{64,96},{96,128},{128,160},{160,192},{192,224},{224... | collective-permute-start | bytes 98312 | tf_op jit(solution)/shard_map/ppermute | solution.py:33
  53.6 15.0 %copy-start.5 = (f32[25,16,16]{2,1,0:T(8,128)S(1)}, f32[25,16,16]{2,1,0:T(8,128)}, u32[]{:S(2)}) copy-start(f32[25,16,16]{2,1,0:T(8,128)} %get-tuple-element.11) | copy-start | bytes 76804
  54.5 6.9 %collective-permute-start.3 = (f32[16,8,2,64]{3,0,2,1:T(8,128)S(1)}, f32[16,8,2,64]{3,0,2,1:T(8,128)S(1)}, u32[]{:S(2)}, u32[]{:S(2)}) collective-permute-start(f32[16,8,2,64]{3,0,2,1:T(8,128)S(1)} %get-tuple-element.15), channel_id=1, source_target_pairs={{1,0},{2,1},{3,2},{4,3},{5,4},{6,5},{7,6},{8,7},{9,8},{10,9},{11,1... | collective-permute-start | bytes 196616 | tf_op jit(solution)/shard_map/ppermute | solution.py:35
  58.2 9.2 %collective-permute-start.2 = (f32[16,8,2,64]{3,0,2,1:T(8,128)S(1)}, f32[16,8,2,64]{3,0,2,1:T(8,128)S(1)}, u32[]{:S(2)}, u32[]{:S(2)}) collective-permute-start(f32[16,8,2,64]{3,0,2,1:T(8,128)S(1)} %get-tuple-element.14), channel_id=1, source_target_pairs={{0,1},{1,2},{2,3},{3,4},{4,5},{5,6},{6,7},{7,8},{8,9},{9,10},{10,1... | collective-permute-start | bytes 196616 | tf_op jit(solution)/shard_map/ppermute | solution.py:33
  68.6 1.3 copy-start.4
  77.2 3.5 %copy-start.16 = (f32[64,16]{0,1:T(8,128)S(1)}, f32[64,16]{0,1:T(8,128)}, u32[]{:S(2)}) copy-start(f32[64,16]{0,1:T(8,128)} %param.21) | copy-start | bytes 12292
  79.3 29.1 %copy-start.23 = (s32[4096]{0:T(1024)S(1)}, s32[4096]{0:T(1024)}, u32[]{:S(2)}) copy-start(s32[4096]{0:T(1024)} %param.15) | copy-start | bytes 49156
  79.3 29.3 %copy-start.18 = (f32[128]{0:T(128)S(1)}, f32[128]{0:T(128)}, u32[]{:S(2)}) copy-start(f32[128]{0:T(128)} %param.18) | copy-start | bytes 1540
  81.9 29.2 %copy-start.3 = (bf16[4096,128]{1,0:T(8,128)(2,1)S(1)}, bf16[4096,128]{1,0:T(8,128)(2,1)}, u32[]{:S(2)}) copy-start(bf16[4096,128]{1,0:T(8,128)(2,1)} %copy-done.2) | copy-start | bytes 3145732
  108.3 3.3 %copy-start.7 = (f32[4096]{0:T(1024)}, f32[4096]{0:T(1024)S(1)}, u32[]{:S(2)}) copy-start(f32[4096]{0:T(1024)S(1)} %reshape.422) | copy-start | bytes 49156
  108.6 3.0 %copy-start.21 = (bf16[128,128]{1,0:T(8,128)(2,1)S(1)}, bf16[128,128]{1,0:T(8,128)(2,1)}, u32[]{:S(2)}) copy-start(bf16[128,128]{1,0:T(8,128)(2,1)} %param.17) | copy-start | bytes 98308
  114.3 3.2 %collective-permute-start.4 = (f32[32902]{0:T(1024)S(1)}, f32[32902]{0:T(1024)S(1)}, u32[]{:S(2)}, u32[]{:S(2)}) collective-permute-start(f32[32902]{0:T(1024)S(1)} %pad_maximum_fusion.3), channel_id=1, source_target_pairs={{0,32},{32,0},{1,33},{33,1},{2,34},{34,2},{3,35},{35,3},{4,36},{36... | collective-permute-start | bytes 394832 | tf_op jit(solution)/shard_map/ppermute | solution.py:101
  132.4 8.3 %collective-permute-start.5 = (f32[1029]{0:T(1024)S(1)}, f32[1029]{0:T(1024)S(1)}, u32[]{:S(2)}, u32[]{:S(2)}) collective-permute-start(f32[1029]{0:T(1024)S(1)} %reduce_sum.29), channel_id=1, source_target_pairs={{0,64},{64,0},{128,192},{192,128},{256,320},{320,256},{384,448},{4... | collective-permute-start | bytes 12356 | tf_op jit(solution)/shard_map/ppermute | solution.py:101
  140.7 8.7 %collective-permute-start.6 = (f32[1029]{0:T(1024)S(1)}, f32[1029]{0:T(1024)S(1)}, u32[]{:S(2)}, u32[]{:S(2)}) collective-permute-start(f32[1029]{0:T(1024)S(1)} %add.203), channel_id=1, source_target_pairs={{0,128},{64,192},{128,0},{192,64},{256,384},{320,448},{384,256},{4... | collective-permute-start | bytes 12356 | tf_op jit(solution)/shard_map/ppermute | solution.py:101
  149.4 10.9 %collective-permute-start.7 = (f32[1029]{0:T(1024)S(1)}, f32[1029]{0:T(1024)S(1)}, u32[]{:S(2)}, u32[]{:S(2)}) collective-permute-start(f32[1029]{0:T(1024)S(1)} %add.204), channel_id=1, source_target_pairs={{0,256},{64,320},{128,384},{192,448},{256,0},{320,64},{384,128},{4... | collective-permute-start | bytes 12356 | tf_op jit(solution)/shard_map/ppermute | solution.py:101

commit v7 on v6

--- a/solution.py
+++ b/solution.py
@@ -157,7 +157,7 @@
         )
 
 
-def atoms_to_slots(values, high, low, box, tile=2048):
+def atoms_to_slots(values, high, low, box, tile=4096):
     rows, count = values.shape
     side = int(round(math.sqrt(count)))
     table = pieces_bf16(values.reshape(rows * side, side), 0)
@@ -200,7 +200,7 @@
     )
 
 
-def slots_to_atoms(values, high, low, count, tile=2048):
+def slots_to_atoms(values, high, low, count, tile=8192):
     side = int(round(math.sqrt(count)))
     pieces = values.reshape(1, -1)
     slots = values.shape[0]
@@ -267,7 +267,7 @@
     )
 
 
-def box_sum(data, boxes, tile=2048):
+def box_sum(data, boxes, tile=4096):
     rows, slots = data.shape
     parts = pl.pallas_call(
         box_sum_kernel,
@@ -289,7 +289,7 @@
     out_ref[...] = jnp.sum(node_rows(data_ref, tile) * picked, axis=0, keepdims=True)
 
 
-def box_pick(table, data, tile=2048):
+def box_pick(table, data, tile=4096):
     rows, slots = data.shape
     stacked = split_two(table)
     return pl.pallas_call(

time: 177 us -> 176 us (level)
  no operation moved by 1% of the time
where the time goes in v7:
time: 176 us; the launch traced here: 175 us
  starting transfers between devices  45.4 us (26%)
  blocking collectives  43.8 us (25%)
  Pallas kernels  23 us (13%)
  waiting for transfers between devices  22.4 us (13%)
  matrix products  22.2 us (13%)
  local copies, waits for them, and re-layouts  10 us (6%)
  other arithmetic  6.79 us (4%)
    ppermute x4, starting transfers between devices, swapped(): return lax.ppermute(x, axis, [(i, i ^ step) for i in range(count)])  24.9 us
    all_to_all x1, blocking collectives, shards(): lax.all_to_all(slot_potential, DEV, split_axis=0, concat_axis=0, tiled=True)  15.5 us
    all_to_all x1, blocking collectives, hybrid_sum(): lax.all_to_all(lines, plane, 0, 0, tiled=True).reshape(peers, -1)  14.4 us
    all_to_all x1, blocking collectives, hybrid_sum(): return lax.all_to_all(copies, plane, 0, 0, tiled=True).reshape(-1)[:length]  13.9 us
    all_to_all x1, starting transfers between devices, shards(): lax.all_to_all(outgoing, DEV, split_axis=1, concat_axis=1, tiled=True)  10.2 us
    all_to_all x1, waiting for transfers between devices, shards(): lax.all_to_all(outgoing, DEV, split_axis=1, concat_axis=1, tiled=True)  8.63 us
    pallas_call x1, Pallas kernels, box_sum(): pl.pallas_call(box_sum_kernel, grid=(slots // tile,), in_specs=[pl.BlockS...  8.61 us
    ppermute x2, waiting for transfers between devices, extended_2(): lax.ppermute(tail, axis, [(i, (i + 1) % count) for i in range(ends)])  6.84 us
  transfers between devices with their start and end apart: 9, of which 8 were waited for; matrix products, arithmetic and copies ran while one was open for 1% of the time, Pallas kernels for 0%

profile of v7, /device:TPU:8, one launch (start us, length us, event | category | flops | bytes accessed | tf_op | source)
XLA Modules:
  0.0 175.0 jit_solution(7427572873571090007)
XLA Ops:
  0.7 1.2 copy-done
  1.9 2.7 %multiply_convert_fusion.1 = (bf16[4096,128]{1,0:T(8,128)(2,1)S(1)}, f32[4096,128]{1,0:T(8,128)}) fusion(bf16[4096,128]{1,0:T(8,128)(2,1)S(1)} %copy-done, bf16[128,128]{1,0:T(8,128)(2,1)} %param.16), kind=kOutput, calls=%fused_computation.8 | convolution fusion | flops 136839168 | bytes 4227072 | tf_op jit(solution)/shard_map/dot_general | solution.py:395
  4.6 0.2 fusion.60
  4.9 2.0 %multiply_reduce_fusion.1 = (f32[4096]{0:T(1024)S(1)}, f32[4096,128]{1,0:T(8,128)}) fusion(f32[128]{0:T(128)S(1)} %copy-done.17, bf16[4096,128]{1,0:T(8,128)(2,1)S(1)} %get-tuple-element.25, bf16[128,128]{1,0:T(8,128)(2,1)S(1)} %copy-done.20), kind=kOutput, calls=%fused_computation.5 | convolution fusion | flops 137359360 | bytes 3195392 | tf_op jit(solution)/shard_map/dot_general | solution.py:397
  7.1 0.6 copy.78
  7.8 0.6 copy.79
  8.4 0.6 copy.80
  9.1 0.7 pad_maximum_fusion.2.table_ref
  9.8 5.3 %shard_map.164 = f32[5,8192]{1,0:T(8,128)} custom-call(bf16[768,64]{1,0:T(8,128)(2,1)} %pad_maximum_fusion.2.table_ref, s32[1,8192]{1,0:T(1,128)} %bitcast.196, s32[1,8192]{1,0:T(1,128)} %bitcast.198, s32[1,8192]{1,0:T(1,128)} %bitcast.200), custom_call_target="tpu_custom_call" | custom-call | tf_op jit(solution)/shard_map/pallas_call | solution.py:165
  15.1 10.2 %all-to-all-start = ((f32[5,32,256]{2,0,1:T(8,128)}), f32[5,32,256]{2,0,1:T(8,128)S(1)}, u32[]{:S(2)}, u32[]{:S(2)}) async-start(f32[5,32,256]{2,0,1:T(8,128)} %bitcast.188), calls=%async_computation | async-start | bytes 524288 | tf_op jit(solution)/shard_map/all_to_all | solution.py:412
  25.3 0.4 copy.44
  26.2 0.4 copy-done.11
  26.5 0.6 copy-done.9
  27.1 0.7 gather_fusion
  27.9 0.9 fusion.83
  28.8 8.6 %all-to-all-done = f32[5,32,256]{2,0,1:T(8,128)S(1)} async-done(((f32[5,32,256]{2,0,1:T(8,128)}), f32[5,32,256]{2,0,1:T(8,128)S(1)}, u32[]{:S(2)}, u32[]{:S(2)}) %all-to-all-start) | async-done | bytes 163872 | tf_op jit(solution)/shard_map/all_to_all | solution.py:412
  37.4 0.7 copy-done.1
  38.1 8.6 %shard_map.165 = f32[128,1024]{1,0:T(8,128)} custom-call(f32[5,8192]{1,0:T(8,128)} %bitcast.186), custom_call_target="tpu_custom_call" | custom-call | tf_op jit(solution)/shard_map/pallas_call | solution.py:272
  46.7 1.1 slice_add_fusion
  47.8 0.3 reshape.420
  48.1 0.5 convolution_bitcast_fusion.7
  48.7 1.3 collective-permute-start.1
  50.0 3.0 %collective-permute-start = (f32[16,2,4,64]{3,0,2,1:T(8,128)S(1)}, f32[16,2,4,64]{3,0,2,1:T(8,128)S(1)}, u32[]{:S(2)}, u32[]{:S(2)}) collective-permute-start(f32[16,2,4,64]{3,0,2,1:T(8,128)S(1)} %get-tuple-element.18), channel_id=1, source_target_pairs={{0,32},{32,64},{64,96},{96,128},{128,160},{160,192},{192,224},{224... | collective-permute-start | bytes 98312 | tf_op jit(solution)/shard_map/ppermute | solution.py:33
  53.1 0.8 collective-permute-done
  54.0 3.7 %collective-permute-start.3 = (f32[16,8,2,64]{3,0,2,1:T(8,128)S(1)}, f32[16,8,2,64]{3,0,2,1:T(8,128)S(1)}, u32[]{:S(2)}, u32[]{:S(2)}) collective-permute-start(f32[16,8,2,64]{3,0,2,1:T(8,128)S(1)} %get-tuple-element.15), channel_id=1, source_target_pairs={{1,0},{2,1},{3,2},{4,3},{5,4},{6,5},{7,6},{8,7},{9,8},{10,9},{11,1... | collective-permute-start | bytes 196616 | tf_op jit(solution)/shard_map/ppermute | solution.py:35
  57.6 2.4 %collective-permute-start.2 = (f32[16,8,2,64]{3,0,2,1:T(8,128)S(1)}, f32[16,8,2,64]{3,0,2,1:T(8,128)S(1)}, u32[]{:S(2)}, u32[]{:S(2)}) collective-permute-start(f32[16,8,2,64]{3,0,2,1:T(8,128)S(1)} %get-tuple-element.14), channel_id=1, source_target_pairs={{0,1},{1,2},{2,3},{3,4},{4,5},{5,6},{6,7},{7,8},{8,9},{9,10},{10,1... | collective-permute-start | bytes 196616 | tf_op jit(solution)/shard_map/ppermute | solution.py:33
  60.1 0.7 collective-permute-done.3
  60.8 6.0 %collective-permute-done.2 = f32[16,8,2,64]{3,0,2,1:T(8,128)S(1)} collective-permute-done((f32[16,8,2,64]{3,0,2,1:T(8,128)S(1)}, f32[16,8,2,64]{3,0,2,1:T(8,128)S(1)}, u32[]{:S(2)}, u32[]{:S(2)}) %collective-permute-start.2) | collective-permute-done | bytes 65568 | tf_op jit(solution)/shard_map/ppermute | solution.py:33
  66.8 1.2 convolution_bitcast_fusion
  68.0 1.3 convolution_bitcast_fusion.5
  69.3 1.3 convolution_bitcast_fusion.4
  70.6 1.3 convolution_bitcast_fusion.3
  72.0 1.3 convolution_bitcast_fusion.2
  73.3 1.3 convolution_bitcast_fusion.1
  74.6 1.0 fusion.13
  75.6 1.0 fusion.40
  76.7 1.0 fusion.37
  77.7 1.0 fusion.34
  78.7 1.2 fusion.31
  80.1 0.4 reduce-precision_convert_fusion
  80.6 0.7 pad_maximum_fusion.1.table_ref
  81.3 6.7 %shard_map.166 = f32[1,8192]{1,0:T(1,128)} custom-call(bf16[128,1024]{1,0:T(8,128)(2,1)} %pad_maximum_fusion.1.table_ref, f32[5,8192]{1,0:T(8,128)} %bitcast.187), custom_call_target="tpu_custom_call" | custom-call | tf_op jit(solution)/shard_map/pallas_call | solution.py:295
  88.0 15.5 %all_to_all.29 = f32[32,1,256]{2,1,0:T(1,128)} all-to-all(f32[32,1,256]{2,1,0:T(1,128)} %bitcast.201), channel_id=1, replica_groups=mesh['grp_0'=8,'grp_1'=2,'dev_0'=8,'dev_1'=4] {'dev_0','dev_1'}, dimensions={0} | all-to-all | bytes 65536 | tf_op jit(solution)/shard_map/all_to_all | solution.py:421
  103.5 2.4 %shard_map.167 = f32[192,64]{1,0:T(8,128)} custom-call(f32[1,8192]{1,0:T(1,128)} %bitcast.202, s32[1,8192]{1,0:T(1,128)} %bitcast.197, s32[1,8192]{1,0:T(1,128)} %bitcast.199), custom_call_target="tpu_custom_call" | custom-call | tf_op jit(solution)/shard_map/pallas_call | solution.py:207
  106.0 0.8 slice_add_fusion.1
  106.9 0.2 fusion.46
  107.2 2.4 %multiply_convert_fusion = (bf16[4096,128]{1,0:T(8,128)(2,1)S(1)}, f32[128]{0:T(128)S(1)}) fusion(f32[4096,128]{1,0:T(8,128)} %get-tuple-element.28, f32[4096]{0:T(1024)S(1)} %reshape.422, f32[128]{0:T(128)S(1)} %copy-done.18), kind=kLoop, calls=%fused_computation.4 | loop fusion | flops 6815616 | bytes 3163136 | tf_op jit(solution)/shard_map/convert_element_type | solution.py:425
  109.6 0.5 fusion.43
  110.1 2.6 %fusion.45 = f32[128,128]{0,1:T(8,128)S(1)} fusion(bf16[4096,128]{1,0:T(8,128)(2,1)S(1)} %copy-done, bf16[4096,128]{1,0:T(8,128)(2,1)S(1)} %get-tuple-element.5, bf16[128,128]{1,0:T(8,128)(2,1)S(1)} %copy-done.21, f32[4096,128]{1,0:T(8,128)} %get-tuple-element.26), kind=kOutput, calls=%fused_computation.47 | convolution fusion | flops 273170432 | bytes 4292608 | tf_op jit(solution)/shard_map/dot_general | solution.py:437
  112.9 1.9 %collective-permute-start.4 = (f32[32902]{0:T(1024)S(1)}, f32[32902]{0:T(1024)S(1)}, u32[]{:S(2)}, u32[]{:S(2)}) collective-permute-start(f32[32902]{0:T(1024)S(1)} %pad_maximum_fusion.3), channel_id=1, source_target_pairs={{0,32},{32,0},{1,33},{33,1},{2,34},{34,2},{3,35},{35,3},{4,36},{36... | collective-permute-start | bytes 394832 | tf_op jit(solution)/shard_map/ppermute | solution.py:101
  114.8 1.3 collective-permute-done.4
  116.2 0.2 all_to_all.22
  116.4 14.4 %all_to_all.30 = f32[32,1,1029]{2,1,0:T(1,128)S(1)} all-to-all(f32[32,1,1029]{2,1,0:T(1,128)S(1)} %all_to_all.22), channel_id=1, replica_groups=mesh['grp_0'=8,'grp_1'=2,'dev_0'=8,'dev_1'=4] {'dev_0','dev_1'}, dimensions={0} | all-to-all | bytes 263424 | tf_op jit(solution)/shard_map/all_to_all | solution.py:117
  131.0 6.7 %collective-permute-start.5 = (f32[1029]{0:T(1024)S(1)}, f32[1029]{0:T(1024)S(1)}, u32[]{:S(2)}, u32[]{:S(2)}) collective-permute-start(f32[1029]{0:T(1024)S(1)} %reduce_sum.29), channel_id=1, source_target_pairs={{0,64},{64,0},{128,192},{192,128},{256,320},{320,256},{384,448},{4... | collective-permute-start | bytes 12356 | tf_op jit(solution)/shard_map/ppermute | solution.py:101
  137.7 1.6 collective-permute-done.5
  139.3 7.1 %collective-permute-start.6 = (f32[1029]{0:T(1024)S(1)}, f32[1029]{0:T(1024)S(1)}, u32[]{:S(2)}, u32[]{:S(2)}) collective-permute-start(f32[1029]{0:T(1024)S(1)} %add.203), channel_id=1, source_target_pairs={{0,128},{64,192},{128,0},{192,64},{256,384},{320,448},{384,256},{4... | collective-permute-start | bytes 12356 | tf_op jit(solution)/shard_map/ppermute | solution.py:101
  146.3 1.6 collective-permute-done.6
  148.0 9.3 %collective-permute-start.7 = (f32[1029]{0:T(1024)S(1)}, f32[1029]{0:T(1024)S(1)}, u32[]{:S(2)}, u32[]{:S(2)}) collective-permute-start(f32[1029]{0:T(1024)S(1)} %add.204), channel_id=1, source_target_pairs={{0,256},{64,320},{128,384},{192,448},{256,0},{320,64},{384,128},{4... | collective-permute-start | bytes 12356 | tf_op jit(solution)/shard_map/ppermute | solution.py:101
  157.2 1.6 collective-permute-done.7
  158.9 13.9 %all_to_all.31 = f32[32,1,1029]{2,1,0:T(1,128)S(1)} all-to-all(f32[32,1,1029]{2,1,0:T(1,128)S(1)} %broadcast_in_dim.10), channel_id=1, replica_groups=mesh['grp_0'=8,'grp_1'=2,'dev_0'=8,'dev_1'=4] {'dev_0','dev_1'}, dimensions={0} | all-to-all | bytes 263424 | tf_op jit(solution)/shard_map/all_to_all | solution.py:120
  172.8 0.3 reduce.1
  173.3 0.7 slice_bitcast_fusion.10
  174.0 0.5 slice.125
  174.5 0.5 slice.126
  (89 shorter events, 1.7 us)
Async XLA Ops:
  0.6 1.2 copy-start
  0.6 4.0 %copy-start.22 = (s32[4096]{0:T(1024)S(1)}, s32[4096]{0:T(1024)}, u32[]{:S(2)}) copy-start(s32[4096]{0:T(1024)} %param.15) | copy-start | bytes 49156
  0.7 3.9 %copy-start.24 = (f32[6]{0:T(128)S(1)}, f32[6]{0:T(128)}, u32[]{:S(2)}) copy-start(f32[6]{0:T(128)} %param.19) | copy-start | bytes 76
  0.7 4.1 %copy-start.17 = (f32[128]{0:T(128)S(1)}, f32[128]{0:T(128)}, u32[]{:S(2)}) copy-start(f32[128]{0:T(128)} %param.18) | copy-start | bytes 1540
  0.7 4.1 %copy-start.20 = (bf16[128,128]{1,0:T(8,128)(2,1)S(1)}, bf16[128,128]{1,0:T(8,128)(2,1)}, u32[]{:S(2)}) copy-start(bf16[128,128]{1,0:T(8,128)(2,1)} %param.17) | copy-start | bytes 98308
  4.6 2.2 %copy-start.2 = (bf16[4096,128]{1,0:T(8,128)(2,1)}, bf16[4096,128]{1,0:T(8,128)(2,1)S(1)}, u32[]{:S(2)}) copy-start(bf16[4096,128]{1,0:T(8,128)(2,1)S(1)} %get-tuple-element.25) | copy-start | bytes 3145732
  4.8 2.0 %copy-start.8 = (f32[3,4096]{1,0:T(4,128)S(1)}, f32[3,4096]{1,0:T(4,128)}, u32[]{:S(2)}) copy-start(f32[3,4096]{1,0:T(4,128)} %param.14) | copy-start | bytes 147460
  4.8 2.2 %copy-start.13 = (s32[32,256]{1,0:T(8,128)S(1)}, s32[32,256]{1,0:T(8,128)}, u32[]{:S(2)}) copy-start(s32[32,256]{1,0:T(8,128)} %param.23) | copy-start | bytes 98308
  4.9 3.6 %copy-start.14 = (s32[32,256]{1,0:T(8,128)S(1)}, s32[32,256]{1,0:T(8,128)}, u32[]{:S(2)}) copy-start(s32[32,256]{1,0:T(8,128)} %param.24) | copy-start | bytes 98308
  6.8 18.5 %copy-start.6 = (f32[98,16,16]{0,2,1:T(8,128)S(1)}, f32[98,16,16]{0,2,1:T(8,128)}, u32[]{:S(2)}) copy-start(f32[98,16,16]{0,2,1:T(8,128)} %param.20) | copy-start | bytes 301060
  8.4 18.7 %copy-start.19 = (s32[125]{0:T(128)S(1)}, s32[125]{0:T(128)}, u32[]{:S(2)}) copy-start(s32[125]{0:T(128)} %constant.75) | copy-start | bytes 1504
  15.1 22.3 %all-to-all-start = ((f32[5,32,256]{2,0,1:T(8,128)}), f32[5,32,256]{2,0,1:T(8,128)S(1)}, u32[]{:S(2)}, u32[]{:S(2)}) async-start(f32[5,32,256]{2,0,1:T(8,128)} %bitcast.188), calls=%async_computation | async-start | bytes 524288 | tf_op jit(solution)/shard_map/all_to_all | solution.py:412
  25.9 0.6 copy-start.11
  26.5 0.6 copy-start.9
  27.9 20.3 %copy-start.15 = (f32[64,16]{0,1:T(8,128)S(1)}, f32[64,16]{0,1:T(8,128)}, u32[]{:S(2)}) copy-start(f32[64,16]{0,1:T(8,128)} %param.22) | copy-start | bytes 12292
  37.4 0.7 copy-start.1
  38.1 21.9 %copy-start.10 = (pred[5,8,4]{1,2,0:T(4,128)(4,1)S(1)}, pred[5,8,4]{1,2,0:T(4,128)(4,1)}, u32[]{:S(2)}) copy-start(pred[5,8,4]{1,2,0:T(4,128)(4,1)} %copy-done.9) | copy-start | bytes 484
  38.1 28.7 %copy-start.12 = (pred[5,64,64]{2,1,0:T(8,128)(4,1)S(1)}, pred[5,64,64]{2,1,0:T(8,128)(4,1)}, u32[]{:S(2)}) copy-start(pred[5,64,64]{2,1,0:T(8,128)(4,1)} %copy-done.11) | copy-start | bytes 61444
  48.7 4.4 %collective-permute-start.1 = (f32[16,2,4,64]{3,0,2,1:T(8,128)S(1)}, f32[16,2,4,64]{3,0,2,1:T(8,128)S(1)}, u32[]{:S(2)}, u32[]{:S(2)}) collective-permute-start(f32[16,2,4,64]{3,0,2,1:T(8,128)S(1)} %get-tuple-element.19), channel_id=1, source_target_pairs={{32,0},{64,32},{96,64},{128,96},{160,128},{192,160},{224,192},{256... | collective-permute-start | bytes 98312 | tf_op jit(solution)/shard_map/ppermute | solution.py:35
  50.0 3.9 %collective-permute-start = (f32[16,2,4,64]{3,0,2,1:T(8,128)S(1)}, f32[16,2,4,64]{3,0,2,1:T(8,128)S(1)}, u32[]{:S(2)}, u32[]{:S(2)}) collective-permute-start(f32[16,2,4,64]{3,0,2,1:T(8,128)S(1)} %get-tuple-element.18), channel_id=1, source_target_pairs={{0,32},{32,64},{64,96},{96,128},{128,160},{160,192},{192,224},{224... | collective-permute-start | bytes 98312 | tf_op jit(solution)/shard_map/ppermute | solution.py:33
  53.0 15.0 %copy-start.5 = (f32[25,16,16]{2,1,0:T(8,128)S(1)}, f32[25,16,16]{2,1,0:T(8,128)}, u32[]{:S(2)}) copy-start(f32[25,16,16]{2,1,0:T(8,128)} %get-tuple-element.11) | copy-start | bytes 76804
  54.0 6.9 %collective-permute-start.3 = (f32[16,8,2,64]{3,0,2,1:T(8,128)S(1)}, f32[16,8,2,64]{3,0,2,1:T(8,128)S(1)}, u32[]{:S(2)}, u32[]{:S(2)}) collective-permute-start(f32[16,8,2,64]{3,0,2,1:T(8,128)S(1)} %get-tuple-element.15), channel_id=1, source_target_pairs={{1,0},{2,1},{3,2},{4,3},{5,4},{6,5},{7,6},{8,7},{9,8},{10,9},{11,1... | collective-permute-start | bytes 196616 | tf_op jit(solution)/shard_map/ppermute | solution.py:35
  57.6 9.2 %collective-permute-start.2 = (f32[16,8,2,64]{3,0,2,1:T(8,128)S(1)}, f32[16,8,2,64]{3,0,2,1:T(8,128)S(1)}, u32[]{:S(2)}, u32[]{:S(2)}) collective-permute-start(f32[16,8,2,64]{3,0,2,1:T(8,128)S(1)} %get-tuple-element.14), channel_id=1, source_target_pairs={{0,1},{1,2},{2,3},{3,4},{4,5},{5,6},{6,7},{7,8},{8,9},{9,10},{10,1... | collective-permute-start | bytes 196616 | tf_op jit(solution)/shard_map/ppermute | solution.py:33
  68.0 1.3 copy-start.4
  76.6 3.5 %copy-start.16 = (f32[64,16]{0,1:T(8,128)S(1)}, f32[64,16]{0,1:T(8,128)}, u32[]{:S(2)}) copy-start(f32[64,16]{0,1:T(8,128)} %param.21) | copy-start | bytes 12292
  78.7 28.2 %copy-start.23 = (s32[4096]{0:T(1024)S(1)}, s32[4096]{0:T(1024)}, u32[]{:S(2)}) copy-start(s32[4096]{0:T(1024)} %param.15) | copy-start | bytes 49156
  78.7 28.4 %copy-start.18 = (f32[128]{0:T(128)S(1)}, f32[128]{0:T(128)}, u32[]{:S(2)}) copy-start(f32[128]{0:T(128)} %param.18) | copy-start | bytes 1540
  81.3 28.3 %copy-start.3 = (bf16[4096,128]{1,0:T(8,128)(2,1)S(1)}, bf16[4096,128]{1,0:T(8,128)(2,1)}, u32[]{:S(2)}) copy-start(bf16[4096,128]{1,0:T(8,128)(2,1)} %copy-done.2) | copy-start | bytes 3145732
  106.8 3.3 %copy-start.7 = (f32[4096]{0:T(1024)}, f32[4096]{0:T(1024)S(1)}, u32[]{:S(2)}) copy-start(f32[4096]{0:T(1024)S(1)} %reshape.422) | copy-start | bytes 49156
  107.2 3.0 %copy-start.21 = (bf16[128,128]{1,0:T(8,128)(2,1)S(1)}, bf16[128,128]{1,0:T(8,128)(2,1)}, u32[]{:S(2)}) copy-start(bf16[128,128]{1,0:T(8,128)(2,1)} %param.17) | copy-start | bytes 98308
  112.9 3.2 %collective-permute-start.4 = (f32[32902]{0:T(1024)S(1)}, f32[32902]{0:T(1024)S(1)}, u32[]{:S(2)}, u32[]{:S(2)}) collective-permute-start(f32[32902]{0:T(1024)S(1)} %pad_maximum_fusion.3), channel_id=1, source_target_pairs={{0,32},{32,0},{1,33},{33,1},{2,34},{34,2},{3,35},{35,3},{4,36},{36... | collective-permute-start | bytes 394832 | tf_op jit(solution)/shard_map/ppermute | solution.py:101
  131.0 8.3 %collective-permute-start.5 = (f32[1029]{0:T(1024)S(1)}, f32[1029]{0:T(1024)S(1)}, u32[]{:S(2)}, u32[]{:S(2)}) collective-permute-start(f32[1029]{0:T(1024)S(1)} %reduce_sum.29), channel_id=1, source_target_pairs={{0,64},{64,0},{128,192},{192,128},{256,320},{320,256},{384,448},{4... | collective-permute-start | bytes 12356 | tf_op jit(solution)/shard_map/ppermute | solution.py:101
  139.3 8.7 %collective-permute-start.6 = (f32[1029]{0:T(1024)S(1)}, f32[1029]{0:T(1024)S(1)}, u32[]{:S(2)}, u32[]{:S(2)}) collective-permute-start(f32[1029]{0:T(1024)S(1)} %add.203), channel_id=1, source_target_pairs={{0,128},{64,192},{128,0},{192,64},{256,384},{320,448},{384,256},{4... | collective-permute-start | bytes 12356 | tf_op jit(solution)/shard_map/ppermute | solution.py:101
  148.0 10.9 %collective-permute-start.7 = (f32[1029]{0:T(1024)S(1)}, f32[1029]{0:T(1024)S(1)}, u32[]{:S(2)}, u32[]{:S(2)}) collective-permute-start(f32[1029]{0:T(1024)S(1)} %add.204), channel_id=1, source_target_pairs={{0,256},{64,320},{128,384},{192,448},{256,0},{320,64},{384,128},{4... | collective-permute-start | bytes 12356 | tf_op jit(solution)/shard_map/ppermute | solution.py:101

commit v8 on v7

--- a/solution.py
+++ b/solution.py
@@ -415,6 +415,9 @@
     node_grid = moments.reshape(NODES, BZ, BX, BY)
     reduced = jnp.einsum("nr,nzxy->rzxy", compress_v, node_grid, precision=lax.Precision.HIGHEST)
     padded = extended_2(reduced, ((GRP, 1), (DEV, 2)), 2)
+    padded, hidden_two, slope_two, slope_one = lax.optimization_barrier(
+        (padded, hidden_two, silu_slope(pre_two), silu_slope(pre_one))
+    )
     local_terms = translate(padded, m2l_kernels)
     expansion = jnp.dot(expand_u, local_terms.reshape(RANK, BOXES), precision=lax.Precision.HIGHEST)
     slot_potential = box_pick(expansion, arrived).reshape(send_list.shape)
@@ -422,7 +425,7 @@
     potential = slots_to_atoms(returned.reshape(-1), atom_high, atom_low, atom_count)
     head_part = jnp.sum(potential[:, None] * hidden_two, axis=0) * grad_scale
     species_part = jnp.dot(species_hot, potential, precision=lax.Precision.HIGHEST) * grad_scale
-    delta_two = (potential[:, None] * w_head[None, :] * silu_slope(pre_two)).astype(jnp.bfloat16)
+    delta_two = (potential[:, None] * w_head[None, :] * slope_two).astype(jnp.bfloat16)
     mid_part = (
         lax.dot_general(
             hidden_one, delta_two, (((0,), (0,)), ((), ())), preferred_element_type=jnp.float32
@@ -432,7 +435,7 @@
     back_one = lax.dot_general(
         delta_two, w_mid, (((1,), (1,)), ((), ())), preferred_element_type=jnp.float32
     )
-    delta_one = (back_one * silu_slope(pre_one)).astype(jnp.bfloat16)
+    delta_one = (back_one * slope_one).astype(jnp.bfloat16)
     in_part = (
         lax.dot_general(
             desc, delta_one, (((0,), (0,)), ((), ())), preferred_element_type=jnp.float32

time: 176 us -> 187 us (1.062)
  waiting for transfers between devices: 22.4 us -> 14 us
  local copies, waits for them, and re-layouts: 10 us -> 16.9 us
  other arithmetic: 6.79 us -> 13.5 us
  matrix products: 22.2 us -> 25 us
  blocking collectives: 43.8 us -> 45.9 us
    all_to_all x1, waiting for transfers between devices: 8.63 us -> 0.01 us  [shards(): lax.all_to_all(outgoing, DEV, split_axis=1, concat_axis=1, tiled=True)]
    unnamed x9, other arithmetic: 0.34 us -> 4.24 us
    convert_element_type x1 -> x0, other arithmetic: 2.4 us -> none  [shards(): (potential[:, None] * w_head[None, :] * silu_slope(pre_two)).astype(jnp.b...]
    concatenate x1, local copies, waits for them, and re-layouts: 0.06 us -> 2.11 us  [translate(): jnp.concatenate([m2l_kernels, jnp.zeros((1, rank_count, rank_count), jnp....]
    reduce_sum x0 -> x1, other arithmetic: none -> 2.01 us  [shards(): head_part = jnp.sum(potential[:, None] * hidden_two, axis=0) * grad_scale]
    gather x1, local copies, waits for them, and re-layouts: 0.75 us -> 2.75 us  [translate(): stencil = extended[jnp.asarray(shell_table())]]
    all_to_all x1, blocking collectives: 15.5 us -> 17.5 us  [shards(): lax.all_to_all(slot_potential, DEV, split_axis=0, concat_axis=0, tiled=True)]
    unnamed x54 -> x48, local copies, waits for them, and re-layouts: 5.29 us -> 5.94 us
  transfers between devices with their start and end apart: 9 -> 9, of which waited for: 8 -> 7; matrix products, arithmetic and copies ran while one was open for 1% -> 9% of each run, Pallas kernels for 0% -> 0%
where the time goes in v8:
time: 187 us; the launch traced here: 185 us
  starting transfers between devices  46.1 us (25%)
  blocking collectives  45.9 us (25%)
  matrix products  25 us (13%)
  Pallas kernels  22.9 us (12%)
  local copies, waits for them, and re-layouts  16.9 us (9%)
  waiting for transfers between devices  14 us (7%)
  other arithmetic  13.5 us (7%)
    ppermute x4, starting transfers between devices, swapped(): return lax.ppermute(x, axis, [(i, i ^ step) for i in range(count)])  24.9 us
    all_to_all x1, blocking collectives, shards(): lax.all_to_all(slot_potential, DEV, split_axis=0, concat_axis=0, tiled=True)  17.5 us
    all_to_all x1, blocking collectives, hybrid_sum(): lax.all_to_all(lines, plane, 0, 0, tiled=True).reshape(peers, -1)  14.5 us
    all_to_all x1, blocking collectives, hybrid_sum(): return lax.all_to_all(copies, plane, 0, 0, tiled=True).reshape(-1)[:length]  13.9 us
    all_to_all x1, starting transfers between devices, shards(): lax.all_to_all(outgoing, DEV, split_axis=1, concat_axis=1, tiled=True)  10.2 us
    pallas_call x1, Pallas kernels, box_sum(): pl.pallas_call(box_sum_kernel, grid=(slots // tile,), in_specs=[pl.BlockS...  8.58 us
    ppermute x2, waiting for transfers between devices, extended_2(): lax.ppermute(tail, axis, [(i, (i + 1) % count) for i in range(ends)])  7.54 us
    pallas_call x1, Pallas kernels, box_pick(): pl.pallas_call(box_pick_kernel, grid=(slots // tile,), in_specs=[pl.Block...  6.64 us
  transfers between devices with their start and end apart: 9, of which 7 were waited for; matrix products, arithmetic and copies ran while one was open for 9% of the time, Pallas kernels for 0%

profile of v8, /device:TPU:8, one launch (start us, length us, event | category | flops | bytes accessed | tf_op | source)
XLA Modules:
  0.0 185.4 jit_solution(11865044083237126967)
XLA Ops:
  0.7 1.2 copy-done
  1.9 3.2 %add_multiply_fusion = (f32[4096,128]{1,0:T(8,128)}, bf16[4096,128]{1,0:T(8,128)(2,1)S(1)}) fusion(bf16[4096,128]{1,0:T(8,128)(2,1)S(1)} %copy-done, bf16[128,128]{1,0:T(8,128)(2,1)} %param.16), kind=kOutput, calls=%fused_computation.4 | convolution fusion | flops 138936320 | bytes 4227072 | tf_op jit(solution)/shard_map/dot_general | solution.py:395
  5.3 2.3 %multiply_reduce_fusion.1 = (f32[4096]{0:T(1024)S(1)}, f32[4096,128]{1,0:T(8,128)}, f32[4096,128]{1,0:T(8,128)S(1)}) fusion(f32[128]{0:T(128)S(1)} %copy-done.17, bf16[4096,128]{1,0:T(8,128)(2,1)S(1)} %get-tuple-element.16, bf16[128,128]{1,0:T(8,128)(2,1)S(1)} %copy-done.12), kind=kOutput, calls=%fused_computation.6 | convolution fusion | flops 139456512 | bytes 5292544 | tf_op jit(solution)/shard_map/dot_general | solution.py:397
  8.0 0.6 copy.94
  8.6 0.6 copy.95
  9.3 1.4 copy.96
  10.7 0.7 pad_maximum_fusion.3.table_ref
  11.4 5.3 %shard_map.164 = f32[5,8192]{1,0:T(8,128)} custom-call(bf16[768,64]{1,0:T(8,128)(2,1)} %pad_maximum_fusion.3.table_ref, s32[1,8192]{1,0:T(1,128)} %bitcast.194, s32[1,8192]{1,0:T(1,128)} %bitcast.196, s32[1,8192]{1,0:T(1,128)} %bitcast.198), custom_call_target="tpu_custom_call" | custom-call | tf_op jit(solution)/shard_map/pallas_call | solution.py:165
  16.6 10.2 %all-to-all-start = ((f32[5,32,256]{2,0,1:T(8,128)}), f32[5,32,256]{2,0,1:T(8,128)S(1)}, u32[]{:S(2)}, u32[]{:S(2)}) async-start(f32[5,32,256]{2,0,1:T(8,128)} %bitcast.186), calls=%async_computation | async-start | bytes 524288 | tf_op jit(solution)/shard_map/all_to_all | solution.py:412
  26.8 0.5 iota_add_fusion.3
  28.4 0.6 iota_add_fusion.7
  29.5 0.6 iota_add_fusion.5
  30.1 1.3 copy.59
  31.3 0.7 fusion.56
  32.0 0.7 fusion.57
  32.7 2.1 %concatenate.28 = f32[99,16,16]{2,1,0:T(8,128)} pad(f32[98,16,16]{2,1,0:T(8,128)} %copy.59, f32[]{:T(128)} %constant.55.clone.1), padding=0_1x0_0x0_0 | pad | bytes 201732 | tf_op jit(solution)/shard_map/concatenate | solution.py:362
  34.8 0.7 fusion.59
  35.5 0.8 constant_dynamic-update-slice_fusion.3
  36.2 0.7 constant_dynamic-update-slice_fusion.2
  36.9 0.7 constant_dynamic-update-slice_fusion.1
  37.7 2.8 %gather_fusion = f32[125,16,16]{2,1,0:T(8,128)} fusion(f32[99,16,16]{2,1,0:T(8,128)} %concatenate.28, s32[1024]{0:T(1024)S(1)} %pad_clamp_fusion), kind=kCustom, calls=%fused_computation | custom fusion | bytes 256500 | tf_op jit(solution)/shard_map/gather | solution.py:365
  40.4 2.3 %fusion.72 = (f32[25,16,16]{2,1,0:T(8,128)}, f32[25,16,16]{2,1,0:T(8,128)}, f32[25,16,16]{2,1,0:T(8,128)}, f32[25,16,16]{2,1,0:T(8,128)}, f32[25,16,16]{2,1,0:T(8,128)}) fusion(f32[125,16,16]{2,1,0:T(8,128)} %gather_fusion), kind=kLoop, calls=%fused_computation.126 | loop fusion | bytes 256000 | tf_op jit(solution)/shard_map/slice | solution.py:370
  42.7 0.7 copy-done.1
  43.4 8.6 %shard_map.165 = f32[128,1024]{1,0:T(8,128)} custom-call(f32[5,8192]{1,0:T(8,128)} %bitcast.184), custom_call_target="tpu_custom_call" | custom-call | tf_op jit(solution)/shard_map/pallas_call | solution.py:272
  52.0 1.1 slice_add_fusion
  53.0 1.1 reshape.420
  54.2 1.6 convolution_bitcast_fusion.7
  55.8 1.3 collective-permute-start.1
  57.1 3.0 %collective-permute-start = (f32[16,2,4,64]{3,0,2,1:T(8,128)S(1)}, f32[16,2,4,64]{3,0,2,1:T(8,128)S(1)}, u32[]{:S(2)}, u32[]{:S(2)}) collective-permute-start(f32[16,2,4,64]{3,0,2,1:T(8,128)S(1)} %get-tuple-element.29), channel_id=1, source_target_pairs={{0,32},{32,64},{64,96},{96,128},{128,160},{160,192},{192,224},{224... | collective-permute-start | bytes 98312 | tf_op jit(solution)/shard_map/ppermute | solution.py:33
  60.1 0.9 collective-permute-done
  61.0 4.6 %collective-permute-start.3 = (f32[16,8,2,64]{3,0,2,1:T(8,128)S(1)}, f32[16,8,2,64]{3,0,2,1:T(8,128)S(1)}, u32[]{:S(2)}, u32[]{:S(2)}) collective-permute-start(f32[16,8,2,64]{3,0,2,1:T(8,128)S(1)} %get-tuple-element.26), channel_id=1, source_target_pairs={{1,0},{2,1},{3,2},{4,3},{5,4},{6,5},{7,6},{8,7},{9,8},{10,9},{11,1... | collective-permute-start | bytes 196616 | tf_op jit(solution)/shard_map/ppermute | solution.py:35
  65.6 2.1 %collective-permute-start.2 = (f32[16,8,2,64]{3,0,2,1:T(8,128)S(1)}, f32[16,8,2,64]{3,0,2,1:T(8,128)S(1)}, u32[]{:S(2)}, u32[]{:S(2)}) collective-permute-start(f32[16,8,2,64]{3,0,2,1:T(8,128)S(1)} %get-tuple-element.25), channel_id=1, source_target_pairs={{0,1},{1,2},{2,3},{3,4},{4,5},{5,6},{6,7},{7,8},{8,9},{9,10},{10,1... | collective-permute-start | bytes 196616 | tf_op jit(solution)/shard_map/ppermute | solution.py:33
  68.1 6.7 %collective-permute-done.2 = f32[16,8,2,64]{3,0,2,1:T(8,128)S(1)} collective-permute-done((f32[16,8,2,64]{3,0,2,1:T(8,128)S(1)}, f32[16,8,2,64]{3,0,2,1:T(8,128)S(1)}, u32[]{:S(2)}, u32[]{:S(2)}) %collective-permute-start.2) | collective-permute-done | bytes 65568 | tf_op jit(solution)/shard_map/ppermute | solution.py:33
  74.9 1.2 convolution_bitcast_fusion
  76.1 1.3 convolution_bitcast_fusion.5
  77.4 1.3 convolution_bitcast_fusion.4
  78.7 1.3 convolution_bitcast_fusion.3
  80.1 1.3 convolution_bitcast_fusion.2
  81.4 1.3 convolution_bitcast_fusion.1
  82.7 1.0 fusion.11
  83.7 1.0 fusion.38
  84.8 1.0 fusion.35
  85.8 1.0 fusion.32
  86.8 1.2 fusion.29
  88.7 0.7 pad_maximum_fusion.2.table_ref
  89.4 6.6 %shard_map.166 = f32[1,8192]{1,0:T(1,128)} custom-call(bf16[128,1024]{1,0:T(8,128)(2,1)} %pad_maximum_fusion.2.table_ref, f32[5,8192]{1,0:T(8,128)} %bitcast.185), custom_call_target="tpu_custom_call" | custom-call | tf_op jit(solution)/shard_map/pallas_call | solution.py:295
  96.0 17.5 %all_to_all.29 = f32[32,1,256]{2,1,0:T(1,128)} all-to-all(f32[32,1,256]{2,1,0:T(1,128)} %bitcast.199), channel_id=1, replica_groups=mesh['grp_0'=8,'grp_1'=2,'dev_0'=8,'dev_1'=4] {'dev_0','dev_1'}, dimensions={0} | all-to-all | bytes 65536 | tf_op jit(solution)/shard_map/all_to_all | solution.py:424
  113.5 2.4 %shard_map.167 = f32[192,64]{1,0:T(8,128)} custom-call(f32[1,8192]{1,0:T(1,128)} %bitcast.200, s32[1,8192]{1,0:T(1,128)} %bitcast.195, s32[1,8192]{1,0:T(1,128)} %bitcast.197), custom_call_target="tpu_custom_call" | custom-call | tf_op jit(solution)/shard_map/pallas_call | solution.py:207
  116.0 0.8 slice_add_fusion.1
  117.2 2.0 %multiply_reduce_fusion = f32[128]{0:T(128)S(1)} fusion(f32[4096,128]{1,0:T(8,128)} %get-tuple-element.12, f32[4096]{0:T(1024)S(1)} %reshape.422), kind=kLoop, calls=%fused_computation.1 | loop fusion | flops 1048448 | bytes 2114048 | tf_op jit(solution)/shard_map/reduce_sum | solution.py:426
  119.2 1.1 fusion.41
  120.3 2.9 %fusion.42 = f32[128,128]{0,1:T(8,128)S(1)} fusion(bf16[4096,128]{1,0:T(8,128)(2,1)S(1)} %copy-done, f32[4096,128]{1,0:T(8,128)} %get-tuple-element.11, bf16[128,128]{1,0:T(8,128)(2,1)S(1)} %copy-done.13, f32[4096,128]{1,0:T(8,128)S(1)} %get-tuple-element.10, f32[4096]{0:T(1024)S(1)} %reshape.422, f32[128]{0:T(128)S(1)} %copy-done.17), kind=kOutput, calls=%fused_computation.47 | convolution fusion | flops 271073280 | bytes 5358080 | tf_op jit(solution)/shard_map/dot_general | solution.py:440
  123.3 1.9 %collective-permute-start.4 = (f32[32902]{0:T(1024)S(1)}, f32[32902]{0:T(1024)S(1)}, u32[]{:S(2)}, u32[]{:S(2)}) collective-permute-start(f32[32902]{0:T(1024)S(1)} %pad_maximum_fusion.4), channel_id=1, source_target_pairs={{0,32},{32,0},{1,33},{33,1},{2,34},{34,2},{3,35},{35,3},{4,36},{36... | collective-permute-start | bytes 394832 | tf_op jit(solution)/shard_map/ppermute | solution.py:101
  125.3 1.3 collective-permute-done.4
  126.9 14.5 %all_to_all.30 = f32[32,1,1029]{2,1,0:T(1,128)S(1)} all-to-all(f32[32,1,1029]{2,1,0:T(1,128)S(1)} %all_to_all.22), channel_id=1, replica_groups=mesh['grp_0'=8,'grp_1'=2,'dev_0'=8,'dev_1'=4] {'dev_0','dev_1'}, dimensions={0} | all-to-all | bytes 263424 | tf_op jit(solution)/shard_map/all_to_all | solution.py:117
  141.5 6.7 %collective-permute-start.5 = (f32[1029]{0:T(1024)S(1)}, f32[1029]{0:T(1024)S(1)}, u32[]{:S(2)}, u32[]{:S(2)}) collective-permute-start(f32[1029]{0:T(1024)S(1)} %reduce_sum.29), channel_id=1, source_target_pairs={{0,64},{64,0},{128,192},{192,128},{256,320},{320,256},{384,448},{4... | collective-permute-start | bytes 12356 | tf_op jit(solution)/shard_map/ppermute | solution.py:101
  148.1 1.6 collective-permute-done.5
  149.8 7.1 %collective-permute-start.6 = (f32[1029]{0:T(1024)S(1)}, f32[1029]{0:T(1024)S(1)}, u32[]{:S(2)}, u32[]{:S(2)}) collective-permute-start(f32[1029]{0:T(1024)S(1)} %add.203), channel_id=1, source_target_pairs={{0,128},{64,192},{128,0},{192,64},{256,384},{320,448},{384,256},{4... | collective-permute-start | bytes 12356 | tf_op jit(solution)/shard_map/ppermute | solution.py:101
  156.8 1.6 collective-permute-done.6
  158.4 9.3 %collective-permute-start.7 = (f32[1029]{0:T(1024)S(1)}, f32[1029]{0:T(1024)S(1)}, u32[]{:S(2)}, u32[]{:S(2)}) collective-permute-start(f32[1029]{0:T(1024)S(1)} %add.204), channel_id=1, source_target_pairs={{0,256},{64,320},{128,384},{192,448},{256,0},{320,64},{384,128},{4... | collective-permute-start | bytes 12356 | tf_op jit(solution)/shard_map/ppermute | solution.py:101
  167.7 1.6 collective-permute-done.7
  169.4 13.9 %all_to_all.31 = f32[32,1,1029]{2,1,0:T(1,128)S(1)} all-to-all(f32[32,1,1029]{2,1,0:T(1,128)S(1)} %broadcast_in_dim.10), channel_id=1, replica_groups=mesh['grp_0'=8,'grp_1'=2,'dev_0'=8,'dev_1'=4] {'dev_0','dev_1'}, dimensions={0} | all-to-all | bytes 263424 | tf_op jit(solution)/shard_map/all_to_all | solution.py:120
  183.8 0.7 slice_bitcast_fusion.10
  184.9 0.5 slice.126
  (84 shorter events, 5.1 us)
Async XLA Ops:
  0.6 1.2 copy-start
  0.6 4.4 %copy-start.19 = (s32[4096]{0:T(1024)S(1)}, s32[4096]{0:T(1024)}, u32[]{:S(2)}) copy-start(s32[4096]{0:T(1024)} %param.15) | copy-start | bytes 49156
  0.7 4.4 %copy-start.21 = (f32[6]{0:T(128)S(1)}, f32[6]{0:T(128)}, u32[]{:S(2)}) copy-start(f32[6]{0:T(128)} %param.19) | copy-start | bytes 76
  0.7 4.6 %copy-start.17 = (f32[128]{0:T(128)S(1)}, f32[128]{0:T(128)}, u32[]{:S(2)}) copy-start(f32[128]{0:T(128)} %param.18) | copy-start | bytes 1540
  0.7 4.6 %copy-start.12 = (bf16[128,128]{1,0:T(8,128)(2,1)S(1)}, bf16[128,128]{1,0:T(8,128)(2,1)}, u32[]{:S(2)}) copy-start(bf16[128,128]{1,0:T(8,128)(2,1)} %param.17) | copy-start | bytes 98308
  5.1 2.6 %copy-start.2 = (bf16[4096,128]{1,0:T(8,128)(2,1)}, bf16[4096,128]{1,0:T(8,128)(2,1)S(1)}, u32[]{:S(2)}) copy-start(bf16[4096,128]{1,0:T(8,128)(2,1)S(1)} %get-tuple-element.16) | copy-start | bytes 3145732
  5.3 2.4 %copy-start.11 = (f32[3,4096]{1,0:T(4,128)S(1)}, f32[3,4096]{1,0:T(4,128)}, u32[]{:S(2)}) copy-start(f32[3,4096]{1,0:T(4,128)} %param.14) | copy-start | bytes 147460
  5.3 2.6 %copy-start.14 = (s32[32,256]{1,0:T(8,128)S(1)}, s32[32,256]{1,0:T(8,128)}, u32[]{:S(2)}) copy-start(s32[32,256]{1,0:T(8,128)} %param.23) | copy-start | bytes 98308
  7.7 22.4 %copy-start.10 = (f32[98,16,16]{0,2,1:T(8,128)S(1)}, f32[98,16,16]{0,2,1:T(8,128)}, u32[]{:S(2)}) copy-start(f32[98,16,16]{0,2,1:T(8,128)} %param.20) | copy-start | bytes 301060
  9.3 28.4 %copy-start.18 = (s32[125]{0:T(128)S(1)}, s32[125]{0:T(128)}, u32[]{:S(2)}) copy-start(s32[125]{0:T(128)} %constant.75) | copy-start | bytes 1504
  16.6 26.0 %all-to-all-start = ((f32[5,32,256]{2,0,1:T(8,128)}), f32[5,32,256]{2,0,1:T(8,128)S(1)}, u32[]{:S(2)}, u32[]{:S(2)}) async-start(f32[5,32,256]{2,0,1:T(8,128)} %bitcast.186), calls=%async_computation | async-start | bytes 524288 | tf_op jit(solution)/shard_map/all_to_all | solution.py:412
  40.4 13.8 %copy-start.15 = (f32[64,16]{0,1:T(8,128)S(1)}, f32[64,16]{0,1:T(8,128)}, u32[]{:S(2)}) copy-start(f32[64,16]{0,1:T(8,128)} %param.22) | copy-start | bytes 12292
  42.7 0.7 copy-start.1
  55.8 4.4 %collective-permute-start.1 = (f32[16,2,4,64]{3,0,2,1:T(8,128)S(1)}, f32[16,2,4,64]{3,0,2,1:T(8,128)S(1)}, u32[]{:S(2)}, u32[]{:S(2)}) collective-permute-start(f32[16,2,4,64]{3,0,2,1:T(8,128)S(1)} %get-tuple-element.30), channel_id=1, source_target_pairs={{32,0},{64,32},{96,64},{128,96},{160,128},{192,160},{224,192},{256... | collective-permute-start | bytes 98312 | tf_op jit(solution)/shard_map/ppermute | solution.py:35
  57.1 3.9 %collective-permute-start = (f32[16,2,4,64]{3,0,2,1:T(8,128)S(1)}, f32[16,2,4,64]{3,0,2,1:T(8,128)S(1)}, u32[]{:S(2)}, u32[]{:S(2)}) collective-permute-start(f32[16,2,4,64]{3,0,2,1:T(8,128)S(1)} %get-tuple-element.29), channel_id=1, source_target_pairs={{0,32},{32,64},{64,96},{96,128},{128,160},{160,192},{192,224},{224... | collective-permute-start | bytes 98312 | tf_op jit(solution)/shard_map/ppermute | solution.py:33
  61.0 7.1 %collective-permute-start.3 = (f32[16,8,2,64]{3,0,2,1:T(8,128)S(1)}, f32[16,8,2,64]{3,0,2,1:T(8,128)S(1)}, u32[]{:S(2)}, u32[]{:S(2)}) collective-permute-start(f32[16,8,2,64]{3,0,2,1:T(8,128)S(1)} %get-tuple-element.26), channel_id=1, source_target_pairs={{1,0},{2,1},{3,2},{4,3},{5,4},{6,5},{7,6},{8,7},{9,8},{10,9},{11,1... | collective-permute-start | bytes 196616 | tf_op jit(solution)/shard_map/ppermute | solution.py:35
  65.6 9.2 %collective-permute-start.2 = (f32[16,8,2,64]{3,0,2,1:T(8,128)S(1)}, f32[16,8,2,64]{3,0,2,1:T(8,128)S(1)}, u32[]{:S(2)}, u32[]{:S(2)}) collective-permute-start(f32[16,8,2,64]{3,0,2,1:T(8,128)S(1)} %get-tuple-element.25), channel_id=1, source_target_pairs={{0,1},{1,2},{2,3},{3,4},{4,5},{5,6},{6,7},{7,8},{8,9},{9,10},{10,1... | collective-permute-start | bytes 196616 | tf_op jit(solution)/shard_map/ppermute | solution.py:33
  67.8 8.2 %copy-start.8 = (f32[25,16,16]{2,1,0:T(8,128)S(1)}, f32[25,16,16]{2,1,0:T(8,128)}, u32[]{:S(2)}) copy-start(f32[25,16,16]{2,1,0:T(8,128)} %get-tuple-element.22) | copy-start | bytes 76804
  76.0 1.3 copy-start.7
  77.4 1.3 copy-start.6
  78.7 1.3 copy-start.5
  80.0 1.3 copy-start.4
  84.8 3.5 %copy-start.16 = (f32[64,16]{0,1:T(8,128)S(1)}, f32[64,16]{0,1:T(8,128)}, u32[]{:S(2)}) copy-start(f32[64,16]{0,1:T(8,128)} %param.21) | copy-start | bytes 12292
  86.8 30.1 %copy-start.20 = (s32[4096]{0:T(1024)S(1)}, s32[4096]{0:T(1024)}, u32[]{:S(2)}) copy-start(s32[4096]{0:T(1024)} %param.15) | copy-start | bytes 49156
  116.8 3.4 %copy-start.9 = (f32[4096]{0:T(1024)}, f32[4096]{0:T(1024)S(1)}, u32[]{:S(2)}) copy-start(f32[4096]{0:T(1024)S(1)} %reshape.422) | copy-start | bytes 49156
  116.9 2.3 %copy-start.3 = (bf16[4096,128]{1,0:T(8,128)(2,1)S(1)}, bf16[4096,128]{1,0:T(8,128)(2,1)}, u32[]{:S(2)}) copy-start(bf16[4096,128]{1,0:T(8,128)(2,1)} %copy-done.2) | copy-start | bytes 3145732
  119.2 1.1 copy-start.13
  123.3 3.2 %collective-permute-start.4 = (f32[32902]{0:T(1024)S(1)}, f32[32902]{0:T(1024)S(1)}, u32[]{:S(2)}, u32[]{:S(2)}) collective-permute-start(f32[32902]{0:T(1024)S(1)} %pad_maximum_fusion.4), channel_id=1, source_target_pairs={{0,32},{32,0},{1,33},{33,1},{2,34},{34,2},{3,35},{35,3},{4,36},{36... | collective-permute-start | bytes 394832 | tf_op jit(solution)/shard_map/ppermute | solution.py:101
  141.5 8.3 %collective-permute-start.5 = (f32[1029]{0:T(1024)S(1)}, f32[1029]{0:T(1024)S(1)}, u32[]{:S(2)}, u32[]{:S(2)}) collective-permute-start(f32[1029]{0:T(1024)S(1)} %reduce_sum.29), channel_id=1, source_target_pairs={{0,64},{64,0},{128,192},{192,128},{256,320},{320,256},{384,448},{4... | collective-permute-start | bytes 12356 | tf_op jit(solution)/shard_map/ppermute | solution.py:101
  149.8 8.7 %collective-permute-start.6 = (f32[1029]{0:T(1024)S(1)}, f32[1029]{0:T(1024)S(1)}, u32[]{:S(2)}, u32[]{:S(2)}) collective-permute-start(f32[1029]{0:T(1024)S(1)} %add.203), channel_id=1, source_target_pairs={{0,128},{64,192},{128,0},{192,64},{256,384},{320,448},{384,256},{4... | collective-permute-start | bytes 12356 | tf_op jit(solution)/shard_map/ppermute | solution.py:101
  158.4 10.9 %collective-permute-start.7 = (f32[1029]{0:T(1024)S(1)}, f32[1029]{0:T(1024)S(1)}, u32[]{:S(2)}, u32[]{:S(2)}) collective-permute-start(f32[1029]{0:T(1024)S(1)} %add.204), channel_id=1, source_target_pairs={{0,256},{64,320},{128,384},{192,448},{256,0},{320,64},{384,128},{4... | collective-permute-start | bytes 12356 | tf_op jit(solution)/shard_map/ppermute | solution.py:101

commit v9 on v7

--- a/solution.py
+++ b/solution.py
@@ -37,6 +37,56 @@
             axis=dim,
         )
     return cells
+
+
+def shifted_pairs(counts, steps):
+    pairs = []
+    total = 1
+    for count in counts:
+        total *= count
+    for source in range(total):
+        place = []
+        rest = source
+        for count in reversed(counts):
+            place.append(rest % count)
+            rest //= count
+        place = place[::-1]
+        target = [p + s for p, s in zip(place, steps)]
+        if all(0 <= t < c for t, c in zip(target, counts)):
+            linear = 0
+            for t, c in zip(target, counts):
+                linear = linear * c + t
+            pairs.append((source, linear))
+    return pairs
+
+
+def extended_at_once(cells, width):
+    grp_count = lax.axis_size(GRP)
+    dev_count = lax.axis_size(DEV)
+    both = GRP + DEV
+
+    def moved(block, axes, counts, steps):
+        return lax.ppermute(block, axes, shifted_pairs(counts, steps))
+
+    head_z, tail_z = cells[:, :width], cells[:, -width:]
+    head_x, tail_x = cells[:, :, :width], cells[:, :, -width:]
+    counts = (grp_count, dev_count)
+    top = moved(tail_z, GRP, (grp_count,), (1,))
+    bottom = moved(head_z, GRP, (grp_count,), (-1,))
+    left = moved(tail_x, DEV, (dev_count,), (1,))
+    right = moved(head_x, DEV, (dev_count,), (-1,))
+    top_left = moved(tail_z[:, :, -width:], both, counts, (1, 1))
+    top_right = moved(tail_z[:, :, :width], both, counts, (1, -1))
+    bottom_left = moved(head_z[:, :, -width:], both, counts, (-1, 1))
+    bottom_right = moved(head_z[:, :, :width], both, counts, (-1, -1))
+    return jnp.concatenate(
+        [
+            jnp.concatenate([top_left, top, top_right], axis=2),
+            jnp.concatenate([left, cells, right], axis=2),
+            jnp.concatenate([bottom_left, bottom, bottom_right], axis=2),
+        ],
+        axis=1,
+    )
 
 
 def in_blocks(x, dim, peers):
@@ -414,7 +464,7 @@
     moments = box_sum(arrived, BOXES)
     node_grid = moments.reshape(NODES, BZ, BX, BY)
     reduced = jnp.einsum("nr,nzxy->rzxy", compress_v, node_grid, precision=lax.Precision.HIGHEST)
-    padded = extended_2(reduced, ((GRP, 1), (DEV, 2)), 2)
+    padded = extended_at_once(reduced, 2)
     local_terms = translate(padded, m2l_kernels)
     expansion = jnp.dot(expand_u, local_terms.reshape(RANK, BOXES), precision=lax.Precision.HIGHEST)
     slot_potential = box_pick(expansion, arrived).reshape(send_list.shape)

time: 176 us -> 188 us (1.068)
  starting transfers between devices: 45.4 us -> 61.1 us
  waiting for transfers between devices: 22.4 us -> 17.5 us
  blocking collectives: 43.8 us -> 46.6 us
    ppermute x4 -> x8, starting transfers between devices: 10.3 us -> 25.4 us  [moved(): return lax.ppermute(block, axes, shifted_pairs(counts, steps))]
    ppermute x4 -> x8, waiting for transfers between devices: 7.57 us -> 1.34 us  [moved(): return lax.ppermute(block, axes, shifted_pairs(counts, steps))]
    all_to_all x1, blocking collectives: 15.5 us -> 18 us  [shards(): lax.all_to_all(slot_potential, DEV, split_axis=0, concat_axis=0, tiled=True)]
    unnamed x54 -> x36, local copies, waits for them, and re-layouts: 5.29 us -> 4.3 us
  transfers between devices with their start and end apart: 9 -> 13, of which waited for: 8 -> 6; matrix products, arithmetic and copies ran while one was open for 1% -> 1% of each run, Pallas kernels for 0% -> 0%
where the time goes in v9:
time: 188 us; the launch traced here: 187 us
  starting transfers between devices  61.1 us (32%)
  blocking collectives  46.6 us (25%)
  Pallas kernels  23 us (12%)
  matrix products  22.2 us (12%)
  waiting for transfers between devices  17.5 us (9%)
  local copies, waits for them, and re-layouts  8.23 us (4%)
  other arithmetic  6.78 us (4%)
    ppermute x4, starting transfers between devices, swapped(): return lax.ppermute(x, axis, [(i, i ^ step) for i in range(count)])  25.5 us
    ppermute x8, starting transfers between devices, moved(): return lax.ppermute(block, axes, shifted_pairs(counts, steps))  25.4 us
    all_to_all x1, blocking collectives, shards(): lax.all_to_all(slot_potential, DEV, split_axis=0, concat_axis=0, tiled=True)  18 us
    all_to_all x1, blocking collectives, hybrid_sum(): lax.all_to_all(lines, plane, 0, 0, tiled=True).reshape(peers, -1)  14.8 us
    all_to_all x1, blocking collectives, hybrid_sum(): return lax.all_to_all(copies, plane, 0, 0, tiled=True).reshape(-1)[:length]  13.9 us
    all_to_all x1, waiting for transfers between devices, shards(): lax.all_to_all(outgoing, DEV, split_axis=1, concat_axis=1, tiled=True)  10.4 us
    all_to_all x1, starting transfers between devices, shards(): lax.all_to_all(outgoing, DEV, split_axis=1, concat_axis=1, tiled=True)  10.2 us
    pallas_call x1, Pallas kernels, box_sum(): pl.pallas_call(box_sum_kernel, grid=(slots // tile,), in_specs=[pl.BlockS...  8.59 us
  transfers between devices with their start and end apart: 13, of which 6 were waited for; matrix products, arithmetic and copies ran while one was open for 1% of the time, Pallas kernels for 0%

profile of v9, /device:TPU:8, one launch (start us, length us, event | category | flops | bytes accessed | tf_op | source)
XLA Modules:
  0.0 186.7 jit_solution(17691462682712913905)
XLA Ops:
  0.7 1.2 copy-done
  1.9 2.7 %multiply_convert_fusion.1 = (bf16[4096,128]{1,0:T(8,128)(2,1)S(1)}, f32[4096,128]{1,0:T(8,128)}) fusion(bf16[4096,128]{1,0:T(8,128)(2,1)S(1)} %copy-done, bf16[128,128]{1,0:T(8,128)(2,1)} %param.16), kind=kOutput, calls=%fused_computation.8 | convolution fusion | flops 136839168 | bytes 4227072 | tf_op jit(solution)/shard_map/dot_general | solution.py:445
  4.6 0.2 fusion.68
  4.8 2.0 %multiply_reduce_fusion.1 = (f32[4096]{0:T(1024)S(1)}, f32[4096,128]{1,0:T(8,128)}) fusion(f32[128]{0:T(128)S(1)} %copy-done.11, bf16[4096,128]{1,0:T(8,128)(2,1)S(1)} %get-tuple-element.29, bf16[128,128]{1,0:T(8,128)(2,1)S(1)} %copy-done.13), kind=kOutput, calls=%fused_computation.5 | convolution fusion | flops 137359360 | bytes 3195392 | tf_op jit(solution)/shard_map/dot_general | solution.py:447
  7.1 0.6 copy.78
  7.7 0.6 copy.79
  8.4 0.6 copy.80
  9.0 0.7 pad_maximum_fusion.1.table_ref
  9.7 5.3 %shard_map.164 = f32[5,8192]{1,0:T(8,128)} custom-call(bf16[768,64]{1,0:T(8,128)(2,1)} %pad_maximum_fusion.1.table_ref, s32[1,8192]{1,0:T(1,128)} %bitcast.196, s32[1,8192]{1,0:T(1,128)} %bitcast.198, s32[1,8192]{1,0:T(1,128)} %bitcast.200), custom_call_target="tpu_custom_call" | custom-call | tf_op jit(solution)/shard_map/pallas_call | solution.py:215
  15.0 10.2 %all-to-all-start = ((f32[5,32,256]{2,0,1:T(8,128)}), f32[5,32,256]{2,0,1:T(8,128)S(1)}, u32[]{:S(2)}, u32[]{:S(2)}) async-start(f32[5,32,256]{2,0,1:T(8,128)} %bitcast.188), calls=%async_computation | async-start | bytes 524288 | tf_op jit(solution)/shard_map/all_to_all | solution.py:462
  25.3 0.4 copy.44
  25.8 0.7 gather_fusion
  27.0 10.4 %all-to-all-done = f32[5,32,256]{2,0,1:T(8,128)S(1)} async-done(((f32[5,32,256]{2,0,1:T(8,128)}), f32[5,32,256]{2,0,1:T(8,128)S(1)}, u32[]{:S(2)}, u32[]{:S(2)}) %all-to-all-start) | async-done | bytes 163872 | tf_op jit(solution)/shard_map/all_to_all | solution.py:462
  37.4 0.7 copy-done.1
  38.1 8.6 %shard_map.165 = f32[128,1024]{1,0:T(8,128)} custom-call(f32[5,8192]{1,0:T(8,128)} %bitcast.186), custom_call_target="tpu_custom_call" | custom-call | tf_op jit(solution)/shard_map/pallas_call | solution.py:322
  46.6 1.1 slice_add_fusion
  47.7 0.3 reshape.420
  48.1 0.5 convolution_bitcast_fusion.7
  48.6 1.3 collective-permute-start.7
  49.9 1.3 collective-permute-start.5
  51.2 6.4 %collective-permute-start.2 = (f32[16,2,2,64]{3,0,2,1:T(8,128)S(1)}, f32[16,2,2,64]{3,0,2,1:T(8,128)S(1)}, u32[]{:S(2)}, u32[]{:S(2)}) collective-permute-start(f32[16,2,2,64]{3,0,2,1:T(8,128)S(1)} %get-tuple-element.19), channel_id=1, source_target_pairs={{1,32},{2,33},{3,34},{4,35},{5,36},{6,37},{7,38},{8,39},{9,40},{10... | collective-permute-start | bytes 49160 | tf_op jit(solution)/shard_map/ppermute | solution.py:69
  57.6 1.3 collective-permute-start.6
  58.9 1.9 %collective-permute-start.4 = (f32[16,4,2,64]{3,0,2,1:T(8,128)S(1)}, f32[16,4,2,64]{3,0,2,1:T(8,128)S(1)}, u32[]{:S(2)}, u32[]{:S(2)}) collective-permute-start(f32[16,4,2,64]{3,0,2,1:T(8,128)S(1)} %get-tuple-element.23), channel_id=1, source_target_pairs={{1,0},{2,1},{3,2},{4,3},{5,4},{6,5},{7,6},{8,7},{9,8},{10,9},{11,1... | collective-permute-start | bytes 98312 | tf_op jit(solution)/shard_map/ppermute | solution.py:69
  60.9 3.9 %collective-permute-start.3 = (f32[16,4,2,64]{3,0,2,1:T(8,128)S(1)}, f32[16,4,2,64]{3,0,2,1:T(8,128)S(1)}, u32[]{:S(2)}, u32[]{:S(2)}) collective-permute-start(f32[16,4,2,64]{3,0,2,1:T(8,128)S(1)} %get-tuple-element.22), channel_id=1, source_target_pairs={{0,1},{1,2},{2,3},{3,4},{4,5},{5,6},{6,7},{7,8},{8,9},{9,10},{10,1... | collective-permute-start | bytes 98312 | tf_op jit(solution)/shard_map/ppermute | solution.py:69
  64.8 5.4 %collective-permute-start.1 = (f32[16,2,4,64]{3,0,2,1:T(8,128)S(1)}, f32[16,2,4,64]{3,0,2,1:T(8,128)S(1)}, u32[]{:S(2)}, u32[]{:S(2)}) collective-permute-start(f32[16,2,4,64]{3,0,2,1:T(8,128)S(1)} %get-tuple-element.20), channel_id=1, source_target_pairs={{0,32},{32,64},{64,96},{96,128},{128,160},{160,192},{192,224},{224... | collective-permute-start | bytes 98312 | tf_op jit(solution)/shard_map/ppermute | solution.py:69
  70.2 4.0 %collective-permute-start = (f32[16,2,2,64]{3,0,2,1:T(8,128)S(1)}, f32[16,2,2,64]{3,0,2,1:T(8,128)S(1)}, u32[]{:S(2)}, u32[]{:S(2)}) collective-permute-start(f32[16,2,2,64]{3,0,2,1:T(8,128)S(1)} %get-tuple-element.16), channel_id=1, source_target_pairs={{0,33},{1,34},{2,35},{3,36},{4,37},{5,38},{6,39},{7,40},{8,41},{9,... | collective-permute-start | bytes 49160 | tf_op jit(solution)/shard_map/ppermute | solution.py:69
  74.3 1.3 collective-permute-done
  75.6 1.2 convolution_bitcast_fusion
  76.8 1.3 convolution_bitcast_fusion.5
  78.1 1.3 convolution_bitcast_fusion.4
  79.4 1.3 convolution_bitcast_fusion.3
  80.7 1.3 convolution_bitcast_fusion.2
  82.0 1.3 convolution_bitcast_fusion.1
  83.3 1.0 fusion.13
  84.4 1.0 fusion.40
  85.4 1.0 fusion.37
  86.4 1.0 fusion.34
  87.5 1.2 fusion.31
  88.7 0.2 reshape.421
  88.9 0.4 reduce-precision_convert_fusion
  89.3 0.7 pad_maximum_fusion.table_ref
  90.0 6.7 %shard_map.166 = f32[1,8192]{1,0:T(1,128)} custom-call(bf16[128,1024]{1,0:T(8,128)(2,1)} %pad_maximum_fusion.table_ref, f32[5,8192]{1,0:T(8,128)} %bitcast.187), custom_call_target="tpu_custom_call" | custom-call | tf_op jit(solution)/shard_map/pallas_call | solution.py:345
  96.8 18.0 %all_to_all.29 = f32[32,1,256]{2,1,0:T(1,128)} all-to-all(f32[32,1,256]{2,1,0:T(1,128)} %bitcast.201), channel_id=1, replica_groups=mesh['grp_0'=8,'grp_1'=2,'dev_0'=8,'dev_1'=4] {'dev_0','dev_1'}, dimensions={0} | all-to-all | bytes 65536 | tf_op jit(solution)/shard_map/all_to_all | solution.py:471
  114.7 2.4 %shard_map.167 = f32[192,64]{1,0:T(8,128)} custom-call(f32[1,8192]{1,0:T(1,128)} %bitcast.202, s32[1,8192]{1,0:T(1,128)} %bitcast.197, s32[1,8192]{1,0:T(1,128)} %bitcast.199), custom_call_target="tpu_custom_call" | custom-call | tf_op jit(solution)/shard_map/pallas_call | solution.py:257
  117.2 0.8 slice_add_fusion.1
  118.1 0.2 fusion.46
  118.3 2.4 %multiply_convert_fusion = (bf16[4096,128]{1,0:T(8,128)(2,1)S(1)}, f32[128]{0:T(128)S(1)}) fusion(f32[4096,128]{1,0:T(8,128)} %get-tuple-element.32, f32[4096]{0:T(1024)S(1)} %reshape.422, f32[128]{0:T(128)S(1)} %copy-done.11), kind=kLoop, calls=%fused_computation.4 | loop fusion | flops 6815616 | bytes 3163136 | tf_op jit(solution)/shard_map/convert_element_type | solution.py:475
  120.8 0.5 fusion.43
  121.3 2.6 %fusion.45 = f32[128,128]{0,1:T(8,128)S(1)} fusion(bf16[4096,128]{1,0:T(8,128)(2,1)S(1)} %copy-done, bf16[4096,128]{1,0:T(8,128)(2,1)S(1)} %get-tuple-element.5, bf16[128,128]{1,0:T(8,128)(2,1)S(1)} %copy-done.13, f32[4096,128]{1,0:T(8,128)} %get-tuple-element.30), kind=kOutput, calls=%fused_computation.47 | convolution fusion | flops 273170432 | bytes 4292608 | tf_op jit(solution)/shard_map/dot_general | solution.py:487
  124.0 3.3 %collective-permute-start.8 = (f32[32902]{0:T(1024)S(1)}, f32[32902]{0:T(1024)S(1)}, u32[]{:S(2)}, u32[]{:S(2)}) collective-permute-start(f32[32902]{0:T(1024)S(1)} %pad_maximum_fusion.2), channel_id=1, source_target_pairs={{0,32},{32,0},{1,33},{33,1},{2,34},{34,2},{3,35},{35,3},{4,36},{36... | collective-permute-start | bytes 394832 | tf_op jit(solution)/shard_map/ppermute | solution.py:151
  127.3 1.0 collective-permute-done.8
  128.3 0.2 all_to_all.22
  128.6 14.8 %all_to_all.30 = f32[32,1,1029]{2,1,0:T(1,128)S(1)} all-to-all(f32[32,1,1029]{2,1,0:T(1,128)S(1)} %all_to_all.22), channel_id=1, replica_groups=mesh['grp_0'=8,'grp_1'=2,'dev_0'=8,'dev_1'=4] {'dev_0','dev_1'}, dimensions={0} | all-to-all | bytes 263424 | tf_op jit(solution)/shard_map/all_to_all | solution.py:167
  143.5 4.6 %collective-permute-start.9 = (f32[1029]{0:T(1024)S(1)}, f32[1029]{0:T(1024)S(1)}, u32[]{:S(2)}, u32[]{:S(2)}) collective-permute-start(f32[1029]{0:T(1024)S(1)} %reduce_sum.29), channel_id=1, source_target_pairs={{0,64},{64,0},{128,192},{192,128},{256,320},{320,256},{384,448},{4... | collective-permute-start | bytes 12356 | tf_op jit(solution)/shard_map/ppermute | solution.py:151
  148.0 1.6 collective-permute-done.9
  149.6 8.2 %collective-permute-start.10 = (f32[1029]{0:T(1024)S(1)}, f32[1029]{0:T(1024)S(1)}, u32[]{:S(2)}, u32[]{:S(2)}) collective-permute-start(f32[1029]{0:T(1024)S(1)} %add.203), channel_id=1, source_target_pairs={{0,128},{64,192},{128,0},{192,64},{256,384},{320,448},{384,256},{4... | collective-permute-start | bytes 12356 | tf_op jit(solution)/shard_map/ppermute | solution.py:151
  157.9 1.6 collective-permute-done.10
  159.5 9.4 %collective-permute-start.11 = (f32[1029]{0:T(1024)S(1)}, f32[1029]{0:T(1024)S(1)}, u32[]{:S(2)}, u32[]{:S(2)}) collective-permute-start(f32[1029]{0:T(1024)S(1)} %add.204), channel_id=1, source_target_pairs={{0,256},{64,320},{128,384},{192,448},{256,0},{320,64},{384,128},{4... | collective-permute-start | bytes 12356 | tf_op jit(solution)/shard_map/ppermute | solution.py:151
  168.9 1.6 collective-permute-done.11
  170.6 13.9 %all_to_all.31 = f32[32,1,1029]{2,1,0:T(1,128)S(1)} all-to-all(f32[32,1,1029]{2,1,0:T(1,128)S(1)} %broadcast_in_dim.10), channel_id=1, replica_groups=mesh['grp_0'=8,'grp_1'=2,'dev_0'=8,'dev_1'=4] {'dev_0','dev_1'}, dimensions={0} | all-to-all | bytes 263424 | tf_op jit(solution)/shard_map/all_to_all | solution.py:170
  184.5 0.3 reduce.1
  185.0 0.7 slice_bitcast_fusion.10
  185.6 0.5 slice.149
  186.1 0.5 slice.150
  (79 shorter events, 1.5 us)
Async XLA Ops:
  0.6 1.2 copy-start
  0.6 3.9 %copy-start.14 = (s32[4096]{0:T(1024)S(1)}, s32[4096]{0:T(1024)}, u32[]{:S(2)}) copy-start(s32[4096]{0:T(1024)} %param.15) | copy-start | bytes 49156
  0.7 3.9 %copy-start.15 = (f32[6]{0:T(128)S(1)}, f32[6]{0:T(128)}, u32[]{:S(2)}) copy-start(f32[6]{0:T(128)} %param.19) | copy-start | bytes 76
  0.7 4.1 %copy-start.11 = (f32[128]{0:T(128)S(1)}, f32[128]{0:T(128)}, u32[]{:S(2)}) copy-start(f32[128]{0:T(128)} %param.18) | copy-start | bytes 1540
  0.7 4.1 %copy-start.13 = (bf16[128,128]{1,0:T(8,128)(2,1)S(1)}, bf16[128,128]{1,0:T(8,128)(2,1)}, u32[]{:S(2)}) copy-start(bf16[128,128]{1,0:T(8,128)(2,1)} %param.17) | copy-start | bytes 98308
  4.6 2.2 %copy-start.2 = (bf16[4096,128]{1,0:T(8,128)(2,1)}, bf16[4096,128]{1,0:T(8,128)(2,1)S(1)}, u32[]{:S(2)}) copy-start(bf16[4096,128]{1,0:T(8,128)(2,1)S(1)} %get-tuple-element.29) | copy-start | bytes 3145732
  4.8 2.0 %copy-start.6 = (f32[3,4096]{1,0:T(4,128)S(1)}, f32[3,4096]{1,0:T(4,128)}, u32[]{:S(2)}) copy-start(f32[3,4096]{1,0:T(4,128)} %param.14) | copy-start | bytes 147460
  4.8 2.2 %copy-start.7 = (s32[32,256]{1,0:T(8,128)S(1)}, s32[32,256]{1,0:T(8,128)}, u32[]{:S(2)}) copy-start(s32[32,256]{1,0:T(8,128)} %param.23) | copy-start | bytes 98308
  4.8 3.6 %copy-start.8 = (s32[32,256]{1,0:T(8,128)S(1)}, s32[32,256]{1,0:T(8,128)}, u32[]{:S(2)}) copy-start(s32[32,256]{1,0:T(8,128)} %param.24) | copy-start | bytes 98308
  6.8 18.5 %copy-start.4 = (f32[98,16,16]{0,2,1:T(8,128)S(1)}, f32[98,16,16]{0,2,1:T(8,128)}, u32[]{:S(2)}) copy-start(f32[98,16,16]{0,2,1:T(8,128)} %param.20) | copy-start | bytes 301060
  6.8 18.9 %copy-start.12 = (s32[125]{0:T(128)S(1)}, s32[125]{0:T(128)}, u32[]{:S(2)}) copy-start(s32[125]{0:T(128)} %constant.75) | copy-start | bytes 1504
  15.0 22.3 %all-to-all-start = ((f32[5,32,256]{2,0,1:T(8,128)}), f32[5,32,256]{2,0,1:T(8,128)S(1)}, u32[]{:S(2)}, u32[]{:S(2)}) async-start(f32[5,32,256]{2,0,1:T(8,128)} %bitcast.188), calls=%async_computation | async-start | bytes 524288 | tf_op jit(solution)/shard_map/all_to_all | solution.py:462
  26.9 21.2 %copy-start.9 = (f32[64,16]{0,1:T(8,128)S(1)}, f32[64,16]{0,1:T(8,128)}, u32[]{:S(2)}) copy-start(f32[64,16]{0,1:T(8,128)} %param.22) | copy-start | bytes 12292
  37.4 0.7 copy-start.1
  48.6 12.2 %collective-permute-start.7 = (f32[16,2,2,64]{3,0,2,1:T(8,128)S(1)}, f32[16,2,2,64]{3,0,2,1:T(8,128)S(1)}, u32[]{:S(2)}, u32[]{:S(2)}) collective-permute-start(f32[16,2,2,64]{3,0,2,1:T(8,128)S(1)} %get-tuple-element.17), channel_id=1, source_target_pairs={{33,0},{34,1},{35,2},{36,3},{37,4},{38,5},{39,6},{40,7},{41,8},{42... | collective-permute-start | bytes 49160 | tf_op jit(solution)/shard_map/ppermute | solution.py:69
  49.9 14.9 %collective-permute-start.5 = (f32[16,2,2,64]{3,0,2,1:T(8,128)S(1)}, f32[16,2,2,64]{3,0,2,1:T(8,128)S(1)}, u32[]{:S(2)}, u32[]{:S(2)}) collective-permute-start(f32[16,2,2,64]{3,0,2,1:T(8,128)S(1)} %get-tuple-element.18), channel_id=1, source_target_pairs={{32,1},{33,2},{34,3},{35,4},{36,5},{37,6},{38,7},{39,8},{40,9},{41... | collective-permute-start | bytes 49160 | tf_op jit(solution)/shard_map/ppermute | solution.py:69
  51.2 18.9 %collective-permute-start.2 = (f32[16,2,2,64]{3,0,2,1:T(8,128)S(1)}, f32[16,2,2,64]{3,0,2,1:T(8,128)S(1)}, u32[]{:S(2)}, u32[]{:S(2)}) collective-permute-start(f32[16,2,2,64]{3,0,2,1:T(8,128)S(1)} %get-tuple-element.19), channel_id=1, source_target_pairs={{1,32},{2,33},{3,34},{4,35},{5,36},{6,37},{7,38},{8,39},{9,40},{10... | collective-permute-start | bytes 49160 | tf_op jit(solution)/shard_map/ppermute | solution.py:69
  57.6 18.0 %collective-permute-start.6 = (f32[16,2,4,64]{3,0,2,1:T(8,128)S(1)}, f32[16,2,4,64]{3,0,2,1:T(8,128)S(1)}, u32[]{:S(2)}, u32[]{:S(2)}) collective-permute-start(f32[16,2,4,64]{3,0,2,1:T(8,128)S(1)} %get-tuple-element.21), channel_id=1, source_target_pairs={{32,0},{64,32},{96,64},{128,96},{160,128},{192,160},{224,192},{256... | collective-permute-start | bytes 98312 | tf_op jit(solution)/shard_map/ppermute | solution.py:69
  58.9 16.7 %collective-permute-start.4 = (f32[16,4,2,64]{3,0,2,1:T(8,128)S(1)}, f32[16,4,2,64]{3,0,2,1:T(8,128)S(1)}, u32[]{:S(2)}, u32[]{:S(2)}) collective-permute-start(f32[16,4,2,64]{3,0,2,1:T(8,128)S(1)} %get-tuple-element.23), channel_id=1, source_target_pairs={{1,0},{2,1},{3,2},{4,3},{5,4},{6,5},{7,6},{8,7},{9,8},{10,9},{11,1... | collective-permute-start | bytes 98312 | tf_op jit(solution)/shard_map/ppermute | solution.py:69
  60.9 14.7 %collective-permute-start.3 = (f32[16,4,2,64]{3,0,2,1:T(8,128)S(1)}, f32[16,4,2,64]{3,0,2,1:T(8,128)S(1)}, u32[]{:S(2)}, u32[]{:S(2)}) collective-permute-start(f32[16,4,2,64]{3,0,2,1:T(8,128)S(1)} %get-tuple-element.22), channel_id=1, source_target_pairs={{0,1},{1,2},{2,3},{3,4},{4,5},{5,6},{6,7},{7,8},{8,9},{9,10},{10,1... | collective-permute-start | bytes 98312 | tf_op jit(solution)/shard_map/ppermute | solution.py:69
  64.8 10.8 %collective-permute-start.1 = (f32[16,2,4,64]{3,0,2,1:T(8,128)S(1)}, f32[16,2,4,64]{3,0,2,1:T(8,128)S(1)}, u32[]{:S(2)}, u32[]{:S(2)}) collective-permute-start(f32[16,2,4,64]{3,0,2,1:T(8,128)S(1)} %get-tuple-element.20), channel_id=1, source_target_pairs={{0,32},{32,64},{64,96},{96,128},{128,160},{160,192},{192,224},{224... | collective-permute-start | bytes 98312 | tf_op jit(solution)/shard_map/ppermute | solution.py:69
  70.2 5.4 %collective-permute-start = (f32[16,2,2,64]{3,0,2,1:T(8,128)S(1)}, f32[16,2,2,64]{3,0,2,1:T(8,128)S(1)}, u32[]{:S(2)}, u32[]{:S(2)}) collective-permute-start(f32[16,2,2,64]{3,0,2,1:T(8,128)S(1)} %get-tuple-element.16), channel_id=1, source_target_pairs={{0,33},{1,34},{2,35},{3,36},{4,37},{5,38},{6,39},{7,40},{8,41},{9,... | collective-permute-start | bytes 49160 | tf_op jit(solution)/shard_map/ppermute | solution.py:69
  85.4 3.5 %copy-start.10 = (f32[64,16]{0,1:T(8,128)S(1)}, f32[64,16]{0,1:T(8,128)}, u32[]{:S(2)}) copy-start(f32[64,16]{0,1:T(8,128)} %param.21) | copy-start | bytes 12292
  90.0 30.8 %copy-start.3 = (bf16[4096,128]{1,0:T(8,128)(2,1)S(1)}, bf16[4096,128]{1,0:T(8,128)(2,1)}, u32[]{:S(2)}) copy-start(bf16[4096,128]{1,0:T(8,128)(2,1)} %copy-done.2) | copy-start | bytes 3145732
  118.0 3.2 %copy-start.5 = (f32[4096]{0:T(1024)}, f32[4096]{0:T(1024)S(1)}, u32[]{:S(2)}) copy-start(f32[4096]{0:T(1024)S(1)} %reshape.422) | copy-start | bytes 49156
  124.0 4.3 %collective-permute-start.8 = (f32[32902]{0:T(1024)S(1)}, f32[32902]{0:T(1024)S(1)}, u32[]{:S(2)}, u32[]{:S(2)}) collective-permute-start(f32[32902]{0:T(1024)S(1)} %pad_maximum_fusion.2), channel_id=1, source_target_pairs={{0,32},{32,0},{1,33},{33,1},{2,34},{34,2},{3,35},{35,3},{4,36},{36... | collective-permute-start | bytes 394832 | tf_op jit(solution)/shard_map/ppermute | solution.py:151
  143.5 6.2 %collective-permute-start.9 = (f32[1029]{0:T(1024)S(1)}, f32[1029]{0:T(1024)S(1)}, u32[]{:S(2)}, u32[]{:S(2)}) collective-permute-start(f32[1029]{0:T(1024)S(1)} %reduce_sum.29), channel_id=1, source_target_pairs={{0,64},{64,0},{128,192},{192,128},{256,320},{320,256},{384,448},{4... | collective-permute-start | bytes 12356 | tf_op jit(solution)/shard_map/ppermute | solution.py:151
  149.6 9.8 %collective-permute-start.10 = (f32[1029]{0:T(1024)S(1)}, f32[1029]{0:T(1024)S(1)}, u32[]{:S(2)}, u32[]{:S(2)}) collective-permute-start(f32[1029]{0:T(1024)S(1)} %add.203), channel_id=1, source_target_pairs={{0,128},{64,192},{128,0},{192,64},{256,384},{320,448},{384,256},{4... | collective-permute-start | bytes 12356 | tf_op jit(solution)/shard_map/ppermute | solution.py:151
  159.5 11.0 %collective-permute-start.11 = (f32[1029]{0:T(1024)S(1)}, f32[1029]{0:T(1024)S(1)}, u32[]{:S(2)}, u32[]{:S(2)}) collective-permute-start(f32[1029]{0:T(1024)S(1)} %add.204), channel_id=1, source_target_pairs={{0,256},{64,320},{128,384},{192,448},{256,0},{320,64},{384,128},{4... | collective-permute-start | bytes 12356 | tf_op jit(solution)/shard_map/ppermute | solution.py:151

commit v10 on v7

--- a/solution.py
+++ b/solution.py
@@ -157,7 +157,7 @@
         )
 
 
-def atoms_to_slots(values, high, low, box, tile=4096):
+def atoms_to_slots(values, high, low, box, tile=8192):
     rows, count = values.shape
     side = int(round(math.sqrt(count)))
     table = pieces_bf16(values.reshape(rows * side, side), 0)

time: 176 us -> 176 us (level)
  no operation moved by 1% of the time
where the time goes in v10:
time: 176 us; the launch traced here: 175 us
  starting transfers between devices  45.4 us (26%)
  blocking collectives  43.9 us (25%)
  Pallas kernels  22.8 us (13%)
  waiting for transfers between devices  22.4 us (13%)
  matrix products  22.2 us (13%)
  local copies, waits for them, and re-layouts  10 us (6%)
  other arithmetic  6.79 us (4%)
    ppermute x4, starting transfers between devices, swapped(): return lax.ppermute(x, axis, [(i, i ^ step) for i in range(count)])  24.9 us
    all_to_all x1, blocking collectives, shards(): lax.all_to_all(slot_potential, DEV, split_axis=0, concat_axis=0, tiled=True)  15.5 us
    all_to_all x1, blocking collectives, hybrid_sum(): lax.all_to_all(lines, plane, 0, 0, tiled=True).reshape(peers, -1)  14.5 us
    all_to_all x1, blocking collectives, hybrid_sum(): return lax.all_to_all(copies, plane, 0, 0, tiled=True).reshape(-1)[:length]  13.9 us
    all_to_all x1, starting transfers between devices, shards(): lax.all_to_all(outgoing, DEV, split_axis=1, concat_axis=1, tiled=True)  10.2 us
    all_to_all x1, waiting for transfers between devices, shards(): lax.all_to_all(outgoing, DEV, split_axis=1, concat_axis=1, tiled=True)  8.63 us
    pallas_call x1, Pallas kernels, box_sum(): pl.pallas_call(box_sum_kernel, grid=(slots // tile,), in_specs=[pl.BlockS...  8.6 us
    ppermute x2, waiting for transfers between devices, extended_2(): lax.ppermute(tail, axis, [(i, (i + 1) % count) for i in range(ends)])  6.85 us
  transfers between devices with their start and end apart: 9, of which 8 were waited for; matrix products, arithmetic and copies ran while one was open for 1% of the time, Pallas kernels for 0%

profile of v10, /device:TPU:8, one launch (start us, length us, event | category | flops | bytes accessed | tf_op | source)
XLA Modules:
  0.0 174.8 jit_solution(17750894393071164029)
XLA Ops:
  0.7 1.2 copy-done
  1.9 2.7 %multiply_convert_fusion.1 = (bf16[4096,128]{1,0:T(8,128)(2,1)S(1)}, f32[4096,128]{1,0:T(8,128)}) fusion(bf16[4096,128]{1,0:T(8,128)(2,1)S(1)} %copy-done, bf16[128,128]{1,0:T(8,128)(2,1)} %param.16), kind=kOutput, calls=%fused_computation.8 | convolution fusion | flops 136839168 | bytes 4227072 | tf_op jit(solution)/shard_map/dot_general | solution.py:395
  4.6 0.2 fusion.60
  4.9 2.0 %multiply_reduce_fusion.1 = (f32[4096]{0:T(1024)S(1)}, f32[4096,128]{1,0:T(8,128)}) fusion(f32[128]{0:T(128)S(1)} %copy-done.17, bf16[4096,128]{1,0:T(8,128)(2,1)S(1)} %get-tuple-element.25, bf16[128,128]{1,0:T(8,128)(2,1)S(1)} %copy-done.20), kind=kOutput, calls=%fused_computation.5 | convolution fusion | flops 137359360 | bytes 3195392 | tf_op jit(solution)/shard_map/dot_general | solution.py:397
  7.1 0.6 copy.78
  7.8 0.6 copy.79
  8.4 0.6 copy.80
  9.1 0.7 pad_maximum_fusion.2.table_ref
  9.8 5.1 %shard_map.164 = f32[5,8192]{1,0:T(8,128)} custom-call(bf16[768,64]{1,0:T(8,128)(2,1)} %pad_maximum_fusion.2.table_ref, s32[1,8192]{1,0:T(1,128)} %bitcast.196, s32[1,8192]{1,0:T(1,128)} %bitcast.198, s32[1,8192]{1,0:T(1,128)} %bitcast.200), custom_call_target="tpu_custom_call" | custom-call | tf_op jit(solution)/shard_map/pallas_call | solution.py:165
  14.9 10.2 %all-to-all-start = ((f32[5,32,256]{2,0,1:T(8,128)}), f32[5,32,256]{2,0,1:T(8,128)S(1)}, u32[]{:S(2)}, u32[]{:S(2)}) async-start(f32[5,32,256]{2,0,1:T(8,128)} %bitcast.188), calls=%async_computation | async-start | bytes 524288 | tf_op jit(solution)/shard_map/all_to_all | solution.py:412
  25.2 0.4 copy.44
  26.0 0.4 copy-done.11
  26.4 0.6 copy-done.9
  27.0 0.7 gather_fusion
  27.7 0.9 fusion.83
  28.6 8.6 %all-to-all-done = f32[5,32,256]{2,0,1:T(8,128)S(1)} async-done(((f32[5,32,256]{2,0,1:T(8,128)}), f32[5,32,256]{2,0,1:T(8,128)S(1)}, u32[]{:S(2)}, u32[]{:S(2)}) %all-to-all-start) | async-done | bytes 163872 | tf_op jit(solution)/shard_map/all_to_all | solution.py:412
  37.2 0.7 copy-done.1
  37.9 8.6 %shard_map.165 = f32[128,1024]{1,0:T(8,128)} custom-call(f32[5,8192]{1,0:T(8,128)} %bitcast.186), custom_call_target="tpu_custom_call" | custom-call | tf_op jit(solution)/shard_map/pallas_call | solution.py:272
  46.5 1.1 slice_add_fusion
  47.6 0.3 reshape.420
  48.0 0.5 convolution_bitcast_fusion.7
  48.5 1.3 collective-permute-start.1
  49.8 3.0 %collective-permute-start = (f32[16,2,4,64]{3,0,2,1:T(8,128)S(1)}, f32[16,2,4,64]{3,0,2,1:T(8,128)S(1)}, u32[]{:S(2)}, u32[]{:S(2)}) collective-permute-start(f32[16,2,4,64]{3,0,2,1:T(8,128)S(1)} %get-tuple-element.18), channel_id=1, source_target_pairs={{0,32},{32,64},{64,96},{96,128},{128,160},{160,192},{192,224},{224... | collective-permute-start | bytes 98312 | tf_op jit(solution)/shard_map/ppermute | solution.py:33
  52.9 0.8 collective-permute-done
  53.8 3.7 %collective-permute-start.3 = (f32[16,8,2,64]{3,0,2,1:T(8,128)S(1)}, f32[16,8,2,64]{3,0,2,1:T(8,128)S(1)}, u32[]{:S(2)}, u32[]{:S(2)}) collective-permute-start(f32[16,8,2,64]{3,0,2,1:T(8,128)S(1)} %get-tuple-element.15), channel_id=1, source_target_pairs={{1,0},{2,1},{3,2},{4,3},{5,4},{6,5},{7,6},{8,7},{9,8},{10,9},{11,1... | collective-permute-start | bytes 196616 | tf_op jit(solution)/shard_map/ppermute | solution.py:35
  57.5 2.4 %collective-permute-start.2 = (f32[16,8,2,64]{3,0,2,1:T(8,128)S(1)}, f32[16,8,2,64]{3,0,2,1:T(8,128)S(1)}, u32[]{:S(2)}, u32[]{:S(2)}) collective-permute-start(f32[16,8,2,64]{3,0,2,1:T(8,128)S(1)} %get-tuple-element.14), channel_id=1, source_target_pairs={{0,1},{1,2},{2,3},{3,4},{4,5},{5,6},{6,7},{7,8},{8,9},{9,10},{10,1... | collective-permute-start | bytes 196616 | tf_op jit(solution)/shard_map/ppermute | solution.py:33
  59.9 0.7 collective-permute-done.3
  60.7 6.0 %collective-permute-done.2 = f32[16,8,2,64]{3,0,2,1:T(8,128)S(1)} collective-permute-done((f32[16,8,2,64]{3,0,2,1:T(8,128)S(1)}, f32[16,8,2,64]{3,0,2,1:T(8,128)S(1)}, u32[]{:S(2)}, u32[]{:S(2)}) %collective-permute-start.2) | collective-permute-done | bytes 65568 | tf_op jit(solution)/shard_map/ppermute | solution.py:33
  66.7 1.2 convolution_bitcast_fusion
  67.8 1.3 convolution_bitcast_fusion.5
  69.2 1.3 convolution_bitcast_fusion.4
  70.5 1.3 convolution_bitcast_fusion.3
  71.8 1.3 convolution_bitcast_fusion.2
  73.1 1.3 convolution_bitcast_fusion.1
  74.4 1.0 fusion.13
  75.4 1.0 fusion.40
  76.5 1.0 fusion.37
  77.5 1.0 fusion.34
  78.6 1.2 fusion.31
  80.0 0.4 reduce-precision_convert_fusion
  80.4 0.7 pad_maximum_fusion.1.table_ref
  81.1 6.7 %shard_map.166 = f32[1,8192]{1,0:T(1,128)} custom-call(bf16[128,1024]{1,0:T(8,128)(2,1)} %pad_maximum_fusion.1.table_ref, f32[5,8192]{1,0:T(8,128)} %bitcast.187), custom_call_target="tpu_custom_call" | custom-call | tf_op jit(solution)/shard_map/pallas_call | solution.py:295
  87.9 15.5 %all_to_all.29 = f32[32,1,256]{2,1,0:T(1,128)} all-to-all(f32[32,1,256]{2,1,0:T(1,128)} %bitcast.201), channel_id=1, replica_groups=mesh['grp_0'=8,'grp_1'=2,'dev_0'=8,'dev_1'=4] {'dev_0','dev_1'}, dimensions={0} | all-to-all | bytes 65536 | tf_op jit(solution)/shard_map/all_to_all | solution.py:421
  103.4 2.4 %shard_map.167 = f32[192,64]{1,0:T(8,128)} custom-call(f32[1,8192]{1,0:T(1,128)} %bitcast.202, s32[1,8192]{1,0:T(1,128)} %bitcast.197, s32[1,8192]{1,0:T(1,128)} %bitcast.199), custom_call_target="tpu_custom_call" | custom-call | tf_op jit(solution)/shard_map/pallas_call | solution.py:207
  105.8 0.8 slice_add_fusion.1
  106.8 0.2 fusion.46
  107.0 2.4 %multiply_convert_fusion = (bf16[4096,128]{1,0:T(8,128)(2,1)S(1)}, f32[128]{0:T(128)S(1)}) fusion(f32[4096,128]{1,0:T(8,128)} %get-tuple-element.28, f32[4096]{0:T(1024)S(1)} %reshape.422, f32[128]{0:T(128)S(1)} %copy-done.18), kind=kLoop, calls=%fused_computation.4 | loop fusion | flops 6815616 | bytes 3163136 | tf_op jit(solution)/shard_map/convert_element_type | solution.py:425
  109.5 0.5 fusion.43
  110.0 2.6 %fusion.45 = f32[128,128]{0,1:T(8,128)S(1)} fusion(bf16[4096,128]{1,0:T(8,128)(2,1)S(1)} %copy-done, bf16[4096,128]{1,0:T(8,128)(2,1)S(1)} %get-tuple-element.5, bf16[128,128]{1,0:T(8,128)(2,1)S(1)} %copy-done.21, f32[4096,128]{1,0:T(8,128)} %get-tuple-element.26), kind=kOutput, calls=%fused_computation.47 | convolution fusion | flops 273170432 | bytes 4292608 | tf_op jit(solution)/shard_map/dot_general | solution.py:437
  112.7 1.9 %collective-permute-start.4 = (f32[32902]{0:T(1024)S(1)}, f32[32902]{0:T(1024)S(1)}, u32[]{:S(2)}, u32[]{:S(2)}) collective-permute-start(f32[32902]{0:T(1024)S(1)} %pad_maximum_fusion.3), channel_id=1, source_target_pairs={{0,32},{32,0},{1,33},{33,1},{2,34},{34,2},{3,35},{35,3},{4,36},{36... | collective-permute-start | bytes 394832 | tf_op jit(solution)/shard_map/ppermute | solution.py:101
  114.7 1.3 collective-permute-done.4
  116.0 0.2 all_to_all.22
  116.3 14.5 %all_to_all.30 = f32[32,1,1029]{2,1,0:T(1,128)S(1)} all-to-all(f32[32,1,1029]{2,1,0:T(1,128)S(1)} %all_to_all.22), channel_id=1, replica_groups=mesh['grp_0'=8,'grp_1'=2,'dev_0'=8,'dev_1'=4] {'dev_0','dev_1'}, dimensions={0} | all-to-all | bytes 263424 | tf_op jit(solution)/shard_map/all_to_all | solution.py:117
  130.9 6.6 %collective-permute-start.5 = (f32[1029]{0:T(1024)S(1)}, f32[1029]{0:T(1024)S(1)}, u32[]{:S(2)}, u32[]{:S(2)}) collective-permute-start(f32[1029]{0:T(1024)S(1)} %reduce_sum.29), channel_id=1, source_target_pairs={{0,64},{64,0},{128,192},{192,128},{256,320},{320,256},{384,448},{4... | collective-permute-start | bytes 12356 | tf_op jit(solution)/shard_map/ppermute | solution.py:101
  137.5 1.6 collective-permute-done.5
  139.1 7.1 %collective-permute-start.6 = (f32[1029]{0:T(1024)S(1)}, f32[1029]{0:T(1024)S(1)}, u32[]{:S(2)}, u32[]{:S(2)}) collective-permute-start(f32[1029]{0:T(1024)S(1)} %add.203), channel_id=1, source_target_pairs={{0,128},{64,192},{128,0},{192,64},{256,384},{320,448},{384,256},{4... | collective-permute-start | bytes 12356 | tf_op jit(solution)/shard_map/ppermute | solution.py:101
  146.2 1.6 collective-permute-done.6
  147.8 9.3 %collective-permute-start.7 = (f32[1029]{0:T(1024)S(1)}, f32[1029]{0:T(1024)S(1)}, u32[]{:S(2)}, u32[]{:S(2)}) collective-permute-start(f32[1029]{0:T(1024)S(1)} %add.204), channel_id=1, source_target_pairs={{0,256},{64,320},{128,384},{192,448},{256,0},{320,64},{384,128},{4... | collective-permute-start | bytes 12356 | tf_op jit(solution)/shard_map/ppermute | solution.py:101
  157.1 1.6 collective-permute-done.7
  158.8 13.9 %all_to_all.31 = f32[32,1,1029]{2,1,0:T(1,128)S(1)} all-to-all(f32[32,1,1029]{2,1,0:T(1,128)S(1)} %broadcast_in_dim.10), channel_id=1, replica_groups=mesh['grp_0'=8,'grp_1'=2,'dev_0'=8,'dev_1'=4] {'dev_0','dev_1'}, dimensions={0} | all-to-all | bytes 263424 | tf_op jit(solution)/shard_map/all_to_all | solution.py:120
  172.6 0.3 reduce.1
  173.1 0.7 slice_bitcast_fusion.10
  173.8 0.5 slice.125
  174.3 0.5 slice.126
  (89 shorter events, 1.7 us)
Async XLA Ops:
  0.6 1.2 copy-start
  0.6 4.0 %copy-start.22 = (s32[4096]{0:T(1024)S(1)}, s32[4096]{0:T(1024)}, u32[]{:S(2)}) copy-start(s32[4096]{0:T(1024)} %param.15) | copy-start | bytes 49156
  0.7 3.9 %copy-start.24 = (f32[6]{0:T(128)S(1)}, f32[6]{0:T(128)}, u32[]{:S(2)}) copy-start(f32[6]{0:T(128)} %param.19) | copy-start | bytes 76
  0.7 4.1 %copy-start.17 = (f32[128]{0:T(128)S(1)}, f32[128]{0:T(128)}, u32[]{:S(2)}) copy-start(f32[128]{0:T(128)} %param.18) | copy-start | bytes 1540
  0.7 4.1 %copy-start.20 = (bf16[128,128]{1,0:T(8,128)(2,1)S(1)}, bf16[128,128]{1,0:T(8,128)(2,1)}, u32[]{:S(2)}) copy-start(bf16[128,128]{1,0:T(8,128)(2,1)} %param.17) | copy-start | bytes 98308
  4.6 2.2 %copy-start.2 = (bf16[4096,128]{1,0:T(8,128)(2,1)}, bf16[4096,128]{1,0:T(8,128)(2,1)S(1)}, u32[]{:S(2)}) copy-start(bf16[4096,128]{1,0:T(8,128)(2,1)S(1)} %get-tuple-element.25) | copy-start | bytes 3145732
  4.8 2.0 %copy-start.8 = (f32[3,4096]{1,0:T(4,128)S(1)}, f32[3,4096]{1,0:T(4,128)}, u32[]{:S(2)}) copy-start(f32[3,4096]{1,0:T(4,128)} %param.14) | copy-start | bytes 147460
  4.8 2.2 %copy-start.13 = (s32[32,256]{1,0:T(8,128)S(1)}, s32[32,256]{1,0:T(8,128)}, u32[]{:S(2)}) copy-start(s32[32,256]{1,0:T(8,128)} %param.23) | copy-start | bytes 98308
  4.9 3.6 %copy-start.14 = (s32[32,256]{1,0:T(8,128)S(1)}, s32[32,256]{1,0:T(8,128)}, u32[]{:S(2)}) copy-start(s32[32,256]{1,0:T(8,128)} %param.24) | copy-start | bytes 98308
  6.8 18.3 %copy-start.6 = (f32[98,16,16]{0,2,1:T(8,128)S(1)}, f32[98,16,16]{0,2,1:T(8,128)}, u32[]{:S(2)}) copy-start(f32[98,16,16]{0,2,1:T(8,128)} %param.20) | copy-start | bytes 301060
  8.4 18.5 %copy-start.19 = (s32[125]{0:T(128)S(1)}, s32[125]{0:T(128)}, u32[]{:S(2)}) copy-start(s32[125]{0:T(128)} %constant.75) | copy-start | bytes 1504
  14.9 22.3 %all-to-all-start = ((f32[5,32,256]{2,0,1:T(8,128)}), f32[5,32,256]{2,0,1:T(8,128)S(1)}, u32[]{:S(2)}, u32[]{:S(2)}) async-start(f32[5,32,256]{2,0,1:T(8,128)} %bitcast.188), calls=%async_computation | async-start | bytes 524288 | tf_op jit(solution)/shard_map/all_to_all | solution.py:412
  25.7 0.6 copy-start.11
  26.4 0.6 copy-start.9
  27.7 20.3 %copy-start.15 = (f32[64,16]{0,1:T(8,128)S(1)}, f32[64,16]{0,1:T(8,128)}, u32[]{:S(2)}) copy-start(f32[64,16]{0,1:T(8,128)} %param.22) | copy-start | bytes 12292
  37.2 0.7 copy-start.1
  37.9 21.9 %copy-start.10 = (pred[5,8,4]{1,2,0:T(4,128)(4,1)S(1)}, pred[5,8,4]{1,2,0:T(4,128)(4,1)}, u32[]{:S(2)}) copy-start(pred[5,8,4]{1,2,0:T(4,128)(4,1)} %copy-done.9) | copy-start | bytes 484
  37.9 28.7 %copy-start.12 = (pred[5,64,64]{2,1,0:T(8,128)(4,1)S(1)}, pred[5,64,64]{2,1,0:T(8,128)(4,1)}, u32[]{:S(2)}) copy-start(pred[5,64,64]{2,1,0:T(8,128)(4,1)} %copy-done.11) | copy-start | bytes 61444
  48.5 4.4 %collective-permute-start.1 = (f32[16,2,4,64]{3,0,2,1:T(8,128)S(1)}, f32[16,2,4,64]{3,0,2,1:T(8,128)S(1)}, u32[]{:S(2)}, u32[]{:S(2)}) collective-permute-start(f32[16,2,4,64]{3,0,2,1:T(8,128)S(1)} %get-tuple-element.19), channel_id=1, source_target_pairs={{32,0},{64,32},{96,64},{128,96},{160,128},{192,160},{224,192},{256... | collective-permute-start | bytes 98312 | tf_op jit(solution)/shard_map/ppermute | solution.py:35
  49.8 3.9 %collective-permute-start = (f32[16,2,4,64]{3,0,2,1:T(8,128)S(1)}, f32[16,2,4,64]{3,0,2,1:T(8,128)S(1)}, u32[]{:S(2)}, u32[]{:S(2)}) collective-permute-start(f32[16,2,4,64]{3,0,2,1:T(8,128)S(1)} %get-tuple-element.18), channel_id=1, source_target_pairs={{0,32},{32,64},{64,96},{96,128},{128,160},{160,192},{192,224},{224... | collective-permute-start | bytes 98312 | tf_op jit(solution)/shard_map/ppermute | solution.py:33
  52.9 15.0 %copy-start.5 = (f32[25,16,16]{2,1,0:T(8,128)S(1)}, f32[25,16,16]{2,1,0:T(8,128)}, u32[]{:S(2)}) copy-start(f32[25,16,16]{2,1,0:T(8,128)} %get-tuple-element.11) | copy-start | bytes 76804
  53.8 6.9 %collective-permute-start.3 = (f32[16,8,2,64]{3,0,2,1:T(8,128)S(1)}, f32[16,8,2,64]{3,0,2,1:T(8,128)S(1)}, u32[]{:S(2)}, u32[]{:S(2)}) collective-permute-start(f32[16,8,2,64]{3,0,2,1:T(8,128)S(1)} %get-tuple-element.15), channel_id=1, source_target_pairs={{1,0},{2,1},{3,2},{4,3},{5,4},{6,5},{7,6},{8,7},{9,8},{10,9},{11,1... | collective-permute-start | bytes 196616 | tf_op jit(solution)/shard_map/ppermute | solution.py:35
  57.5 9.2 %collective-permute-start.2 = (f32[16,8,2,64]{3,0,2,1:T(8,128)S(1)}, f32[16,8,2,64]{3,0,2,1:T(8,128)S(1)}, u32[]{:S(2)}, u32[]{:S(2)}) collective-permute-start(f32[16,8,2,64]{3,0,2,1:T(8,128)S(1)} %get-tuple-element.14), channel_id=1, source_target_pairs={{0,1},{1,2},{2,3},{3,4},{4,5},{5,6},{6,7},{7,8},{8,9},{9,10},{10,1... | collective-permute-start | bytes 196616 | tf_op jit(solution)/shard_map/ppermute | solution.py:33
  67.8 1.3 copy-start.4
  76.5 3.5 %copy-start.16 = (f32[64,16]{0,1:T(8,128)S(1)}, f32[64,16]{0,1:T(8,128)}, u32[]{:S(2)}) copy-start(f32[64,16]{0,1:T(8,128)} %param.21) | copy-start | bytes 12292
  78.5 28.2 %copy-start.23 = (s32[4096]{0:T(1024)S(1)}, s32[4096]{0:T(1024)}, u32[]{:S(2)}) copy-start(s32[4096]{0:T(1024)} %param.15) | copy-start | bytes 49156
  78.5 28.4 %copy-start.18 = (f32[128]{0:T(128)S(1)}, f32[128]{0:T(128)}, u32[]{:S(2)}) copy-start(f32[128]{0:T(128)} %param.18) | copy-start | bytes 1540
  81.1 28.3 %copy-start.3 = (bf16[4096,128]{1,0:T(8,128)(2,1)S(1)}, bf16[4096,128]{1,0:T(8,128)(2,1)}, u32[]{:S(2)}) copy-start(bf16[4096,128]{1,0:T(8,128)(2,1)} %copy-done.2) | copy-start | bytes 3145732
  106.7 3.3 %copy-start.7 = (f32[4096]{0:T(1024)}, f32[4096]{0:T(1024)S(1)}, u32[]{:S(2)}) copy-start(f32[4096]{0:T(1024)S(1)} %reshape.422) | copy-start | bytes 49156
  107.0 3.0 %copy-start.21 = (bf16[128,128]{1,0:T(8,128)(2,1)S(1)}, bf16[128,128]{1,0:T(8,128)(2,1)}, u32[]{:S(2)}) copy-start(bf16[128,128]{1,0:T(8,128)(2,1)} %param.17) | copy-start | bytes 98308
  112.7 3.2 %collective-permute-start.4 = (f32[32902]{0:T(1024)S(1)}, f32[32902]{0:T(1024)S(1)}, u32[]{:S(2)}, u32[]{:S(2)}) collective-permute-start(f32[32902]{0:T(1024)S(1)} %pad_maximum_fusion.3), channel_id=1, source_target_pairs={{0,32},{32,0},{1,33},{33,1},{2,34},{34,2},{3,35},{35,3},{4,36},{36... | collective-permute-start | bytes 394832 | tf_op jit(solution)/shard_map/ppermute | solution.py:101
  130.9 8.2 %collective-permute-start.5 = (f32[1029]{0:T(1024)S(1)}, f32[1029]{0:T(1024)S(1)}, u32[]{:S(2)}, u32[]{:S(2)}) collective-permute-start(f32[1029]{0:T(1024)S(1)} %reduce_sum.29), channel_id=1, source_target_pairs={{0,64},{64,0},{128,192},{192,128},{256,320},{320,256},{384,448},{4... | collective-permute-start | bytes 12356 | tf_op jit(solution)/shard_map/ppermute | solution.py:101
  139.1 8.7 %collective-permute-start.6 = (f32[1029]{0:T(1024)S(1)}, f32[1029]{0:T(1024)S(1)}, u32[]{:S(2)}, u32[]{:S(2)}) collective-permute-start(f32[1029]{0:T(1024)S(1)} %add.203), channel_id=1, source_target_pairs={{0,128},{64,192},{128,0},{192,64},{256,384},{320,448},{384,256},{4... | collective-permute-start | bytes 12356 | tf_op jit(solution)/shard_map/ppermute | solution.py:101
  147.8 10.9 %collective-permute-start.7 = (f32[1029]{0:T(1024)S(1)}, f32[1029]{0:T(1024)S(1)}, u32[]{:S(2)}, u32[]{:S(2)}) collective-permute-start(f32[1029]{0:T(1024)S(1)} %add.204), channel_id=1, source_target_pairs={{0,256},{64,320},{128,384},{192,448},{256,0},{320,64},{384,128},{4... | collective-permute-start | bytes 12356 | tf_op jit(solution)/shard_map/ppermute | solution.py:101

commit v11 on v7

--- a/solution.py
+++ b/solution.py
@@ -267,7 +267,7 @@
     )
 
 
-def box_sum(data, boxes, tile=4096):
+def box_sum(data, boxes, tile=8192):
     rows, slots = data.shape
     parts = pl.pallas_call(
         box_sum_kernel,

time: 176 us -> 176 us (level)
  no operation moved by 1% of the time
where the time goes in v11:
time: 176 us; the launch traced here: 175 us
  starting transfers between devices  45.4 us (26%)
  blocking collectives  43.8 us (25%)
  Pallas kernels  22.8 us (13%)
  waiting for transfers between devices  22.4 us (13%)
  matrix products  22.2 us (13%)
  local copies, waits for them, and re-layouts  10 us (6%)
  other arithmetic  6.79 us (4%)
    ppermute x4, starting transfers between devices, swapped(): return lax.ppermute(x, axis, [(i, i ^ step) for i in range(count)])  24.9 us
    all_to_all x1, blocking collectives, shards(): lax.all_to_all(slot_potential, DEV, split_axis=0, concat_axis=0, tiled=True)  15.5 us
    all_to_all x1, blocking collectives, hybrid_sum(): lax.all_to_all(lines, plane, 0, 0, tiled=True).reshape(peers, -1)  14.5 us
    all_to_all x1, blocking collectives, hybrid_sum(): return lax.all_to_all(copies, plane, 0, 0, tiled=True).reshape(-1)[:length]  13.9 us
    all_to_all x1, starting transfers between devices, shards(): lax.all_to_all(outgoing, DEV, split_axis=1, concat_axis=1, tiled=True)  10.2 us
    all_to_all x1, waiting for transfers between devices, shards(): lax.all_to_all(outgoing, DEV, split_axis=1, concat_axis=1, tiled=True)  8.63 us
    pallas_call x1, Pallas kernels, box_sum(): pl.pallas_call(box_sum_kernel, grid=(slots // tile,), in_specs=[pl.BlockS...  8.41 us
    ppermute x2, waiting for transfers between devices, extended_2(): lax.ppermute(tail, axis, [(i, (i + 1) % count) for i in range(ends)])  6.84 us
  transfers between devices with their start and end apart: 9, of which 8 were waited for; matrix products, arithmetic and copies ran while one was open for 1% of the time, Pallas kernels for 0%

profile of v11, /device:TPU:8, one launch (start us, length us, event | category | flops | bytes accessed | tf_op | source)
XLA Modules:
  0.0 174.8 jit_solution(135952303378395585)
XLA Ops:
  0.7 1.2 copy-done
  1.9 2.7 %multiply_convert_fusion.1 = (bf16[4096,128]{1,0:T(8,128)(2,1)S(1)}, f32[4096,128]{1,0:T(8,128)}) fusion(bf16[4096,128]{1,0:T(8,128)(2,1)S(1)} %copy-done, bf16[128,128]{1,0:T(8,128)(2,1)} %param.16), kind=kOutput, calls=%fused_computation.8 | convolution fusion | flops 136839168 | bytes 4227072 | tf_op jit(solution)/shard_map/dot_general | solution.py:395
  4.6 0.2 fusion.60
  4.9 2.0 %multiply_reduce_fusion.1 = (f32[4096]{0:T(1024)S(1)}, f32[4096,128]{1,0:T(8,128)}) fusion(f32[128]{0:T(128)S(1)} %copy-done.17, bf16[4096,128]{1,0:T(8,128)(2,1)S(1)} %get-tuple-element.25, bf16[128,128]{1,0:T(8,128)(2,1)S(1)} %copy-done.20), kind=kOutput, calls=%fused_computation.5 | convolution fusion | flops 137359360 | bytes 3195392 | tf_op jit(solution)/shard_map/dot_general | solution.py:397
  7.1 0.6 copy.78
  7.8 0.6 copy.79
  8.4 0.6 copy.80
  9.1 0.7 pad_maximum_fusion.2.table_ref
  9.8 5.3 %shard_map.164 = f32[5,8192]{1,0:T(8,128)} custom-call(bf16[768,64]{1,0:T(8,128)(2,1)} %pad_maximum_fusion.2.table_ref, s32[1,8192]{1,0:T(1,128)} %bitcast.196, s32[1,8192]{1,0:T(1,128)} %bitcast.198, s32[1,8192]{1,0:T(1,128)} %bitcast.200), custom_call_target="tpu_custom_call" | custom-call | tf_op jit(solution)/shard_map/pallas_call | solution.py:165
  15.1 10.2 %all-to-all-start = ((f32[5,32,256]{2,0,1:T(8,128)}), f32[5,32,256]{2,0,1:T(8,128)S(1)}, u32[]{:S(2)}, u32[]{:S(2)}) async-start(f32[5,32,256]{2,0,1:T(8,128)} %bitcast.188), calls=%async_computation | async-start | bytes 524288 | tf_op jit(solution)/shard_map/all_to_all | solution.py:412
  25.3 0.4 copy.44
  26.2 0.4 copy-done.11
  26.5 0.6 copy-done.9
  27.1 0.7 gather_fusion
  27.9 0.9 fusion.83
  28.8 8.6 %all-to-all-done = f32[5,32,256]{2,0,1:T(8,128)S(1)} async-done(((f32[5,32,256]{2,0,1:T(8,128)}), f32[5,32,256]{2,0,1:T(8,128)S(1)}, u32[]{:S(2)}, u32[]{:S(2)}) %all-to-all-start) | async-done | bytes 163872 | tf_op jit(solution)/shard_map/all_to_all | solution.py:412
  37.4 0.7 copy-done.1
  38.1 8.4 %shard_map.165 = f32[128,1024]{1,0:T(8,128)} custom-call(f32[5,8192]{1,0:T(8,128)} %bitcast.186), custom_call_target="tpu_custom_call" | custom-call | tf_op jit(solution)/shard_map/pallas_call | solution.py:272
  46.5 1.1 slice_add_fusion
  47.6 0.3 reshape.420
  47.9 0.5 convolution_bitcast_fusion.7
  48.5 1.3 collective-permute-start.1
  49.8 3.0 %collective-permute-start = (f32[16,2,4,64]{3,0,2,1:T(8,128)S(1)}, f32[16,2,4,64]{3,0,2,1:T(8,128)S(1)}, u32[]{:S(2)}, u32[]{:S(2)}) collective-permute-start(f32[16,2,4,64]{3,0,2,1:T(8,128)S(1)} %get-tuple-element.18), channel_id=1, source_target_pairs={{0,32},{32,64},{64,96},{96,128},{128,160},{160,192},{192,224},{224... | collective-permute-start | bytes 98312 | tf_op jit(solution)/shard_map/ppermute | solution.py:33
  52.9 0.8 collective-permute-done
  53.8 3.7 %collective-permute-start.3 = (f32[16,8,2,64]{3,0,2,1:T(8,128)S(1)}, f32[16,8,2,64]{3,0,2,1:T(8,128)S(1)}, u32[]{:S(2)}, u32[]{:S(2)}) collective-permute-start(f32[16,8,2,64]{3,0,2,1:T(8,128)S(1)} %get-tuple-element.15), channel_id=1, source_target_pairs={{1,0},{2,1},{3,2},{4,3},{5,4},{6,5},{7,6},{8,7},{9,8},{10,9},{11,1... | collective-permute-start | bytes 196616 | tf_op jit(solution)/shard_map/ppermute | solution.py:35
  57.4 2.4 %collective-permute-start.2 = (f32[16,8,2,64]{3,0,2,1:T(8,128)S(1)}, f32[16,8,2,64]{3,0,2,1:T(8,128)S(1)}, u32[]{:S(2)}, u32[]{:S(2)}) collective-permute-start(f32[16,8,2,64]{3,0,2,1:T(8,128)S(1)} %get-tuple-element.14), channel_id=1, source_target_pairs={{0,1},{1,2},{2,3},{3,4},{4,5},{5,6},{6,7},{7,8},{8,9},{9,10},{10,1... | collective-permute-start | bytes 196616 | tf_op jit(solution)/shard_map/ppermute | solution.py:33
  59.9 0.7 collective-permute-done.3
  60.6 6.0 %collective-permute-done.2 = f32[16,8,2,64]{3,0,2,1:T(8,128)S(1)} collective-permute-done((f32[16,8,2,64]{3,0,2,1:T(8,128)S(1)}, f32[16,8,2,64]{3,0,2,1:T(8,128)S(1)}, u32[]{:S(2)}, u32[]{:S(2)}) %collective-permute-start.2) | collective-permute-done | bytes 65568 | tf_op jit(solution)/shard_map/ppermute | solution.py:33
  66.6 1.2 convolution_bitcast_fusion
  67.8 1.3 convolution_bitcast_fusion.5
  69.1 1.3 convolution_bitcast_fusion.4
  70.4 1.3 convolution_bitcast_fusion.3
  71.8 1.3 convolution_bitcast_fusion.2
  73.1 1.3 convolution_bitcast_fusion.1
  74.4 1.0 fusion.13
  75.4 1.0 fusion.40
  76.4 1.0 fusion.37
  77.5 1.0 fusion.34
  78.5 1.2 fusion.31
  79.9 0.4 reduce-precision_convert_fusion
  80.4 0.7 pad_maximum_fusion.1.table_ref
  81.1 6.7 %shard_map.166 = f32[1,8192]{1,0:T(1,128)} custom-call(bf16[128,1024]{1,0:T(8,128)(2,1)} %pad_maximum_fusion.1.table_ref, f32[5,8192]{1,0:T(8,128)} %bitcast.187), custom_call_target="tpu_custom_call" | custom-call | tf_op jit(solution)/shard_map/pallas_call | solution.py:295
  87.8 15.5 %all_to_all.29 = f32[32,1,256]{2,1,0:T(1,128)} all-to-all(f32[32,1,256]{2,1,0:T(1,128)} %bitcast.201), channel_id=1, replica_groups=mesh['grp_0'=8,'grp_1'=2,'dev_0'=8,'dev_1'=4] {'dev_0','dev_1'}, dimensions={0} | all-to-all | bytes 65536 | tf_op jit(solution)/shard_map/all_to_all | solution.py:421
  103.3 2.4 %shard_map.167 = f32[192,64]{1,0:T(8,128)} custom-call(f32[1,8192]{1,0:T(1,128)} %bitcast.202, s32[1,8192]{1,0:T(1,128)} %bitcast.197, s32[1,8192]{1,0:T(1,128)} %bitcast.199), custom_call_target="tpu_custom_call" | custom-call | tf_op jit(solution)/shard_map/pallas_call | solution.py:207
  105.8 0.8 slice_add_fusion.1
  106.7 0.2 fusion.46
  107.0 2.4 %multiply_convert_fusion = (bf16[4096,128]{1,0:T(8,128)(2,1)S(1)}, f32[128]{0:T(128)S(1)}) fusion(f32[4096,128]{1,0:T(8,128)} %get-tuple-element.28, f32[4096]{0:T(1024)S(1)} %reshape.422, f32[128]{0:T(128)S(1)} %copy-done.18), kind=kLoop, calls=%fused_computation.4 | loop fusion | flops 6815616 | bytes 3163136 | tf_op jit(solution)/shard_map/convert_element_type | solution.py:425
  109.4 0.5 fusion.43
  109.9 2.6 %fusion.45 = f32[128,128]{0,1:T(8,128)S(1)} fusion(bf16[4096,128]{1,0:T(8,128)(2,1)S(1)} %copy-done, bf16[4096,128]{1,0:T(8,128)(2,1)S(1)} %get-tuple-element.5, bf16[128,128]{1,0:T(8,128)(2,1)S(1)} %copy-done.21, f32[4096,128]{1,0:T(8,128)} %get-tuple-element.26), kind=kOutput, calls=%fused_computation.47 | convolution fusion | flops 273170432 | bytes 4292608 | tf_op jit(solution)/shard_map/dot_general | solution.py:437
  112.7 1.9 %collective-permute-start.4 = (f32[32902]{0:T(1024)S(1)}, f32[32902]{0:T(1024)S(1)}, u32[]{:S(2)}, u32[]{:S(2)}) collective-permute-start(f32[32902]{0:T(1024)S(1)} %pad_maximum_fusion.3), channel_id=1, source_target_pairs={{0,32},{32,0},{1,33},{33,1},{2,34},{34,2},{3,35},{35,3},{4,36},{36... | collective-permute-start | bytes 394832 | tf_op jit(solution)/shard_map/ppermute | solution.py:101
  114.6 1.3 collective-permute-done.4
  116.0 0.2 all_to_all.22
  116.2 14.5 %all_to_all.30 = f32[32,1,1029]{2,1,0:T(1,128)S(1)} all-to-all(f32[32,1,1029]{2,1,0:T(1,128)S(1)} %all_to_all.22), channel_id=1, replica_groups=mesh['grp_0'=8,'grp_1'=2,'dev_0'=8,'dev_1'=4] {'dev_0','dev_1'}, dimensions={0} | all-to-all | bytes 263424 | tf_op jit(solution)/shard_map/all_to_all | solution.py:117
  130.8 6.7 %collective-permute-start.5 = (f32[1029]{0:T(1024)S(1)}, f32[1029]{0:T(1024)S(1)}, u32[]{:S(2)}, u32[]{:S(2)}) collective-permute-start(f32[1029]{0:T(1024)S(1)} %reduce_sum.29), channel_id=1, source_target_pairs={{0,64},{64,0},{128,192},{192,128},{256,320},{320,256},{384,448},{4... | collective-permute-start | bytes 12356 | tf_op jit(solution)/shard_map/ppermute | solution.py:101
  137.5 1.6 collective-permute-done.5
  139.1 7.1 %collective-permute-start.6 = (f32[1029]{0:T(1024)S(1)}, f32[1029]{0:T(1024)S(1)}, u32[]{:S(2)}, u32[]{:S(2)}) collective-permute-start(f32[1029]{0:T(1024)S(1)} %add.203), channel_id=1, source_target_pairs={{0,128},{64,192},{128,0},{192,64},{256,384},{320,448},{384,256},{4... | collective-permute-start | bytes 12356 | tf_op jit(solution)/shard_map/ppermute | solution.py:101
  146.2 1.6 collective-permute-done.6
  147.8 9.3 %collective-permute-start.7 = (f32[1029]{0:T(1024)S(1)}, f32[1029]{0:T(1024)S(1)}, u32[]{:S(2)}, u32[]{:S(2)}) collective-permute-start(f32[1029]{0:T(1024)S(1)} %add.204), channel_id=1, source_target_pairs={{0,256},{64,320},{128,384},{192,448},{256,0},{320,64},{384,128},{4... | collective-permute-start | bytes 12356 | tf_op jit(solution)/shard_map/ppermute | solution.py:101
  157.0 1.6 collective-permute-done.7
  158.7 13.9 %all_to_all.31 = f32[32,1,1029]{2,1,0:T(1,128)S(1)} all-to-all(f32[32,1,1029]{2,1,0:T(1,128)S(1)} %broadcast_in_dim.10), channel_id=1, replica_groups=mesh['grp_0'=8,'grp_1'=2,'dev_0'=8,'dev_1'=4] {'dev_0','dev_1'}, dimensions={0} | all-to-all | bytes 263424 | tf_op jit(solution)/shard_map/all_to_all | solution.py:120
  172.6 0.3 reduce.1
  173.1 0.7 slice_bitcast_fusion.10
  173.8 0.5 slice.125
  174.3 0.5 slice.126
  (89 shorter events, 1.7 us)
Async XLA Ops:
  0.6 1.2 copy-start
  0.6 4.0 %copy-start.22 = (s32[4096]{0:T(1024)S(1)}, s32[4096]{0:T(1024)}, u32[]{:S(2)}) copy-start(s32[4096]{0:T(1024)} %param.15) | copy-start | bytes 49156
  0.7 3.9 %copy-start.24 = (f32[6]{0:T(128)S(1)}, f32[6]{0:T(128)}, u32[]{:S(2)}) copy-start(f32[6]{0:T(128)} %param.19) | copy-start | bytes 76
  0.7 4.1 %copy-start.17 = (f32[128]{0:T(128)S(1)}, f32[128]{0:T(128)}, u32[]{:S(2)}) copy-start(f32[128]{0:T(128)} %param.18) | copy-start | bytes 1540
  0.7 4.1 %copy-start.20 = (bf16[128,128]{1,0:T(8,128)(2,1)S(1)}, bf16[128,128]{1,0:T(8,128)(2,1)}, u32[]{:S(2)}) copy-start(bf16[128,128]{1,0:T(8,128)(2,1)} %param.17) | copy-start | bytes 98308
  4.6 2.2 %copy-start.2 = (bf16[4096,128]{1,0:T(8,128)(2,1)}, bf16[4096,128]{1,0:T(8,128)(2,1)S(1)}, u32[]{:S(2)}) copy-start(bf16[4096,128]{1,0:T(8,128)(2,1)S(1)} %get-tuple-element.25) | copy-start | bytes 3145732
  4.8 2.0 %copy-start.8 = (f32[3,4096]{1,0:T(4,128)S(1)}, f32[3,4096]{1,0:T(4,128)}, u32[]{:S(2)}) copy-start(f32[3,4096]{1,0:T(4,128)} %param.14) | copy-start | bytes 147460
  4.8 2.2 %copy-start.13 = (s32[32,256]{1,0:T(8,128)S(1)}, s32[32,256]{1,0:T(8,128)}, u32[]{:S(2)}) copy-start(s32[32,256]{1,0:T(8,128)} %param.23) | copy-start | bytes 98308
  4.9 3.6 %copy-start.14 = (s32[32,256]{1,0:T(8,128)S(1)}, s32[32,256]{1,0:T(8,128)}, u32[]{:S(2)}) copy-start(s32[32,256]{1,0:T(8,128)} %param.24) | copy-start | bytes 98308
  6.8 18.5 %copy-start.6 = (f32[98,16,16]{0,2,1:T(8,128)S(1)}, f32[98,16,16]{0,2,1:T(8,128)}, u32[]{:S(2)}) copy-start(f32[98,16,16]{0,2,1:T(8,128)} %param.20) | copy-start | bytes 301060
  8.4 18.7 %copy-start.19 = (s32[125]{0:T(128)S(1)}, s32[125]{0:T(128)}, u32[]{:S(2)}) copy-start(s32[125]{0:T(128)} %constant.75) | copy-start | bytes 1504
  15.1 22.3 %all-to-all-start = ((f32[5,32,256]{2,0,1:T(8,128)}), f32[5,32,256]{2,0,1:T(8,128)S(1)}, u32[]{:S(2)}, u32[]{:S(2)}) async-start(f32[5,32,256]{2,0,1:T(8,128)} %bitcast.188), calls=%async_computation | async-start | bytes 524288 | tf_op jit(solution)/shard_map/all_to_all | solution.py:412
  25.9 0.6 copy-start.11
  26.5 0.6 copy-start.9
  27.9 20.1 %copy-start.15 = (f32[64,16]{0,1:T(8,128)S(1)}, f32[64,16]{0,1:T(8,128)}, u32[]{:S(2)}) copy-start(f32[64,16]{0,1:T(8,128)} %param.22) | copy-start | bytes 12292
  37.4 0.7 copy-start.1
  38.1 21.7 %copy-start.10 = (pred[5,8,4]{1,2,0:T(4,128)(4,1)S(1)}, pred[5,8,4]{1,2,0:T(4,128)(4,1)}, u32[]{:S(2)}) copy-start(pred[5,8,4]{1,2,0:T(4,128)(4,1)} %copy-done.9) | copy-start | bytes 484
  38.1 28.5 %copy-start.12 = (pred[5,64,64]{2,1,0:T(8,128)(4,1)S(1)}, pred[5,64,64]{2,1,0:T(8,128)(4,1)}, u32[]{:S(2)}) copy-start(pred[5,64,64]{2,1,0:T(8,128)(4,1)} %copy-done.11) | copy-start | bytes 61444
  48.5 4.4 %collective-permute-start.1 = (f32[16,2,4,64]{3,0,2,1:T(8,128)S(1)}, f32[16,2,4,64]{3,0,2,1:T(8,128)S(1)}, u32[]{:S(2)}, u32[]{:S(2)}) collective-permute-start(f32[16,2,4,64]{3,0,2,1:T(8,128)S(1)} %get-tuple-element.19), channel_id=1, source_target_pairs={{32,0},{64,32},{96,64},{128,96},{160,128},{192,160},{224,192},{256... | collective-permute-start | bytes 98312 | tf_op jit(solution)/shard_map/ppermute | solution.py:35
  49.8 3.9 %collective-permute-start = (f32[16,2,4,64]{3,0,2,1:T(8,128)S(1)}, f32[16,2,4,64]{3,0,2,1:T(8,128)S(1)}, u32[]{:S(2)}, u32[]{:S(2)}) collective-permute-start(f32[16,2,4,64]{3,0,2,1:T(8,128)S(1)} %get-tuple-element.18), channel_id=1, source_target_pairs={{0,32},{32,64},{64,96},{96,128},{128,160},{160,192},{192,224},{224... | collective-permute-start | bytes 98312 | tf_op jit(solution)/shard_map/ppermute | solution.py:33
  52.8 15.0 %copy-start.5 = (f32[25,16,16]{2,1,0:T(8,128)S(1)}, f32[25,16,16]{2,1,0:T(8,128)}, u32[]{:S(2)}) copy-start(f32[25,16,16]{2,1,0:T(8,128)} %get-tuple-element.11) | copy-start | bytes 76804
  53.8 6.9 %collective-permute-start.3 = (f32[16,8,2,64]{3,0,2,1:T(8,128)S(1)}, f32[16,8,2,64]{3,0,2,1:T(8,128)S(1)}, u32[]{:S(2)}, u32[]{:S(2)}) collective-permute-start(f32[16,8,2,64]{3,0,2,1:T(8,128)S(1)} %get-tuple-element.15), channel_id=1, source_target_pairs={{1,0},{2,1},{3,2},{4,3},{5,4},{6,5},{7,6},{8,7},{9,8},{10,9},{11,1... | collective-permute-start | bytes 196616 | tf_op jit(solution)/shard_map/ppermute | solution.py:35
  57.4 9.2 %collective-permute-start.2 = (f32[16,8,2,64]{3,0,2,1:T(8,128)S(1)}, f32[16,8,2,64]{3,0,2,1:T(8,128)S(1)}, u32[]{:S(2)}, u32[]{:S(2)}) collective-permute-start(f32[16,8,2,64]{3,0,2,1:T(8,128)S(1)} %get-tuple-element.14), channel_id=1, source_target_pairs={{0,1},{1,2},{2,3},{3,4},{4,5},{5,6},{6,7},{7,8},{8,9},{9,10},{10,1... | collective-permute-start | bytes 196616 | tf_op jit(solution)/shard_map/ppermute | solution.py:33
  67.8 1.3 copy-start.4
  76.4 3.5 %copy-start.16 = (f32[64,16]{0,1:T(8,128)S(1)}, f32[64,16]{0,1:T(8,128)}, u32[]{:S(2)}) copy-start(f32[64,16]{0,1:T(8,128)} %param.21) | copy-start | bytes 12292
  78.5 28.2 %copy-start.23 = (s32[4096]{0:T(1024)S(1)}, s32[4096]{0:T(1024)}, u32[]{:S(2)}) copy-start(s32[4096]{0:T(1024)} %param.15) | copy-start | bytes 49156
  78.5 28.4 %copy-start.18 = (f32[128]{0:T(128)S(1)}, f32[128]{0:T(128)}, u32[]{:S(2)}) copy-start(f32[128]{0:T(128)} %param.18) | copy-start | bytes 1540
  81.1 28.3 %copy-start.3 = (bf16[4096,128]{1,0:T(8,128)(2,1)S(1)}, bf16[4096,128]{1,0:T(8,128)(2,1)}, u32[]{:S(2)}) copy-start(bf16[4096,128]{1,0:T(8,128)(2,1)} %copy-done.2) | copy-start | bytes 3145732
  106.6 3.3 %copy-start.7 = (f32[4096]{0:T(1024)}, f32[4096]{0:T(1024)S(1)}, u32[]{:S(2)}) copy-start(f32[4096]{0:T(1024)S(1)} %reshape.422) | copy-start | bytes 49156
  107.0 3.0 %copy-start.21 = (bf16[128,128]{1,0:T(8,128)(2,1)S(1)}, bf16[128,128]{1,0:T(8,128)(2,1)}, u32[]{:S(2)}) copy-start(bf16[128,128]{1,0:T(8,128)(2,1)} %param.17) | copy-start | bytes 98308
  112.7 3.2 %collective-permute-start.4 = (f32[32902]{0:T(1024)S(1)}, f32[32902]{0:T(1024)S(1)}, u32[]{:S(2)}, u32[]{:S(2)}) collective-permute-start(f32[32902]{0:T(1024)S(1)} %pad_maximum_fusion.3), channel_id=1, source_target_pairs={{0,32},{32,0},{1,33},{33,1},{2,34},{34,2},{3,35},{35,3},{4,36},{36... | collective-permute-start | bytes 394832 | tf_op jit(solution)/shard_map/ppermute | solution.py:101
  130.8 8.3 %collective-permute-start.5 = (f32[1029]{0:T(1024)S(1)}, f32[1029]{0:T(1024)S(1)}, u32[]{:S(2)}, u32[]{:S(2)}) collective-permute-start(f32[1029]{0:T(1024)S(1)} %reduce_sum.29), channel_id=1, source_target_pairs={{0,64},{64,0},{128,192},{192,128},{256,320},{320,256},{384,448},{4... | collective-permute-start | bytes 12356 | tf_op jit(solution)/shard_map/ppermute | solution.py:101
  139.1 8.7 %collective-permute-start.6 = (f32[1029]{0:T(1024)S(1)}, f32[1029]{0:T(1024)S(1)}, u32[]{:S(2)}, u32[]{:S(2)}) collective-permute-start(f32[1029]{0:T(1024)S(1)} %add.203), channel_id=1, source_target_pairs={{0,128},{64,192},{128,0},{192,64},{256,384},{320,448},{384,256},{4... | collective-permute-start | bytes 12356 | tf_op jit(solution)/shard_map/ppermute | solution.py:101
  147.8 10.9 %collective-permute-start.7 = (f32[1029]{0:T(1024)S(1)}, f32[1029]{0:T(1024)S(1)}, u32[]{:S(2)}, u32[]{:S(2)}) collective-permute-start(f32[1029]{0:T(1024)S(1)} %add.204), channel_id=1, source_target_pairs={{0,256},{64,320},{128,384},{192,448},{256,0},{320,64},{384,128},{4... | collective-permute-start | bytes 12356 | tf_op jit(solution)/shard_map/ppermute | solution.py:101
